TPU v7x, 512 devices: a whole 4x4x16 slice. The times are simulated.
512 devices in a mesh: head: 8 (over x, core), group: 64 (over z, y).
Axes of the slice: x: 4, y: 4, z: 16, core: 2. Of those that a mesh axis runs over, the one named last changes fastest.
Arguments:
- query_proj: bfloat16 [8192, 2048], P('group', 'head'), may hold values from -6 to 6
- key_proj: bfloat16 [8192, 2048], P('group', 'head'), may hold values from -6 to 6
- value_proj: bfloat16 [8192, 4096], P('group', 'head'), may hold values from -6 to 6
- gate_proj: bfloat16 [8192, 4096], P('group', 'head'), may hold values from -6 to 6
- log_decay: float32 [8192, 8], P('group', 'head'), may hold values from -0.75 to 0
- out_weight: bfloat16 [4096, 2048], P('head'), may hold values from -0.09375 to 0.09375
- residual: bfloat16 [64, 128, 2048], P('group', 'head'), may hold values from -30 to 30
- norm_gain: float32 [2048], replicated, may hold values from 0.5 to 1.5
- vocab_weight: bfloat16 [49152, 2048], P(('head', 'group')), may hold values from -2 to 2
- targets: int32 [64, 128], P('group', 'head'), may hold values from 0 to 49151
- ref_logp: float32 [64, 128], P('group', 'head'), may hold values from -16 to -1
- response_mask: int32 [64, 128], P('group', 'head'), may hold values 0 or 1
- seq_lengths: int32 [32], replicated, may hold values from 1 to 4096, 8192 in all
Outputs:
- seq_ratio: float32 [32], replicated
- state_norms: float32 [64, 8], P('group', 'head')
- max_logits: float32 [64, 128], P('group', 'head')
Inputs may be any that keep to these rules, and one draw needn't show every extreme that they name: `seq_lengths`: the sequences lie end to end in order from position 0, the lengths summing to 8192.
All inputs are finite; a program needn't handle non-finite values. No bound on the sum of `response_mask` on one device may be relied on, other than what follows from the above.
Results may differ from a plain program's by a relative error of at most 0.00093.
Values may be sent and summed in bfloat16 or wider, within the bound.
No kernel may reach another device: no remote copies, remote signals or barrier semaphores. Data moves between devices by JAX's collectives and lax.ppermute only.
A program may use at most 192 MiB of HBM per device.

v0:
```python
import jax
import jax.numpy as jnp
from jax import lax
from jax.sharding import PartitionSpec as P


def entering(value, axis, combine, identity):
    size, index = (lax.axis_size(axis), lax.axis_index(axis))
    everything = jax.tree.map(lambda part: lax.all_gather(part, axis), value)
    start = jax.tree.map(
        lambda part, zero: jnp.broadcast_to(jnp.asarray(zero, part.dtype), part.shape),
        value,
        identity,
    )

    def lap(k, before):
        reached = k < index
        new = combine(before, jax.tree.map(lambda part: part[k], everything))
        return jax.tree.map(lambda a, b: jnp.where(reached, a, b), new, before)

    return lax.fori_loop(0, size, lap, start)


def merged_2(part, axis, combine):
    gathered = jax.tree.map(lambda a: lax.all_gather(a, axis), part)

    def take(source):
        return jax.tree.map(lambda a: lax.dynamic_index_in_dim(a, source, 0, False), gathered)

    return lax.fori_loop(
        1, lax.axis_size(axis), lambda source, state: combine(state, take(source)), take(0)
    )


def layer_norm(stream, width_eps):
    mean_val = jnp.mean(stream, axis=-1, keepdims=True)
    centered = stream - mean_val
    var_val = jnp.mean(centered * centered, axis=-1, keepdims=True)
    return centered / jnp.sqrt(var_val + width_eps)


def combine_state(earlier, later):
    decay_first, state_first = earlier
    decay_second, state_second = later
    return (decay_first * decay_second, decay_second[:, None, None] * state_first + state_second)


def combine_totals(first, second):
    max_first, sum_first, target_first = first
    max_second, sum_second, target_second = second
    top = jnp.maximum(max_first, max_second)
    merged = sum_first * jnp.exp(max_first - top) + sum_second * jnp.exp(max_second - top)
    return (top, merged, target_first + target_second)


def per_device(
    query_proj,
    key_proj,
    value_proj,
    gate_proj,
    log_decay,
    out_weight,
    residual,
    norm_gain,
    vocab_weight,
    targets,
    ref_logp,
    response_mask,
    seq_lengths,
):
    highest_precision = lax.Precision.HIGHEST
    head_count = lax.axis_size("head")
    group_count = lax.axis_size("group")
    head_index = lax.axis_index("head")
    group_index = lax.axis_index("group")
    tok_count = query_proj.shape[0]
    heads_here = log_decay.shape[1]
    key_width = query_proj.shape[1] // heads_here
    value_width = value_proj.shape[1] // heads_here
    slice_rows = residual.shape[1]
    seq_count = seq_lengths.shape[0]
    vocab_here = vocab_weight.shape[0]
    key_scaling = key_width ** (-0.5)
    starts = jnp.cumsum(seq_lengths) - seq_lengths
    local_pos = jnp.arange(tok_count, dtype=jnp.int32)
    positions = group_index * tok_count + local_pos
    seq_ids = jnp.sum((positions[:, None] >= starts[None, 1:]).astype(jnp.int32), axis=1)
    is_start = jnp.any(positions[:, None] == starts[None, :], axis=1)
    cumulative_decay = jnp.cumsum(log_decay, axis=0)
    same_seq = (seq_ids[:, None] == seq_ids[None, :]) & (local_pos[None, :] <= local_pos[:, None])
    gap_log = cumulative_decay[:, None, :] - cumulative_decay[None, :, :]
    decay_mat = jnp.where(same_seq[:, :, None], jnp.exp(jnp.minimum(gap_log, 0.0)), 0.0)
    query_heads = query_proj.reshape(tok_count, heads_here, key_width)
    key_heads = key_proj.reshape(tok_count, heads_here, key_width)
    value_heads = value_proj.reshape(tok_count, heads_here, value_width)
    raw_scores = jnp.einsum(
        "thd,shd->tsh", query_heads, key_heads, preferred_element_type=jnp.float32
    )
    weights_in = (raw_scores * key_scaling * decay_mat).astype(jnp.bfloat16)
    in_block = jnp.einsum(
        "tsh,shv->thv", weights_in, value_heads, preferred_element_type=jnp.float32
    )
    continuation_flags = (seq_ids == seq_ids[0]) & jnp.logical_not(is_start[0])
    final_decay_weight = jnp.where(
        (seq_ids == seq_ids[-1])[:, None],
        jnp.exp(cumulative_decay[-1][None, :] - cumulative_decay),
        0.0,
    )
    key_as_float = key_heads.astype(jnp.float32)
    value_as_float = value_heads.astype(jnp.float32)
    block_total_sum = jnp.einsum(
        "ane,anl->nel",
        key_as_float * final_decay_weight[:, :, None],
        value_as_float,
        precision=highest_precision,
    )
    block_decay = jnp.where(jnp.all(continuation_flags), jnp.exp(cumulative_decay[-1]), 0.0)
    decay_prefix, carried_state = entering(
        (block_decay, block_total_sum),
        "group",
        combine_state,
        (jnp.ones_like(block_decay), jnp.zeros_like(block_total_sum)),
    )
    query_as_float = query_heads.astype(jnp.float32)
    state_contribution = (
        jnp.einsum("ugo,gow->ugw", query_as_float, carried_state, precision=highest_precision)
        * key_scaling
        * (jnp.exp(cumulative_decay) * continuation_flags[:, None].astype(jnp.float32))[:, :, None]
    )
    retained = in_block + state_contribution
    state_norms = jnp.log(
        1.0 + jnp.sqrt(jnp.mean(carried_state * carried_state, axis=(1, 2)) + 1e-06)
    )[None, :]
    normed = layer_norm(retained, 1e-06)
    gate_float = gate_proj.reshape(tok_count, heads_here, value_width).astype(jnp.float32)
    gated_out = (
        (normed * jax.nn.silu(gate_float))
        .astype(jnp.bfloat16)
        .reshape(tok_count, heads_here * value_width)
    )
    full_branch = lax.psum(
        jnp.dot(gated_out, out_weight, preferred_element_type=jnp.float32), "head"
    )
    own_branch = lax.dynamic_slice_in_dim(full_branch, head_index * slice_rows, slice_rows, 0)
    stream = residual[0].astype(jnp.float32) + own_branch
    hidden = (layer_norm(stream, 1e-05) * norm_gain).astype(jnp.bfloat16)
    vocab_rows = lax.all_gather(vocab_weight, "head", axis=0, tiled=True)
    entry_ids = (
        (jnp.arange(head_count, dtype=jnp.int32)[:, None] * group_count + group_index) * vocab_here
        + jnp.arange(vocab_here, dtype=jnp.int32)[None, :]
    ).reshape(-1)
    all_targets = lax.all_gather(targets, "group", axis=0, tiled=True).reshape(-1)
    logits = lax.dot_general(
        lax.all_gather(hidden, "group", axis=0, tiled=True),
        vocab_rows,
        (((1,), (1,)), ((), ())),
        preferred_element_type=jnp.float32,
    )
    top = jnp.max(logits, axis=1)
    exp_total = jnp.sum(jnp.exp(logits - top[:, None]), axis=1)
    picked = jnp.sum(jnp.where(entry_ids[None, :] == all_targets[:, None], logits, 0.0), axis=1)
    merged_max, merged_total, merged_target = merged_2(
        (top, exp_total, picked), "group", combine_totals
    )
    own_start = group_index * slice_rows
    own_max = lax.dynamic_slice_in_dim(merged_max, own_start, slice_rows, 0)
    own_total = lax.dynamic_slice_in_dim(merged_total, own_start, slice_rows, 0)
    own_target = lax.dynamic_slice_in_dim(merged_target, own_start, slice_rows, 0)
    token_logp = own_target - own_max - jnp.log(own_total)
    token_ratio = response_mask[0].astype(jnp.float32) * (token_logp - ref_logp[0])
    own_positions = (
        group_index * tok_count + head_index * slice_rows + jnp.arange(slice_rows, dtype=jnp.int32)
    )
    own_seq = jnp.sum((own_positions[:, None] >= starts[None, 1:]).astype(jnp.int32), axis=1)
    member = (own_seq[:, None] == jnp.arange(seq_count, dtype=jnp.int32)[None, :]).astype(
        jnp.float32
    )
    partial_sums = jnp.sum(member * token_ratio[:, None], axis=0)
    seq_total = lax.psum(partial_sums, ("head", "group"))
    seq_ratio = seq_total / seq_lengths.astype(jnp.float32)
    return (seq_ratio, state_norms, own_max[None, :])


def solution(mesh):
    placed = (
        P("group", "head"),
        P("group", "head"),
        P("group", "head"),
        P("group", "head"),
        P("group", "head"),
        P("head", None),
        P("group", "head", None),
        P(),
        P(("head", "group"), None),
        P("group", "head"),
        P("group", "head"),
        P("group", "head"),
        P(),
    )
    return jax.shard_map(
        per_device,
        mesh=mesh,
        in_specs=placed,
        out_specs=(P(), P("group", "head"), P("group", "head")),
        check_vma=False,
    )
```

profile of v0, /device:TPU:1, one launch (start us, length us, event | category | flops | bytes accessed | tf_op | source)
XLA Modules:
  0.0 1104.0 jit_solution(7736796579347406270)
XLA Ops:
  11.4 2.0 select_multiply_fusion
  13.4 2.2 fusion.19
  20.4 124.9 %all-reduce = f32[64]{0:T(128)S(1)} all-reduce(f32[64]{0:T(128)S(1)} %fusion.38), channel_id=2, replica_groups=mesh['head'=8,'group'=64] {'group'}, use_global_device_ids=true, to_apply=%add | all-reduce | flops 64 | bytes 512
  146.7 167.5 %all-gather.14.cloned.1.call-done = f32[16384,512]{1,0:T(8,128)} async-done(((f32[256,512]{1,0:T(8,128)}), f32[16384,512]{1,0:T(8,128)}) %all-gather.14.cloned.1.call-update) | async-done | bytes 33554448 | tf_op jit(solution)/shard_map/all_gather | solution.py:9
  314.2 163.2 %while.34 = (s32[]{:T(128)}, f32[1,256,512]{2,1,0:T(8,128)S(1)}, s32[]{:T(128)}, f32[64,1]{0,1:T(1,128)S(1)}, f32[64,1,256,512]{3,2,1,0:T(8,128)}, /*index=5*/s32[]{:T(128)}, s32[]{:T(128)}) while((s32[]{:T(128)}, f32[1,256,512]{2,1,0:T(8,128)S(1)}, s32[]{:T(128)}, f32[64,1]{0,1:T(1,128)S(1)}, f32[64,1,256,512]{3,2,1,0:T(8,128)}, ...), condition=%wide.region_7.8_spmd.clone, body=%wide.region_6.7_spmd.clone.sunk | while | flops 524292 | bytes 1572981 | solution.py:21
  314.7 1.9 fusion.55
  317.3 1.9 fusion.55
  319.8 1.9 fusion.55
  322.4 1.9 fusion.55
  324.9 1.9 fusion.55
  327.5 1.9 fusion.55
  330.0 1.9 fusion.55
  332.6 1.9 fusion.55
  335.1 1.9 fusion.55
  337.7 1.9 fusion.55
  340.2 1.9 fusion.55
  342.8 1.9 fusion.55
  345.3 1.9 fusion.55
  347.9 1.9 fusion.55
  350.4 1.9 fusion.55
  353.0 1.9 fusion.55
  355.5 1.9 fusion.55
  358.1 1.9 fusion.55
  360.6 1.9 fusion.55
  363.2 1.9 fusion.55
  365.7 1.9 fusion.55
  368.3 1.9 fusion.55
  370.8 1.9 fusion.55
  373.4 1.9 fusion.55
  375.9 1.9 fusion.55
  378.5 1.9 fusion.55
  381.0 1.9 fusion.55
  383.6 1.9 fusion.55
  386.1 1.9 fusion.55
  388.7 1.9 fusion.55
  391.2 1.9 fusion.55
  393.8 1.9 fusion.55
  396.3 1.9 fusion.55
  398.9 1.9 fusion.55
  401.4 1.9 fusion.55
  404.0 1.9 fusion.55
  406.5 1.9 fusion.55
  409.1 1.9 fusion.55
  411.6 1.9 fusion.55
  414.2 1.9 fusion.55
  416.7 1.9 fusion.55
  419.3 1.9 fusion.55
  421.8 1.9 fusion.55
  424.4 1.9 fusion.55
  426.9 1.9 fusion.55
  429.5 1.9 fusion.55
  432.0 1.9 fusion.55
  434.6 1.9 fusion.55
  437.1 1.9 fusion.55
  439.7 1.9 fusion.55
  480.4 72.8 %all-reduce.3.cloned.1.call-done = f32[128,2048]{1,0:T(8,128)} async-done(((f32[128,2048]{1,0:T(8,128)}), f32[128,2048]{1,0:T(8,128)}) %all-reduce.3.cloned.1.call-update) | async-done | bytes 1048592 | tf_op jit(solution)/shard_map/psum | solution.py:141
  557.2 63.4 %all-gather.5 = s32[64,1,16]{2,1,0:T(1,128)S(1)} all-gather(s32[1,1,16]{2,1,0:T(1,128)S(1)} %bitcast.113), channel_id=1, replica_groups=mesh['head'=8,'group'=64] {'group'}, dimensions={0}, use_global_device_ids=true | all-gather | bytes 4160 | tf_op jit(solution)/shard_map/all_gather | solution.py:152
  623.5 107.8 %all-gather.10.cloned.1.call-done = bf16[1024,2048]{1,0:T(8,128)(2,1)} async-done(((bf16[16,2048]{1,0:T(8,128)(2,1)}), bf16[1024,2048]{1,0:T(8,128)(2,1)}) %all-gather.10.cloned.1.call-update) | async-done | bytes 4194320 | tf_op jit(solution)/shard_map/all_gather | solution.py:154
  731.3 6.2 fusion.45
  738.3 61.6 %all-gather.3 = f32[65536]{0:T(1024)S(1)} all-gather(f32[1024]{0:T(1024)S(1)} %get-tuple-element.318), channel_id=5, replica_groups=mesh['head'=8,'group'=64] {'group'}, dimensions={0}, use_global_device_ids=true | all-gather | bytes 266240 | tf_op jit(solution)/shard_map/all_gather | solution.py:25
  800.0 62.9 %all-gather.4 = f32[65536]{0:T(1024)S(1)} all-gather(f32[1024]{0:T(1024)S(1)} %get-tuple-element.317), channel_id=6, replica_groups=mesh['head'=8,'group'=64] {'group'}, dimensions={0}, use_global_device_ids=true | all-gather | bytes 266240 | tf_op jit(solution)/shard_map/all_gather | solution.py:25
  863.0 63.5 %all-gather.2 = f32[65536]{0:T(1024)S(1)} all-gather(f32[1024]{0:T(1024)S(1)} %get-tuple-element.355), channel_id=4, replica_groups=mesh['head'=8,'group'=64] {'group'}, dimensions={0}, use_global_device_ids=true | all-gather | bytes 266240 | tf_op jit(solution)/shard_map/all_gather | solution.py:25
  926.6 5.9 while.33
  933.3 162.6 %psum.15 = f32[32]{0:T(128)S(1)} all-reduce(f32[32]{0:T(128)S(1)} %select_reduce_fusion.1), channel_id=1, replica_groups=mesh['head'=8,'group'=64] {'head','group'}, use_global_device_ids=true, to_apply=%region_19.20 | all-reduce | flops 32 | bytes 256 | tf_op jit(solution)/shard_map/psum | solution.py:179
  (405 shorter events, 88.4 us)
Async XLA Ops:
  7.2 470.9 %copy-start = (bf16[512,2048]{1,0:T(8,128)(2,1)S(1)}, bf16[512,2048]{1,0:T(8,128)(2,1)}, u32[]{:S(2)}) copy-start(bf16[512,2048]{1,0:T(8,128)(2,1)} %param.22) | copy-start | bytes 6291460
  7.2 307.0 %all-gather.14.cloned.1.call-start = ((), (), s32[]{:S(2)}) async-start(), calls=%async_computation.3 | async-start | bytes 34078720 | tf_op jit(solution)/shard_map/all_gather | solution.py:9
  15.6 537.5 %all-reduce.3.cloned.1.call-start = ((), (), s32[]{:S(2)}) async-start(), calls=%async_computation | async-start | bytes 2097152 | tf_op jit(solution)/shard_map/psum | solution.py:141
  314.2 163.2 %copy-start.2 = (bf16[128,256]{1,0:T(8,128)(2,1)S(1)}, bf16[128,256]{1,0:T(8,128)(2,1)}, u32[]{:S(2)}) copy-start(bf16[128,256]{1,0:T(8,128)(2,1)} %param.17) | copy-start | bytes 196612
  314.2 163.9 %copy-start.8 = (bf16[128,512]{1,0:T(8,128)(2,1)S(1)}, bf16[128,512]{1,0:T(8,128)(2,1)}, u32[]{:S(2)}) copy-start(bf16[128,512]{1,0:T(8,128)(2,1)} %param.20) | copy-start | bytes 393220
  477.4 75.8 %copy-start.1 = (bf16[1,16,2048]{2,1,0:T(8,128)(2,1)S(1)}, bf16[1,16,2048]{2,1,0:T(8,128)(2,1)}, u32[]{:S(2)}) copy-start(bf16[1,16,2048]{2,1,0:T(8,128)(2,1)} %param.23) | copy-start | bytes 196612
  477.8 77.5 %copy-start.3 = (f32[2048]{0:T(1024)S(1)}, f32[2048]{0:T(1024)}, u32[]{:S(2)}) copy-start(f32[2048]{0:T(1024)} %param.24) | copy-start | bytes 24580
  478.0 79.2 %copy-start.4 = (s32[1,16]{1,0:T(1,128)S(1)}, s32[1,16]{1,0:T(1,128)}, u32[]{:S(2)}) copy-start(s32[1,16]{1,0:T(1,128)} %param.26) | copy-start | bytes 196
  479.6 143.9 %all-gather.12.cloned.1.call-start = ((), (), s32[]{:S(2)}) async-start(), calls=%async_computation.2 | async-start | bytes 3538944 | tf_op jit(solution)/shard_map/all_gather | solution.py:147
  480.4 251.0 %all-gather.10.cloned.1.call-start = ((), (), s32[]{:S(2)}) async-start(), calls=%async_computation.1 | async-start | bytes 4259840 | tf_op jit(solution)/shard_map/all_gather | solution.py:154
  737.5 195.0 %copy-start.6 = (f32[1,16]{1,0:T(1,128)S(1)}, f32[1,16]{1,0:T(1,128)}, u32[]{:S(2)}) copy-start(f32[1,16]{1,0:T(1,128)} %param.27) | copy-start | bytes 196
  737.6 195.0 %copy-start.7 = (s32[1,16]{1,0:T(1,128)S(1)}, s32[1,16]{1,0:T(1,128)}, u32[]{:S(2)}) copy-start(s32[1,16]{1,0:T(1,128)} %param.28) | copy-start | bytes 196
  737.6 358.3 %copy-start.5 = (s32[32]{0:T(128)S(1)}, s32[32]{0:T(128)}, u32[]{:S(2)}) copy-start(s32[32]{0:T(128)} %param.29) | copy-start | bytes 388
Sparse Core Ops, SparseCore 0:
  15.8 298.3 all-gather.13
  479.7 73.3 all-reduce.2
  555.3 36.6 all-gather.11
  594.8 136.4 all-gather.9
where the time goes:
time: 1110 us; the launch traced here: 1100 us
  blocking collectives  539 us (49%)
  waiting for transfers between devices  349 us (31%)
  other arithmetic  139 us (13%)
  local copies, waits for them, and re-layouts  44.2 us (4%)
  between operations  16.6 us (1%)
  matrix products  11.8 us (1%)
    all_gather x3, blocking collectives, merged_2(): gathered = jax.tree.map(lambda a: lax.all_gather(a, axis), part)  188 us
    all_gather x1, waiting for transfers between devices, entering(): everything = jax.tree.map(lambda part: lax.all_gather(part, axis), value)  167 us
    psum x1, blocking collectives, per_device(): seq_total = lax.psum(partial_sums, ('head', 'group'))  163 us
    unnamed x1, blocking collectives  125 us
    select_n x64, other arithmetic, lap(): return jax.tree.map(lambda a, b: jnp.where(reached, a, b), new, before)  125 us
    all_gather x1, waiting for transfers between devices, per_device(): lax.all_gather(hidden, 'group', axis=0, tiled=True)  108 us
    psum x1, waiting for transfers between devices, per_device(): lax.psum(jnp.dot(gated_out, out_weight, preferred_element_type=jnp.float3...  72.8 us
    all_gather x1, blocking collectives, per_device(): lax.all_gather(targets, 'group', axis=0, tiled=True).reshape(-1)  63.4 us
  transfers between devices with their start and end apart: 4, of which 3 were waited for; matrix products, arithmetic and copies ran while one was open for 1% of the time, Pallas kernels for 0%

commit v1 on v0

--- a/solution.py
+++ b/solution.py
@@ -2,34 +2,6 @@
 import jax.numpy as jnp
 from jax import lax
 from jax.sharding import PartitionSpec as P
-
-
-def entering(value, axis, combine, identity):
-    size, index = (lax.axis_size(axis), lax.axis_index(axis))
-    everything = jax.tree.map(lambda part: lax.all_gather(part, axis), value)
-    start = jax.tree.map(
-        lambda part, zero: jnp.broadcast_to(jnp.asarray(zero, part.dtype), part.shape),
-        value,
-        identity,
-    )
-
-    def lap(k, before):
-        reached = k < index
-        new = combine(before, jax.tree.map(lambda part: part[k], everything))
-        return jax.tree.map(lambda a, b: jnp.where(reached, a, b), new, before)
-
-    return lax.fori_loop(0, size, lap, start)
-
-
-def merged_2(part, axis, combine):
-    gathered = jax.tree.map(lambda a: lax.all_gather(a, axis), part)
-
-    def take(source):
-        return jax.tree.map(lambda a: lax.dynamic_index_in_dim(a, source, 0, False), gathered)
-
-    return lax.fori_loop(
-        1, lax.axis_size(axis), lambda source, state: combine(state, take(source)), take(0)
-    )
 
 
 def layer_norm(stream, width_eps):
@@ -37,20 +9,6 @@
     centered = stream - mean_val
     var_val = jnp.mean(centered * centered, axis=-1, keepdims=True)
     return centered / jnp.sqrt(var_val + width_eps)
-
-
-def combine_state(earlier, later):
-    decay_first, state_first = earlier
-    decay_second, state_second = later
-    return (decay_first * decay_second, decay_second[:, None, None] * state_first + state_second)
-
-
-def combine_totals(first, second):
-    max_first, sum_first, target_first = first
-    max_second, sum_second, target_second = second
-    top = jnp.maximum(max_first, max_second)
-    merged = sum_first * jnp.exp(max_first - top) + sum_second * jnp.exp(max_second - top)
-    return (top, merged, target_first + target_second)
 
 
 def per_device(
@@ -115,12 +73,41 @@
         precision=highest_precision,
     )
     block_decay = jnp.where(jnp.all(continuation_flags), jnp.exp(cumulative_decay[-1]), 0.0)
-    decay_prefix, carried_state = entering(
-        (block_decay, block_total_sum),
-        "group",
-        combine_state,
-        (jnp.ones_like(block_decay), jnp.zeros_like(block_total_sum)),
+
+    assert heads_here == 1
+    chunk = key_width * value_width // group_count
+    extras = jnp.concatenate(
+        [
+            block_decay,
+            targets[0].astype(jnp.float32),
+            ref_logp[0],
+            response_mask[0].astype(jnp.float32),
+        ]
     )
+    extra_width = 128 * pl_cdiv(extras.shape[0], 128)
+    extras = jnp.pad(extras, (0, extra_width - extras.shape[0]))
+    payload = jnp.concatenate(
+        [
+            block_total_sum.reshape(group_count, chunk),
+            jnp.broadcast_to(extras[None, :], (group_count, extra_width)),
+        ],
+        axis=1,
+    )
+    received = lax.all_to_all(payload, "group", 0, 0, tiled=True)
+    slices_in = received[:, :chunk]
+    decay_all = received[:, chunk]
+    targets_all = received[:, chunk + 1 : chunk + 1 + slice_rows].astype(jnp.int32)
+    ref_all = received[:, chunk + 1 + slice_rows : chunk + 1 + 2 * slice_rows]
+    mask_all = received[:, chunk + 1 + 2 * slice_rows : chunk + 1 + 3 * slice_rows]
+    blk = jnp.arange(group_count, dtype=jnp.int32)
+    between = (blk[None, None, :] > blk[None, :, None]) & (blk[None, None, :] < blk[:, None, None])
+    weights = jnp.prod(jnp.where(between, decay_all[None, None, :], 1.0), axis=2)
+    weights = jnp.where(blk[None, :] < blk[:, None], weights, 0.0)
+    slices_out = jnp.dot(weights, slices_in, precision=highest_precision)
+    carried_state = lax.all_to_all(slices_out, "group", 0, 0, tiled=True).reshape(
+        heads_here, key_width, value_width
+    )
+
     query_as_float = query_heads.astype(jnp.float32)
     state_contribution = (
         jnp.einsum("ugo,gow->ugw", query_as_float, carried_state, precision=highest_precision)
@@ -138,10 +125,12 @@
         .astype(jnp.bfloat16)
         .reshape(tok_count, heads_here * value_width)
     )
-    full_branch = lax.psum(
-        jnp.dot(gated_out, out_weight, preferred_element_type=jnp.float32), "head"
+    own_branch = lax.psum_scatter(
+        jnp.dot(gated_out, out_weight, preferred_element_type=jnp.float32),
+        "head",
+        scatter_dimension=0,
+        tiled=True,
     )
-    own_branch = lax.dynamic_slice_in_dim(full_branch, head_index * slice_rows, slice_rows, 0)
     stream = residual[0].astype(jnp.float32) + own_branch
     hidden = (layer_norm(stream, 1e-05) * norm_gain).astype(jnp.bfloat16)
     vocab_rows = lax.all_gather(vocab_weight, "head", axis=0, tiled=True)
@@ -149,7 +138,7 @@
         (jnp.arange(head_count, dtype=jnp.int32)[:, None] * group_count + group_index) * vocab_here
         + jnp.arange(vocab_here, dtype=jnp.int32)[None, :]
     ).reshape(-1)
-    all_targets = lax.all_gather(targets, "group", axis=0, tiled=True).reshape(-1)
+    all_targets = targets_all.reshape(-1)
     logits = lax.dot_general(
         lax.all_gather(hidden, "group", axis=0, tiled=True),
         vocab_rows,
@@ -159,26 +148,30 @@
     top = jnp.max(logits, axis=1)
     exp_total = jnp.sum(jnp.exp(logits - top[:, None]), axis=1)
     picked = jnp.sum(jnp.where(entry_ids[None, :] == all_targets[:, None], logits, 0.0), axis=1)
-    merged_max, merged_total, merged_target = merged_2(
-        (top, exp_total, picked), "group", combine_totals
-    )
-    own_start = group_index * slice_rows
-    own_max = lax.dynamic_slice_in_dim(merged_max, own_start, slice_rows, 0)
-    own_total = lax.dynamic_slice_in_dim(merged_total, own_start, slice_rows, 0)
-    own_target = lax.dynamic_slice_in_dim(merged_target, own_start, slice_rows, 0)
-    token_logp = own_target - own_max - jnp.log(own_total)
-    token_ratio = response_mask[0].astype(jnp.float32) * (token_logp - ref_logp[0])
-    own_positions = (
-        group_index * tok_count + head_index * slice_rows + jnp.arange(slice_rows, dtype=jnp.int32)
-    )
-    own_seq = jnp.sum((own_positions[:, None] >= starts[None, 1:]).astype(jnp.int32), axis=1)
-    member = (own_seq[:, None] == jnp.arange(seq_count, dtype=jnp.int32)[None, :]).astype(
+    stats = lax.all_gather(jnp.stack([top, exp_total, picked]), "group")
+    merged_max = jnp.max(stats[:, 0], axis=0)
+    merged_total = jnp.sum(stats[:, 1] * jnp.exp(stats[:, 0] - merged_max[None, :]), axis=0)
+    merged_target = jnp.sum(stats[:, 2], axis=0)
+    token_logp = merged_target - merged_max - jnp.log(merged_total)
+    token_ratio = mask_all.reshape(-1) * (token_logp - ref_all.reshape(-1))
+    own_max = lax.dynamic_slice_in_dim(merged_max, group_index * slice_rows, slice_rows, 0)
+    token_positions = (
+        blk[:, None] * tok_count
+        + head_index * slice_rows
+        + jnp.arange(slice_rows, dtype=jnp.int32)[None, :]
+    ).reshape(-1)
+    token_seq = jnp.sum((token_positions[:, None] >= starts[None, 1:]).astype(jnp.int32), axis=1)
+    member = (token_seq[:, None] == jnp.arange(seq_count, dtype=jnp.int32)[None, :]).astype(
         jnp.float32
     )
     partial_sums = jnp.sum(member * token_ratio[:, None], axis=0)
-    seq_total = lax.psum(partial_sums, ("head", "group"))
+    seq_total = lax.psum(partial_sums, "head")
     seq_ratio = seq_total / seq_lengths.astype(jnp.float32)
     return (seq_ratio, state_norms, own_max[None, :])
+
+
+def pl_cdiv(a, b):
+    return (a + b - 1) // b
 
 
 def solution(mesh):

time: 1110 us -> 470 us (0.42)
  blocking collectives: 539 us -> 121 us
  other arithmetic: 139 us -> 16.7 us
  waiting for transfers between devices: 349 us -> 266 us
  local copies, waits for them, and re-layouts: 44.2 us -> 7.98 us
  starting transfers between devices: 0.16 us -> 26.8 us
    all_gather x4 -> x1, blocking collectives: 251 us -> 73.6 us  [per_device(): stats = lax.all_gather(jnp.stack([top, exp_total, picked]), 'group')]
    all_gather x1 -> x0, waiting for transfers between devices: 167 us -> none  [entering(): everything = jax.tree.map(lambda part: lax.all_gather(part, axis), value)]
    unnamed x1 -> x0, blocking collectives: 125 us -> none
    select_n x64 -> x0, other arithmetic: 125 us -> none  [lap(): return jax.tree.map(lambda a, b: jnp.where(reached, a, b), new, before)]
    psum x1, blocking collectives: 163 us -> 47.5 us  [per_device(): seq_total = lax.psum(partial_sums, 'head')]
    psum x1 -> x0, waiting for transfers between devices: 72.8 us -> none  [per_device(): lax.psum(jnp.dot(gated_out, out_weight, preferred_element_type=jnp.float3...]
    all_to_all x0 -> x2, waiting for transfers between devices: none -> 59.9 us  [the longest x1 32 us: per_device(): received = lax.all_to_all(payload, 'group', 0, 0, tiled=True)]
    dynamic_slice x193 -> x0, local copies, waits for them, and re-layouts: 39.2 us -> none  [the longest x64 37.4 us: lap(): new = combine(before, jax.tree.map(lambda part: part[k], everything))]
  transfers between devices with their start and end apart: 4 -> 5, of which waited for: 3 -> 5; matrix products, arithmetic and copies ran while one was open for 1% -> 1% of each run, Pallas kernels for 0% -> 0%
where the time goes in v1:
time: 470 us; the launch traced here: 469 us
  waiting for transfers between devices  266 us (57%)
  blocking collectives  121 us (26%)
  starting transfers between devices  26.8 us (6%)
  between operations  17.2 us (4%)
  other arithmetic  16.7 us (4%)
  matrix products  13.3 us (3%)
  local copies, waits for them, and re-layouts  7.98 us (2%)
    all_gather x1, waiting for transfers between devices, per_device(): lax.all_gather(hidden, 'group', axis=0, tiled=True)  140 us
    all_gather x1, blocking collectives, per_device(): stats = lax.all_gather(jnp.stack([top, exp_total, picked]), 'group')  73.6 us
    psum x1, blocking collectives, per_device(): seq_total = lax.psum(partial_sums, 'head')  47.5 us
    all_gather x1, waiting for transfers between devices, per_device(): vocab_rows = lax.all_gather(vocab_weight, 'head', axis=0, tiled=True)  33.1 us
    reduce_scatter x1, waiting for transfers between devices, per_device(): lax.psum_scatter(jnp.dot(gated_out, out_weight, preferred_element_type=jn...  32.8 us
    all_to_all x1, waiting for transfers between devices, per_device(): received = lax.all_to_all(payload, 'group', 0, 0, tiled=True)  32 us
    all_to_all x1, waiting for transfers between devices, per_device(): lax.all_to_all(slices_out, 'group', 0, 0, tiled=True)  27.9 us
    all_to_all x1, starting transfers between devices, per_device(): received = lax.all_to_all(payload, 'group', 0, 0, tiled=True)  19.3 us
  transfers between devices with their start and end apart: 5, of which 5 were waited for; matrix products, arithmetic and copies ran while one was open for 1% of the time, Pallas kernels for 0%

profile of v1, /device:TPU:1, one launch (start us, length us, event | category | flops | bytes accessed | tf_op | source)
XLA Modules:
  0.0 469.1 jit_solution(7822007279205202960)
XLA Ops:
  7.2 0.0 copy-start
  7.2 0.9 copy.34
  8.1 0.1 reduce-window.9
  8.1 0.1 reduce.8
  8.3 0.7 sub.94
  8.9 0.1 slice.42
  9.0 0.1 compare_reduce_fusion
  9.1 0.1 convert_reduce_fusion.1
  9.2 0.6 fusion.46
  9.8 0.8 copy.35
  10.6 0.2 reduce_window_sum.20
  10.7 0.6 slice.55
  12.1 0.1 reduce.9
  12.2 1.3 fusion.45
  13.5 2.0 select_multiply_fusion
  15.4 1.4 fusion.21
  16.9 0.2 reshape.415
  17.1 0.7 convert_bitcast_fusion
  18.4 0.7 select_maximum_fusion
  19.2 1.2 all_to_all.14
  20.3 19.3 %all-to-all-start = ((f32[64,1,2176]{2,1,0:T(1,128)}), f32[64,1,2176]{2,1,0:T(1,128)S(1)}, u32[]{:S(2)}, u32[]{:S(2)}) async-start(f32[64,1,2176]{2,1,0:T(1,128)} %all_to_all.14), calls=%async_computation | async-start | bytes 1114112 | tf_op jit(solution)/shard_map/all_to_all | solution.py:96
  39.6 32.0 %all-to-all-done = f32[64,1,2176]{2,1,0:T(1,128)S(1)} async-done(((f32[64,1,2176]{2,1,0:T(1,128)}), f32[64,1,2176]{2,1,0:T(1,128)S(1)}, u32[]{:S(2)}, u32[]{:S(2)}) %all-to-all-start) | async-done | bytes 557088 | tf_op jit(solution)/shard_map/all_to_all | solution.py:96
  71.7 0.1 slice_reduce_fusion.1
  71.8 1.2 select_reduce_fusion.1
  73.0 0.6 convolution_bitcast_fusion
  73.6 1.3 copy.36
  74.9 7.2 %all-to-all-start.1 = ((f32[64,1,2048]{2,1,0:T(1,128)}), f32[64,1,2048]{2,1,0:T(1,128)S(1)}, u32[]{:S(2)}, u32[]{:S(2)}) async-start(f32[64,1,2048]{2,1,0:T(1,128)} %copy.36), calls=%async_computation.1 | async-start | bytes 1048576 | tf_op jit(solution)/shard_map/all_to_all | solution.py:107
  82.1 0.0 reduce-scatter.2.cloned.1.call-start
  82.1 1.4 convolution_bitcast_fusion.2
  83.5 27.9 %all-to-all-done.1 = f32[64,1,2048]{2,1,0:T(1,128)S(1)} async-done(((f32[64,1,2048]{2,1,0:T(1,128)}), f32[64,1,2048]{2,1,0:T(1,128)S(1)}, u32[]{:S(2)}, u32[]{:S(2)}) %all-to-all-start.1) | async-done | bytes 524320 | tf_op jit(solution)/shard_map/all_to_all | solution.py:107
  111.4 3.0 multiply_reduce_fusion
  114.5 1.2 reshape.418
  115.7 1.3 fusion.47
  117.0 0.2 multiply_reduce_fusion.1
  117.2 2.4 fusion.16
  119.6 0.0 reduce-scatter.2.cloned.1.call-update
  119.7 0.0 all-gather.7.cloned.1.call-start
  119.7 0.7 all-gather.7.cloned.1.call-update
  120.4 0.2 all-gather.5.cloned.1.call-start
  120.6 32.8 %reduce-scatter.2.cloned.1.call-done = f32[16,2048]{1,0:T(8,128)} async-done(((f32[128,2048]{1,0:T(8,128)}), f32[16,2048]{1,0:T(8,128)}) %reduce-scatter.2.cloned.1.call-update) | async-done | bytes 131088 | tf_op jit(solution)/shard_map/reduce_scatter | solution.py:128
  153.5 1.0 fusion.32
  154.5 1.1 multiply_reduce_fusion.2
  155.6 1.6 multiply_convert_fusion
  157.2 0.0 all-gather.5.cloned.1.call-update
  157.3 0.1 iota_add_fusion.1
  157.3 0.1 add.141
  157.4 0.1 iota_add_fusion
  157.5 0.1 add.127
  157.6 0.1 convert_reduce_fusion
  157.7 0.1 slice_convert_fusion
  157.8 0.1 eq.97
  157.8 0.1 reshape.420
  157.9 0.1 reshape.416
  158.7 33.1 %all-gather.7.cloned.1.call-done = bf16[768,2048]{1,0:T(8,128)(2,1)} async-done(((bf16[96,2048]{1,0:T(8,128)(2,1)}), bf16[768,2048]{1,0:T(8,128)(2,1)}) %all-gather.7.cloned.1.call-update) | async-done | bytes 3145744 | tf_op jit(solution)/shard_map/all_gather | solution.py:136
  191.8 139.5 %all-gather.5.cloned.1.call-done = bf16[1024,2048]{1,0:T(8,128)(2,1)} async-done(((bf16[16,2048]{1,0:T(8,128)(2,1)}), bf16[1024,2048]{1,0:T(8,128)(2,1)}) %all-gather.5.cloned.1.call-update) | async-done | bytes 4194320 | tf_op jit(solution)/shard_map/all_gather | solution.py:143
  331.3 6.2 %fusion.48 = (f32[1024]{0:T(1024)S(1)}, f32[1024,768]{0,1:T(8,128)S(1)}) fusion(bf16[1024,2048]{1,0:T(8,128)(2,1)} %all-gather.5.cloned.1.call-done, bf16[768,2048]{1,0:T(8,128)(2,1)} %all-gather.7.cloned.1.call-done), kind=kOutput, calls=%fused_computation.98 | convolution fusion | flops 3222010880 | bytes 10489856 | tf_op jit(solution)/shard_map/dot_general | solution.py:142
  337.6 0.7 exponential_reduce_fusion
  338.4 73.6 %all-gather.1 = f32[64,3,1024]{2,1,0:T(4,128)S(1)} all-gather(f32[1,3,1024]{2,1,0:T(4,128)S(1)} %maximum_bitcast_fusion), channel_id=2, replica_groups=mesh['head'=8,'group'=64] {'group'}, dimensions={0}, use_global_device_ids=true | all-gather | bytes 798720 | tf_op jit(solution)/shard_map/all_gather | solution.py:151
  411.9 0.6 slice_reduce_fusion
  412.6 0.6 dynamic-slice_bitcast_fusion
  413.2 0.1 fusion.14
  413.3 0.1 select_reduce_fusion.2
  413.4 47.5 %psum.7 = f32[32]{0:T(128)S(1)} all-reduce(f32[32]{0:T(128)S(1)} %select_reduce_fusion.2), channel_id=1, replica_groups=mesh['head'=8,'group'=64] {'head'}, use_global_device_ids=true, to_apply=%region_19.20 | all-reduce | flops 32 | bytes 256 | tf_op jit(solution)/shard_map/psum | solution.py:168
  460.9 0.5 convert_divide_fusion
  (20 shorter events, 0.2 us)
Async XLA Ops:
  7.2 110.0 %copy-start = (bf16[512,2048]{1,0:T(8,128)(2,1)S(1)}, bf16[512,2048]{1,0:T(8,128)(2,1)}, u32[]{:S(2)}) copy-start(bf16[512,2048]{1,0:T(8,128)(2,1)} %param.18) | copy-start | bytes 6291460
  20.3 51.3 %all-to-all-start = ((f32[64,1,2176]{2,1,0:T(1,128)}), f32[64,1,2176]{2,1,0:T(1,128)S(1)}, u32[]{:S(2)}, u32[]{:S(2)}) async-start(f32[64,1,2176]{2,1,0:T(1,128)} %all_to_all.14), calls=%async_computation | async-start | bytes 1114112 | tf_op jit(solution)/shard_map/all_to_all | solution.py:96
  74.9 36.6 %all-to-all-start.1 = ((f32[64,1,2048]{2,1,0:T(1,128)}), f32[64,1,2048]{2,1,0:T(1,128)S(1)}, u32[]{:S(2)}, u32[]{:S(2)}) async-start(f32[64,1,2048]{2,1,0:T(1,128)} %copy.36), calls=%async_computation.1 | async-start | bytes 1048576 | tf_op jit(solution)/shard_map/all_to_all | solution.py:107
  82.1 71.4 %reduce-scatter.2.cloned.1.call-start = ((), (), s32[]{:S(2)}) async-start(), calls=%async_computation.3 | async-start | bytes 1179648 | tf_op jit(solution)/shard_map/reduce_scatter | solution.py:128
  115.7 37.8 %copy-start.1 = (bf16[1,16,2048]{2,1,0:T(8,128)(2,1)S(1)}, bf16[1,16,2048]{2,1,0:T(8,128)(2,1)}, u32[]{:S(2)}) copy-start(bf16[1,16,2048]{2,1,0:T(8,128)(2,1)} %param.19) | copy-start | bytes 196612
  117.0 38.6 %copy-start.2 = (f32[2048]{0:T(1024)S(1)}, f32[2048]{0:T(1024)}, u32[]{:S(2)}) copy-start(f32[2048]{0:T(1024)} %param.20) | copy-start | bytes 24580
  119.7 72.1 %all-gather.7.cloned.1.call-start = ((), (), s32[]{:S(2)}) async-start(), calls=%async_computation.5 | async-start | bytes 3538944 | tf_op jit(solution)/shard_map/all_gather | solution.py:136
  120.4 210.9 %all-gather.5.cloned.1.call-start = ((), (), s32[]{:S(2)}) async-start(), calls=%async_computation.4 | async-start | bytes 4259840 | tf_op jit(solution)/shard_map/all_gather | solution.py:143
  337.6 123.3 %copy-start.3 = (s32[32]{0:T(128)S(1)}, s32[32]{0:T(128)}, u32[]{:S(2)}) copy-start(s32[32]{0:T(128)} %param.25) | copy-start | bytes 388
Sparse Core Ops, SparseCore 0:
  119.8 33.6 reduce-scatter.1
  155.6 36.1 all-gather.6
  194.8 136.5 all-gather.4

commit v2 on v1

--- a/solution.py
+++ b/solution.py
@@ -28,9 +28,9 @@
 ):
     highest_precision = lax.Precision.HIGHEST
     head_count = lax.axis_size("head")
-    group_count = lax.axis_size("group")
+    group_count = lax.axis_size(("ga", "gb"))
     head_index = lax.axis_index("head")
-    group_index = lax.axis_index("group")
+    group_index = lax.axis_index(("ga", "gb"))
     tok_count = query_proj.shape[0]
     heads_here = log_decay.shape[1]
     key_width = query_proj.shape[1] // heads_here
@@ -76,14 +76,7 @@
 
     assert heads_here == 1
     chunk = key_width * value_width // group_count
-    extras = jnp.concatenate(
-        [
-            block_decay,
-            targets[0].astype(jnp.float32),
-            ref_logp[0],
-            response_mask[0].astype(jnp.float32),
-        ]
-    )
+    extras = block_decay
     extra_width = 128 * pl_cdiv(extras.shape[0], 128)
     extras = jnp.pad(extras, (0, extra_width - extras.shape[0]))
     payload = jnp.concatenate(
@@ -93,18 +86,15 @@
         ],
         axis=1,
     )
-    received = lax.all_to_all(payload, "group", 0, 0, tiled=True)
+    received = lax.all_to_all(payload, ("ga", "gb"), 0, 0, tiled=True)
     slices_in = received[:, :chunk]
     decay_all = received[:, chunk]
-    targets_all = received[:, chunk + 1 : chunk + 1 + slice_rows].astype(jnp.int32)
-    ref_all = received[:, chunk + 1 + slice_rows : chunk + 1 + 2 * slice_rows]
-    mask_all = received[:, chunk + 1 + 2 * slice_rows : chunk + 1 + 3 * slice_rows]
     blk = jnp.arange(group_count, dtype=jnp.int32)
     between = (blk[None, None, :] > blk[None, :, None]) & (blk[None, None, :] < blk[:, None, None])
     weights = jnp.prod(jnp.where(between, decay_all[None, None, :], 1.0), axis=2)
     weights = jnp.where(blk[None, :] < blk[:, None], weights, 0.0)
     slices_out = jnp.dot(weights, slices_in, precision=highest_precision)
-    carried_state = lax.all_to_all(slices_out, "group", 0, 0, tiled=True).reshape(
+    carried_state = lax.all_to_all(slices_out, ("ga", "gb"), 0, 0, tiled=True).reshape(
         heads_here, key_width, value_width
     )
 
@@ -133,14 +123,30 @@
     )
     stream = residual[0].astype(jnp.float32) + own_branch
     hidden = (layer_norm(stream, 1e-05) * norm_gain).astype(jnp.bfloat16)
-    vocab_rows = lax.all_gather(vocab_weight, "head", axis=0, tiled=True)
+
+    sub = lax.axis_size("gb")
+    ga_index = lax.axis_index("ga")
+    gb_index = lax.axis_index("gb")
+    code = jnp.concatenate([targets[0] // 256, targets[0] % 256]).astype(jnp.bfloat16)
+    code_row = jnp.pad(code, (0, hidden.shape[1] - code.shape[0]))[None, :]
+    hidden_ext = jnp.concatenate([hidden, code_row], axis=0)
+    gathered = lax.all_gather(lax.all_gather(hidden_ext, "head"), "gb")
+    hidden_all = gathered[:, :, :slice_rows, :].reshape(-1, hidden.shape[1])
+    code_all = gathered[:, :, slice_rows, : 2 * slice_rows].astype(jnp.int32)
+    all_targets = (code_all[..., :slice_rows] * 256 + code_all[..., slice_rows:]).reshape(-1)
+    vocab_rows = lax.all_gather(vocab_weight, "ga", axis=0, tiled=True)
+    part_count = lax.axis_size("ga")
     entry_ids = (
-        (jnp.arange(head_count, dtype=jnp.int32)[:, None] * group_count + group_index) * vocab_here
+        (
+            head_index * group_count
+            + jnp.arange(part_count, dtype=jnp.int32)[:, None] * sub
+            + gb_index
+        )
+        * vocab_here
         + jnp.arange(vocab_here, dtype=jnp.int32)[None, :]
     ).reshape(-1)
-    all_targets = targets_all.reshape(-1)
     logits = lax.dot_general(
-        lax.all_gather(hidden, "group", axis=0, tiled=True),
+        hidden_all,
         vocab_rows,
         (((1,), (1,)), ((), ())),
         preferred_element_type=jnp.float32,
@@ -148,24 +154,39 @@
     top = jnp.max(logits, axis=1)
     exp_total = jnp.sum(jnp.exp(logits - top[:, None]), axis=1)
     picked = jnp.sum(jnp.where(entry_ids[None, :] == all_targets[:, None], logits, 0.0), axis=1)
-    stats = lax.all_gather(jnp.stack([top, exp_total, picked]), "group")
+    own_mask = response_mask[0].astype(jnp.float32)
+    own_positions = positions[0] + head_index * slice_rows + jnp.arange(slice_rows, dtype=jnp.int32)
+    own_seq = jnp.sum((own_positions[:, None] >= starts[None, 1:]).astype(jnp.int32), axis=1)
+    own_member = (own_seq[:, None] == jnp.arange(seq_count, dtype=jnp.int32)[None, :]).astype(
+        jnp.float32
+    )
+    ref_sums = jnp.sum(own_member * (own_mask * ref_logp[0])[:, None], axis=0)
+    token_count = top.shape[0]
+    side = jnp.concatenate([ref_sums, own_mask])
+    side = jnp.pad(side, (0, token_count - side.shape[0]))
+    stats = lax.all_gather(jnp.stack([top, exp_total, picked, side]), ("head", "gb"))
     merged_max = jnp.max(stats[:, 0], axis=0)
     merged_total = jnp.sum(stats[:, 1] * jnp.exp(stats[:, 0] - merged_max[None, :]), axis=0)
     merged_target = jnp.sum(stats[:, 2], axis=0)
     token_logp = merged_target - merged_max - jnp.log(merged_total)
-    token_ratio = mask_all.reshape(-1) * (token_logp - ref_all.reshape(-1))
-    own_max = lax.dynamic_slice_in_dim(merged_max, group_index * slice_rows, slice_rows, 0)
+    class_ref = jnp.sum(stats[:, 3, :seq_count], axis=0)
+    class_mask = jnp.transpose(
+        stats[:, 3, seq_count : seq_count + slice_rows].reshape(head_count, sub, slice_rows),
+        (1, 0, 2),
+    ).reshape(-1)
+    own_max = lax.dynamic_slice_in_dim(
+        merged_max, (gb_index * head_count + head_index) * slice_rows, slice_rows, 0
+    )
     token_positions = (
-        blk[:, None] * tok_count
-        + head_index * slice_rows
-        + jnp.arange(slice_rows, dtype=jnp.int32)[None, :]
+        (ga_index * sub + jnp.arange(sub, dtype=jnp.int32))[:, None] * tok_count
+        + jnp.arange(tok_count, dtype=jnp.int32)[None, :]
     ).reshape(-1)
     token_seq = jnp.sum((token_positions[:, None] >= starts[None, 1:]).astype(jnp.int32), axis=1)
     member = (token_seq[:, None] == jnp.arange(seq_count, dtype=jnp.int32)[None, :]).astype(
         jnp.float32
     )
-    partial_sums = jnp.sum(member * token_ratio[:, None], axis=0)
-    seq_total = lax.psum(partial_sums, "head")
+    partial_sums = jnp.sum(member * (class_mask * token_logp)[:, None], axis=0) - class_ref
+    seq_total = lax.psum(partial_sums, "ga")
     seq_ratio = seq_total / seq_lengths.astype(jnp.float32)
     return (seq_ratio, state_norms, own_max[None, :])
 
@@ -175,25 +196,33 @@
 
 
 def solution(mesh):
+    from jax.sharding import Mesh
+
+    head_size, group_size = mesh.devices.shape
+    sub = 8 if group_size % 8 == 0 else 1
+    fine = Mesh(
+        mesh.devices.reshape(head_size, group_size // sub, sub), ("head", "ga", "gb")
+    )
+    group = ("ga", "gb")
     placed = (
-        P("group", "head"),
-        P("group", "head"),
-        P("group", "head"),
-        P("group", "head"),
-        P("group", "head"),
+        P(group, "head"),
+        P(group, "head"),
+        P(group, "head"),
+        P(group, "head"),
+        P(group, "head"),
         P("head", None),
-        P("group", "head", None),
+        P(group, "head", None),
         P(),
-        P(("head", "group"), None),
-        P("group", "head"),
-        P("group", "head"),
-        P("group", "head"),
+        P(("head", "ga", "gb"), None),
+        P(group, "head"),
+        P(group, "head"),
+        P(group, "head"),
         P(),
     )
     return jax.shard_map(
         per_device,
-        mesh=mesh,
+        mesh=fine,
         in_specs=placed,
-        out_specs=(P(), P("group", "head"), P("group", "head")),
+        out_specs=(P(), P(group, "head"), P(group, "head")),
         check_vma=False,
     )

time: 470 us -> 517 us (1.10)
  waiting for transfers between devices: 266 us -> 390 us
  blocking collectives: 121 us -> 34.1 us
  local copies, waits for them, and re-layouts: 7.98 us -> 16.1 us
    all_gather x2 -> x3, waiting for transfers between devices: 173 us -> 295 us  [the longest x1 160 us: per_device(): lax.all_gather(jnp.stack([top, exp_total, picked, side]), ('head', 'gb'))]
    all_gather x1, blocking collectives: 73.6 us -> 15.4 us  [per_device(): gathered = lax.all_gather(lax.all_gather(hidden_ext, 'head'), 'gb')]
    psum x1, blocking collectives: 47.5 us -> 18.7 us  [per_device(): seq_total = lax.psum(partial_sums, 'ga')]
    all_gather x0 -> x2, local copies, waits for them, and re-layouts: none -> 6.03 us  [per_device(): gathered = lax.all_gather(lax.all_gather(hidden_ext, 'head'), 'gb')]
  transfers between devices with their start and end apart: 5 -> 6, of which waited for: 5 -> 6; matrix products, arithmetic and copies ran while one was open for 1% -> 2% of each run, Pallas kernels for 0% -> 0%
where the time goes in v2:
time: 517 us; the launch traced here: 515 us
  waiting for transfers between devices  390 us (75%)
  blocking collectives  34.1 us (7%)
  starting transfers between devices  26.8 us (5%)
  other arithmetic  18.7 us (4%)
  between operations  17.4 us (3%)
  local copies, waits for them, and re-layouts  16.1 us (3%)
  matrix products  11.5 us (2%)
    all_gather x1, waiting for transfers between devices, per_device(): lax.all_gather(jnp.stack([top, exp_total, picked, side]), ('head', 'gb'))  160 us
    all_gather x1, waiting for transfers between devices, per_device(): vocab_rows = lax.all_gather(vocab_weight, 'ga', axis=0, tiled=True)  74.6 us
    all_gather x1, waiting for transfers between devices, per_device(): gathered = lax.all_gather(lax.all_gather(hidden_ext, 'head'), 'gb')  60.5 us
    reduce_scatter x1, waiting for transfers between devices, per_device(): lax.psum_scatter(jnp.dot(gated_out, out_weight, preferred_element_type=jn...  33.6 us
    all_to_all x1, waiting for transfers between devices, per_device(): received = lax.all_to_all(payload, ('ga', 'gb'), 0, 0, tiled=True)  32 us
    all_to_all x1, waiting for transfers between devices, per_device(): lax.all_to_all(slices_out, ('ga', 'gb'), 0, 0, tiled=True)  28.9 us
    all_to_all x1, starting transfers between devices, per_device(): received = lax.all_to_all(payload, ('ga', 'gb'), 0, 0, tiled=True)  19.3 us
    psum x1, blocking collectives, per_device(): seq_total = lax.psum(partial_sums, 'ga')  18.7 us
  transfers between devices with their start and end apart: 6, of which 6 were waited for; matrix products, arithmetic and copies ran while one was open for 2% of the time, Pallas kernels for 0%

profile of v2, /device:TPU:1, one launch (start us, length us, event | category | flops | bytes accessed | tf_op | source)
XLA Modules:
  0.0 514.7 jit_solution(11105353993521949024)
XLA Ops:
  7.2 0.9 copy.48
  8.1 0.1 reduce.9
  8.3 0.7 sub.96
  8.9 0.1 slice.55
  9.0 0.1 compare_reduce_fusion
  9.1 0.1 convert_reduce_fusion.1
  9.2 0.6 fusion.52
  9.8 0.8 copy.49
  10.6 0.2 reduce_window_sum.18
  10.7 0.6 slice.72
  12.1 0.1 reduce.10
  12.2 1.3 fusion.51
  14.0 2.0 select_multiply_fusion
  16.0 1.4 fusion.22
  17.5 0.2 reshape.428
  17.8 1.2 all_to_all.14
  19.0 19.3 %all-to-all-start = ((f32[64,1,2176]{2,1,0:T(1,128)}), f32[64,1,2176]{2,1,0:T(1,128)S(1)}, u32[]{:S(2)}, u32[]{:S(2)}) async-start(f32[64,1,2176]{2,1,0:T(1,128)} %all_to_all.14), calls=%async_computation | async-start | bytes 1114112 | tf_op jit(solution)/shard_map/all_to_all | solution.py:89
  38.3 32.0 %all-to-all-done = f32[64,1,2176]{2,1,0:T(1,128)S(1)} async-done(((f32[64,1,2176]{2,1,0:T(1,128)}), f32[64,1,2176]{2,1,0:T(1,128)S(1)}, u32[]{:S(2)}, u32[]{:S(2)}) %all-to-all-start) | async-done | bytes 557088 | tf_op jit(solution)/shard_map/all_to_all | solution.py:89
  70.3 0.1 slice_reduce_fusion.2
  70.4 1.2 select_reduce_fusion.1
  71.6 0.6 convolution_bitcast_fusion
  72.2 1.3 copy.50
  73.5 7.2 %all-to-all-start.1 = ((f32[64,1,2048]{2,1,0:T(1,128)}), f32[64,1,2048]{2,1,0:T(1,128)S(1)}, u32[]{:S(2)}, u32[]{:S(2)}) async-start(f32[64,1,2048]{2,1,0:T(1,128)} %copy.50), calls=%async_computation.1 | async-start | bytes 1048576 | tf_op jit(solution)/shard_map/all_to_all | solution.py:97
  80.8 0.4 convolution_bitcast_fusion.2
  81.2 28.9 %all-to-all-done.1 = f32[64,1,2048]{2,1,0:T(1,128)S(1)} async-done(((f32[64,1,2048]{2,1,0:T(1,128)}), f32[64,1,2048]{2,1,0:T(1,128)S(1)}, u32[]{:S(2)}, u32[]{:S(2)}) %all-to-all-start.1) | async-done | bytes 524320 | tf_op jit(solution)/shard_map/all_to_all | solution.py:97
  110.1 2.7 multiply_reduce_fusion
  112.8 0.1 reshape.429
  113.0 0.4 fusion.53
  113.4 0.2 multiply_reduce_fusion.1
  113.6 2.4 fusion.17
  116.2 0.1 fusion.44
  116.3 33.6 %reduce-scatter.2.cloned.1.call-done = f32[16,2048]{1,0:T(8,128)} async-done(((f32[128,2048]{1,0:T(8,128)}), f32[16,2048]{1,0:T(8,128)}) %reduce-scatter.2.cloned.1.call-update) | async-done | bytes 131088 | tf_op jit(solution)/shard_map/reduce_scatter | solution.py:118
  149.9 1.0 fusion.33
  150.9 1.1 multiply_reduce_fusion.2
  152.1 1.0 multiply_convert_fusion
  153.1 15.4 %all-gather.3 = bf16[8,17,2048]{2,1,0:T(8,128)(2,1)S(1)} all-gather(bf16[1,17,2048]{2,1,0:T(8,128)(2,1)S(1)} %maximum_bitcast_fusion), channel_id=2, replica_groups=mesh['head'=8,'ga'=8,'gb'=8] {'head'}, dimensions={0}, use_global_device_ids=true | all-gather | bytes 626688 | tf_op jit(solution)/shard_map/all_gather | solution.py:133
  168.5 1.1 copy.52
  169.7 0.7 all-gather.9.cloned.1.call-update
  170.4 0.2 all-gather.13.cloned.1.call-start
  170.7 0.1 iota_add_fusion
  170.7 0.1 add.188
  170.9 0.2 convert_reduce_fusion.2
  171.1 0.1 select_reduce_fusion.3
  171.2 0.1 select_maximum_fusion
  171.2 60.5 %all-gather.11.cloned.1.call-done = bf16[64,17,2048]{2,0,1:T(8,128)(2,1)} async-done(((bf16[8,17,2048]{2,0,1:T(8,128)(2,1)}), bf16[64,17,2048]{2,0,1:T(8,128)(2,1)}) %all-gather.11.cloned.1.call-update) | async-done | bytes 4456464 | tf_op jit(solution)/shard_map/all_gather | solution.py:133
  231.7 4.9 copy.53
  236.6 2.2 slice.75
  238.9 0.1 slice_add_fusion
  239.0 0.1 eq.112
  239.1 74.6 %all-gather.9.cloned.1.call-done = bf16[768,2048]{1,0:T(8,128)(2,1)} async-done(((bf16[96,2048]{1,0:T(8,128)(2,1)}), bf16[768,2048]{1,0:T(8,128)(2,1)}) %all-gather.9.cloned.1.call-update) | async-done | bytes 3145744 | tf_op jit(solution)/shard_map/all_gather | solution.py:137
  313.6 6.2 %fusion.54 = (f32[1024]{0:T(1024)S(1)}, f32[1024,768]{0,1:T(8,128)S(1)}) fusion(bf16[1024,2048]{1,0:T(8,128)(2,1)} %bitcast.134, bf16[768,2048]{1,0:T(8,128)(2,1)} %all-gather.9.cloned.1.call-done), kind=kOutput, calls=%fused_computation.118 | convolution fusion | flops 3222010880 | bytes 10489856 | tf_op jit(solution)/shard_map/dot_general | solution.py:148
  319.9 0.7 exponential_reduce_fusion
  320.6 0.6 maximum_bitcast_fusion.1
  321.4 0.1 convert_reduce_fusion
  322.2 159.8 %all-gather.13.cloned.1.call-done = f32[64,4,1024]{2,1,0:T(4,128)} async-done(((f32[1,4,1024]{2,1,0:T(4,128)}), f32[64,4,1024]{2,1,0:T(4,128)}) %all-gather.13.cloned.1.call-update) | async-done | bytes 1048592 | tf_op jit(solution)/shard_map/all_gather | solution.py:167
  482.0 1.0 slice.79
  483.1 0.1 reshape.432
  483.1 2.9 slice_reduce_fusion
  486.0 0.6 dynamic-slice_bitcast_fusion
  486.6 0.1 fusion.16
  486.7 0.1 select_reduce_fusion.2
  486.8 1.0 slice_reduce_fusion.1
  487.8 18.7 %psum.7 = f32[32]{0:T(128)S(1)} all-reduce(f32[32]{0:T(128)S(1)} %sub.115), channel_id=1, replica_groups=mesh['head'=8,'ga'=8,'gb'=8] {'ga'}, use_global_device_ids=true, to_apply=%region_22.23 | all-reduce | flops 32 | bytes 256 | tf_op jit(solution)/shard_map/psum | solution.py:189
  506.5 0.5 convert_divide_fusion
  (49 shorter events, 0.6 us)
Async XLA Ops:
  7.2 106.5 %copy-start = (bf16[512,2048]{1,0:T(8,128)(2,1)S(1)}, bf16[512,2048]{1,0:T(8,128)(2,1)}, u32[]{:S(2)}) copy-start(bf16[512,2048]{1,0:T(8,128)(2,1)} %param.18) | copy-start | bytes 6291460
  17.8 63.0 %copy-start.2 = (bf16[128,512]{1,0:T(8,128)(2,1)S(1)}, bf16[128,512]{1,0:T(8,128)(2,1)}, u32[]{:S(2)}) copy-start(bf16[128,512]{1,0:T(8,128)(2,1)} %param.15) | copy-start | bytes 393220
  17.8 63.0 %copy-start.3 = (bf16[128,256]{1,0:T(8,128)(2,1)S(1)}, bf16[128,256]{1,0:T(8,128)(2,1)}, u32[]{:S(2)}) copy-start(bf16[128,256]{1,0:T(8,128)(2,1)} %param.14) | copy-start | bytes 196612
  17.8 63.0 %copy-start.4 = (bf16[128,256]{1,0:T(8,128)(2,1)S(1)}, bf16[128,256]{1,0:T(8,128)(2,1)}, u32[]{:S(2)}) copy-start(bf16[128,256]{1,0:T(8,128)(2,1)} %param.13) | copy-start | bytes 196612
  19.0 51.3 %all-to-all-start = ((f32[64,1,2176]{2,1,0:T(1,128)}), f32[64,1,2176]{2,1,0:T(1,128)S(1)}, u32[]{:S(2)}, u32[]{:S(2)}) async-start(f32[64,1,2176]{2,1,0:T(1,128)} %all_to_all.14), calls=%async_computation | async-start | bytes 1114112 | tf_op jit(solution)/shard_map/all_to_all | solution.py:89
  73.5 36.6 %all-to-all-start.1 = ((f32[64,1,2048]{2,1,0:T(1,128)}), f32[64,1,2048]{2,1,0:T(1,128)S(1)}, u32[]{:S(2)}, u32[]{:S(2)}) async-start(f32[64,1,2048]{2,1,0:T(1,128)} %copy.50), calls=%async_computation.1 | async-start | bytes 1048576 | tf_op jit(solution)/shard_map/all_to_all | solution.py:97
  80.7 69.2 %reduce-scatter.2.cloned.1.call-start = ((), (), s32[]{:S(2)}) async-start(), calls=%async_computation.3 | async-start | bytes 1179648 | tf_op jit(solution)/shard_map/reduce_scatter | solution.py:118
  113.0 3.2 copy-start.7
  113.0 36.9 %copy-start.1 = (bf16[1,16,2048]{2,1,0:T(8,128)(2,1)S(1)}, bf16[1,16,2048]{2,1,0:T(8,128)(2,1)}, u32[]{:S(2)}) copy-start(bf16[1,16,2048]{2,1,0:T(8,128)(2,1)} %param.19) | copy-start | bytes 196612
  113.0 39.1 %copy-start.5 = (f32[2048]{0:T(1024)S(1)}, f32[2048]{0:T(1024)}, u32[]{:S(2)}) copy-start(f32[2048]{0:T(1024)} %param.20) | copy-start | bytes 24580
  116.1 55.0 %copy-start.8 = (f32[1,16]{1,0:T(1,128)S(1)}, f32[1,16]{1,0:T(1,128)}, u32[]{:S(2)}) copy-start(f32[1,16]{1,0:T(1,128)} %param.23) | copy-start | bytes 196
  116.1 55.0 %copy-start.9 = (s32[1,16]{1,0:T(1,128)S(1)}, s32[1,16]{1,0:T(1,128)}, u32[]{:S(2)}) copy-start(s32[1,16]{1,0:T(1,128)} %param.24) | copy-start | bytes 196
  116.1 115.6 %all-gather.11.cloned.1.call-start = ((), (), s32[]{:S(2)}) async-start(), calls=%async_computation.5 | async-start | bytes 5013504 | tf_op jit(solution)/shard_map/all_gather | solution.py:133
  169.7 143.9 %all-gather.9.cloned.1.call-start = ((), (), s32[]{:S(2)}) async-start(), calls=%async_computation.4 | async-start | bytes 3538944 | tf_op jit(solution)/shard_map/all_gather | solution.py:137
  170.4 311.6 %all-gather.13.cloned.1.call-start = ((), (), s32[]{:S(2)}) async-start(), calls=%async_computation.6 | async-start | bytes 1064960 | tf_op jit(solution)/shard_map/all_gather | solution.py:167
  319.9 186.7 %copy-start.6 = (s32[32]{0:T(128)S(1)}, s32[32]{0:T(128)}, u32[]{:S(2)}) copy-start(s32[32]{0:T(128)} %param.25) | copy-start | bytes 388
Sparse Core Ops, SparseCore 0:
  116.2 33.6 reduce-scatter.1
  169.8 61.8 all-gather.10
  233.8 79.7 all-gather.8
  321.4 160.5 all-gather.12

commit v3 on v2

--- a/solution.py
+++ b/solution.py
@@ -98,6 +98,8 @@
         heads_here, key_width, value_width
     )
 
+    vocab_rows = lax.all_gather(vocab_weight, "ga", axis=0, tiled=True)
+    vocab_rows, carried_state = lax.optimization_barrier((vocab_rows, carried_state))
     query_as_float = query_heads.astype(jnp.float32)
     state_contribution = (
         jnp.einsum("ugo,gow->ugw", query_as_float, carried_state, precision=highest_precision)
@@ -134,7 +136,6 @@
     hidden_all = gathered[:, :, :slice_rows, :].reshape(-1, hidden.shape[1])
     code_all = gathered[:, :, slice_rows, : 2 * slice_rows].astype(jnp.int32)
     all_targets = (code_all[..., :slice_rows] * 256 + code_all[..., slice_rows:]).reshape(-1)
-    vocab_rows = lax.all_gather(vocab_weight, "ga", axis=0, tiled=True)
     part_count = lax.axis_size("ga")
     entry_ids = (
         (
@@ -154,39 +155,23 @@
     top = jnp.max(logits, axis=1)
     exp_total = jnp.sum(jnp.exp(logits - top[:, None]), axis=1)
     picked = jnp.sum(jnp.where(entry_ids[None, :] == all_targets[:, None], logits, 0.0), axis=1)
-    own_mask = response_mask[0].astype(jnp.float32)
+    outgoing = jnp.stack([top, exp_total, picked]).reshape(3, sub, head_count, slice_rows)
+    outgoing = jnp.transpose(outgoing, (2, 1, 0, 3)).reshape(head_count * sub, 3 * slice_rows)
+    incoming = lax.all_to_all(outgoing, ("head", "gb"), 0, 0, tiled=True).reshape(
+        head_count * sub, 3, slice_rows
+    )
+    own_max = jnp.max(incoming[:, 0], axis=0)
+    own_total = jnp.sum(incoming[:, 1] * jnp.exp(incoming[:, 0] - own_max[None, :]), axis=0)
+    own_target = jnp.sum(incoming[:, 2], axis=0)
+    token_logp = own_target - own_max - jnp.log(own_total)
+    token_ratio = response_mask[0].astype(jnp.float32) * (token_logp - ref_logp[0])
     own_positions = positions[0] + head_index * slice_rows + jnp.arange(slice_rows, dtype=jnp.int32)
     own_seq = jnp.sum((own_positions[:, None] >= starts[None, 1:]).astype(jnp.int32), axis=1)
-    own_member = (own_seq[:, None] == jnp.arange(seq_count, dtype=jnp.int32)[None, :]).astype(
+    member = (own_seq[:, None] == jnp.arange(seq_count, dtype=jnp.int32)[None, :]).astype(
         jnp.float32
     )
-    ref_sums = jnp.sum(own_member * (own_mask * ref_logp[0])[:, None], axis=0)
-    token_count = top.shape[0]
-    side = jnp.concatenate([ref_sums, own_mask])
-    side = jnp.pad(side, (0, token_count - side.shape[0]))
-    stats = lax.all_gather(jnp.stack([top, exp_total, picked, side]), ("head", "gb"))
-    merged_max = jnp.max(stats[:, 0], axis=0)
-    merged_total = jnp.sum(stats[:, 1] * jnp.exp(stats[:, 0] - merged_max[None, :]), axis=0)
-    merged_target = jnp.sum(stats[:, 2], axis=0)
-    token_logp = merged_target - merged_max - jnp.log(merged_total)
-    class_ref = jnp.sum(stats[:, 3, :seq_count], axis=0)
-    class_mask = jnp.transpose(
-        stats[:, 3, seq_count : seq_count + slice_rows].reshape(head_count, sub, slice_rows),
-        (1, 0, 2),
-    ).reshape(-1)
-    own_max = lax.dynamic_slice_in_dim(
-        merged_max, (gb_index * head_count + head_index) * slice_rows, slice_rows, 0
-    )
-    token_positions = (
-        (ga_index * sub + jnp.arange(sub, dtype=jnp.int32))[:, None] * tok_count
-        + jnp.arange(tok_count, dtype=jnp.int32)[None, :]
-    ).reshape(-1)
-    token_seq = jnp.sum((token_positions[:, None] >= starts[None, 1:]).astype(jnp.int32), axis=1)
-    member = (token_seq[:, None] == jnp.arange(seq_count, dtype=jnp.int32)[None, :]).astype(
-        jnp.float32
-    )
-    partial_sums = jnp.sum(member * (class_mask * token_logp)[:, None], axis=0) - class_ref
-    seq_total = lax.psum(partial_sums, "ga")
+    partial_sums = jnp.sum(member * token_ratio[:, None], axis=0)
+    seq_total = lax.psum(partial_sums, ("head", "ga", "gb"))
     seq_ratio = seq_total / seq_lengths.astype(jnp.float32)
     return (seq_ratio, state_norms, own_max[None, :])
 

time: 517 us -> 409 us (0.79)
  waiting for transfers between devices: 390 us -> 197 us
  blocking collectives: 34.1 us -> 118 us
  starting transfers between devices: 26.8 us -> 32.2 us
    all_gather x1 -> x0, waiting for transfers between devices: 160 us -> none  [per_device(): lax.all_gather(jnp.stack([top, exp_total, picked, side]), ('head', 'gb'))]
    psum x1, blocking collectives: 18.7 us -> 102 us  [per_device(): seq_total = lax.psum(partial_sums, ('head', 'ga', 'gb'))]
    all_gather x1, waiting for transfers between devices: 74.6 us -> 2.7 us  [per_device(): vocab_rows = lax.all_gather(vocab_weight, 'ga', axis=0, tiled=True)]
    all_to_all x1, waiting for transfers between devices: 28.9 us -> 42.8 us  [per_device(): lax.all_to_all(slices_out, ('ga', 'gb'), 0, 0, tiled=True)]
    all_to_all x1, waiting for transfers between devices: 32 us -> 45.2 us  [per_device(): received = lax.all_to_all(payload, ('ga', 'gb'), 0, 0, tiled=True)]
    all_to_all x0 -> x1, starting transfers between devices: none -> 6.52 us  [per_device(): lax.all_to_all(outgoing, ('head', 'gb'), 0, 0, tiled=True)]
    all_to_all x0 -> x1, waiting for transfers between devices: none -> 6.36 us  [per_device(): lax.all_to_all(outgoing, ('head', 'gb'), 0, 0, tiled=True)]
  transfers between devices with their start and end apart: 6 -> 6, of which waited for: 6 -> 6; matrix products, arithmetic and copies ran while one was open for 2% -> 4% of each run, Pallas kernels for 0% -> 0%
where the time goes in v3:
time: 409 us; the launch traced here: 408 us
  waiting for transfers between devices  197 us (48%)
  blocking collectives  118 us (29%)
  starting transfers between devices  32.2 us (8%)
  between operations  17.3 us (4%)
  local copies, waits for them, and re-layouts  15.3 us (4%)
  other arithmetic  15 us (4%)
  matrix products  13.6 us (3%)
    psum x1, blocking collectives, per_device(): seq_total = lax.psum(partial_sums, ('head', 'ga', 'gb'))  102 us
    all_gather x1, waiting for transfers between devices, per_device(): gathered = lax.all_gather(lax.all_gather(hidden_ext, 'head'), 'gb')  61.8 us
    all_to_all x1, waiting for transfers between devices, per_device(): received = lax.all_to_all(payload, ('ga', 'gb'), 0, 0, tiled=True)  45.2 us
    all_to_all x1, waiting for transfers between devices, per_device(): lax.all_to_all(slices_out, ('ga', 'gb'), 0, 0, tiled=True)  42.8 us
    reduce_scatter x1, waiting for transfers between devices, per_device(): lax.psum_scatter(jnp.dot(gated_out, out_weight, preferred_element_type=jn...  37.8 us
    all_to_all x1, starting transfers between devices, per_device(): received = lax.all_to_all(payload, ('ga', 'gb'), 0, 0, tiled=True)  19.3 us
    all_gather x1, blocking collectives, per_device(): gathered = lax.all_gather(lax.all_gather(hidden_ext, 'head'), 'gb')  15.6 us
    dot_general x1, matrix products, per_device(): lax.dot_general(hidden_all, vocab_rows, (((1,), (1,)), ((), ())), preferr...  8.35 us
  transfers between devices with their start and end apart: 6, of which 6 were waited for; matrix products, arithmetic and copies ran while one was open for 4% of the time, Pallas kernels for 0%

profile of v3, /device:TPU:1, one launch (start us, length us, event | category | flops | bytes accessed | tf_op | source)
XLA Modules:
  0.0 408.2 jit_solution(647367555433837423)
XLA Ops:
  7.2 0.7 all-gather.6.cloned.1.call-update
  7.9 0.7 copy.49
  8.7 0.1 reduce-window.9
  8.7 0.1 reduce.7
  8.8 0.7 sub.100
  9.5 0.1 slice.49
  9.6 0.1 compare_reduce_fusion
  9.7 0.1 convert_reduce_fusion
  9.8 0.6 fusion.53
  10.4 0.8 copy.50
  11.2 0.2 reduce_window_sum.18
  11.3 0.5 slice.63
  11.8 0.1 reduce.8
  11.9 1.9 select_multiply_fusion
  13.8 1.4 fusion.19
  15.2 1.3 fusion.52
  17.1 0.2 reshape.412
  18.1 1.2 all_to_all.20
  19.3 19.3 %all-to-all-start = ((f32[64,1,2176]{2,1,0:T(1,128)}), f32[64,1,2176]{2,1,0:T(1,128)S(1)}, u32[]{:S(2)}, u32[]{:S(2)}) async-start(f32[64,1,2176]{2,1,0:T(1,128)} %all_to_all.20), calls=%async_computation | async-start | bytes 1114112 | tf_op jit(solution)/shard_map/all_to_all | solution.py:89
  38.5 45.2 %all-to-all-done = f32[64,1,2176]{2,1,0:T(1,128)S(1)} async-done(((f32[64,1,2176]{2,1,0:T(1,128)}), f32[64,1,2176]{2,1,0:T(1,128)S(1)}, u32[]{:S(2)}, u32[]{:S(2)}) %all-to-all-start) | async-done | bytes 557088 | tf_op jit(solution)/shard_map/all_to_all | solution.py:89
  83.8 0.1 slice_reduce_fusion
  83.9 1.2 select_reduce_fusion.1
  85.0 0.6 convolution_bitcast_fusion
  85.6 1.3 copy.51
  86.9 6.3 %all-to-all-start.1 = ((f32[64,1,2048]{2,1,0:T(1,128)}), f32[64,1,2048]{2,1,0:T(1,128)S(1)}, u32[]{:S(2)}, u32[]{:S(2)}) async-start(f32[64,1,2048]{2,1,0:T(1,128)} %copy.51), calls=%async_computation.1 | async-start | bytes 1048576 | tf_op jit(solution)/shard_map/all_to_all | solution.py:97
  93.3 0.4 convolution_bitcast_fusion.2
  93.7 42.8 %all-to-all-done.1 = f32[64,1,2048]{2,1,0:T(1,128)S(1)} async-done(((f32[64,1,2048]{2,1,0:T(1,128)}), f32[64,1,2048]{2,1,0:T(1,128)S(1)}, u32[]{:S(2)}, u32[]{:S(2)}) %all-to-all-start.1) | async-done | bytes 524320 | tf_op jit(solution)/shard_map/all_to_all | solution.py:97
  136.4 1.2 reduce.10
  137.7 0.1 reshape.413
  137.8 2.7 all-gather.6.cloned.1.call-done
  140.6 0.4 fusion.54
  141.0 0.2 multiply_reduce_fusion.1
  141.2 2.4 fusion.14
  143.7 0.1 fusion.44
  143.8 37.8 %reduce-scatter.2.cloned.1.call-done = f32[16,2048]{1,0:T(8,128)} async-done(((f32[128,2048]{1,0:T(8,128)}), f32[16,2048]{1,0:T(8,128)}) %reduce-scatter.2.cloned.1.call-update) | async-done | bytes 131088 | tf_op jit(solution)/shard_map/reduce_scatter | solution.py:120
  181.6 1.0 fusion.30
  182.7 1.1 multiply_reduce_fusion.2
  183.8 1.0 multiply_convert_fusion
  184.8 15.6 %all-gather.2 = bf16[8,17,2048]{2,1,0:T(8,128)(2,1)S(1)} all-gather(bf16[1,17,2048]{2,1,0:T(8,128)(2,1)S(1)} %maximum_bitcast_fusion), channel_id=2, replica_groups=mesh['head'=8,'ga'=8,'gb'=8] {'head'}, dimensions={0}, use_global_device_ids=true | all-gather | bytes 626688 | tf_op jit(solution)/shard_map/all_gather | solution.py:135
  200.4 1.1 copy.53
  201.6 0.1 iota_add_fusion
  201.6 0.1 add.147
  201.8 0.2 convert_reduce_fusion.1
  202.0 61.8 %all-gather.8.cloned.1.call-done = bf16[64,17,2048]{2,0,1:T(8,128)(2,1)} async-done(((bf16[8,17,2048]{2,0,1:T(8,128)(2,1)}), bf16[64,17,2048]{2,0,1:T(8,128)(2,1)}) %all-gather.8.cloned.1.call-update) | async-done | bytes 4456464 | tf_op jit(solution)/shard_map/all_gather | solution.py:135
  263.7 4.9 %copy.54 = bf16[64,17,2048]{2,1,0:T(8,128)(2,1)S(1)} copy(bf16[64,17,2048]{2,0,1:T(8,128)(2,1)} %all-gather.8.cloned.1.call-done) | data formatting | bytes 8912896 | tf_op jit(solution)/shard_map/all_gather | solution.py:135
  268.7 2.3 slice.66
  271.0 0.1 slice_add_fusion
  271.1 0.1 eq.99
  271.2 8.3 %fusion.55 = (f32[1024]{0:T(1024)S(1)}, f32[1024,768]{0,1:T(8,128)}) fusion(bf16[1024,2048]{1,0:T(8,128)(2,1)} %bitcast.128, bf16[768,2048]{1,0:T(8,128)(2,1)} %all-gather.6.cloned.1.call-done), kind=kOutput, calls=%fused_computation.109 | convolution fusion | flops 3222010880 | bytes 10489856 | tf_op jit(solution)/shard_map/dot_general | solution.py:149
  279.5 0.1 stack.12
  279.6 2.6 exponential_reduce_fusion
  282.2 0.1 stack.13
  282.3 0.1 stack.14
  282.4 0.1 copy.55
  282.5 0.7 all_to_all.25
  283.2 6.5 %all-to-all-start.2 = ((f32[64,1,48]{2,1,0:T(1,128)}), f32[64,1,48]{2,1,0:T(1,128)S(1)}, u32[]{:S(2)}, u32[]{:S(2)}) async-start(f32[64,1,48]{2,1,0:T(1,128)} %bitcast.27), calls=%async_computation.3 | async-start | bytes 65536 | tf_op jit(solution)/shard_map/all_to_all | solution.py:160
  289.7 0.7 multiply_reduce_fusion
  291.1 6.4 %all-to-all-done.2 = f32[64,1,48]{2,1,0:T(1,128)S(1)} async-done(((f32[64,1,48]{2,1,0:T(1,128)}), f32[64,1,48]{2,1,0:T(1,128)S(1)}, u32[]{:S(2)}, u32[]{:S(2)}) %all-to-all-start.2) | async-done | bytes 12320 | tf_op jit(solution)/shard_map/all_to_all | solution.py:160
  297.5 0.1 copy.57
  297.6 0.1 slice_reduce_fusion.1
  297.7 0.2 fusion.40
  297.9 0.1 select_reduce_fusion.2
  298.1 102.0 %psum.7 = f32[32]{0:T(128)S(1)} all-reduce(f32[32]{0:T(128)S(1)} %select_reduce_fusion.2), channel_id=1, replica_groups=mesh['head'=8,'ga'=8,'gb'=8] {'head','ga','gb'}, use_global_device_ids=true, to_apply=%region_19.20 | all-reduce | flops 32 | bytes 256 | tf_op jit(solution)/shard_map/psum | solution.py:174
  400.0 0.5 convert_divide_fusion
  (44 shorter events, 0.5 us)
Async XLA Ops:
  7.2 134.0 %copy-start = (bf16[512,2048]{1,0:T(8,128)(2,1)S(1)}, bf16[512,2048]{1,0:T(8,128)(2,1)}, u32[]{:S(2)}) copy-start(bf16[512,2048]{1,0:T(8,128)(2,1)} %param.18) | copy-start | bytes 6291460
  7.2 133.4 %all-gather.6.cloned.1.call-start = ((), (), s32[]{:S(2)}) async-start(), calls=%async_computation.4 | async-start | bytes 3538944 | tf_op jit(solution)/shard_map/all_gather | solution.py:101
  18.0 75.2 %copy-start.2 = (bf16[128,512]{1,0:T(8,128)(2,1)S(1)}, bf16[128,512]{1,0:T(8,128)(2,1)}, u32[]{:S(2)}) copy-start(bf16[128,512]{1,0:T(8,128)(2,1)} %param.15) | copy-start | bytes 393220
  18.0 75.2 %copy-start.3 = (bf16[128,256]{1,0:T(8,128)(2,1)S(1)}, bf16[128,256]{1,0:T(8,128)(2,1)}, u32[]{:S(2)}) copy-start(bf16[128,256]{1,0:T(8,128)(2,1)} %param.14) | copy-start | bytes 196612
  18.1 75.2 %copy-start.4 = (bf16[128,256]{1,0:T(8,128)(2,1)S(1)}, bf16[128,256]{1,0:T(8,128)(2,1)}, u32[]{:S(2)}) copy-start(bf16[128,256]{1,0:T(8,128)(2,1)} %param.13) | copy-start | bytes 196612
  19.3 64.5 %all-to-all-start = ((f32[64,1,2176]{2,1,0:T(1,128)}), f32[64,1,2176]{2,1,0:T(1,128)S(1)}, u32[]{:S(2)}, u32[]{:S(2)}) async-start(f32[64,1,2176]{2,1,0:T(1,128)} %all_to_all.20), calls=%async_computation | async-start | bytes 1114112 | tf_op jit(solution)/shard_map/all_to_all | solution.py:89
  86.9 49.5 %all-to-all-start.1 = ((f32[64,1,2048]{2,1,0:T(1,128)}), f32[64,1,2048]{2,1,0:T(1,128)S(1)}, u32[]{:S(2)}, u32[]{:S(2)}) async-start(f32[64,1,2048]{2,1,0:T(1,128)} %copy.51), calls=%async_computation.1 | async-start | bytes 1048576 | tf_op jit(solution)/shard_map/all_to_all | solution.py:97
  93.2 88.4 %reduce-scatter.2.cloned.1.call-start = ((), (), s32[]{:S(2)}) async-start(), calls=%async_computation.5 | async-start | bytes 1179648 | tf_op jit(solution)/shard_map/reduce_scatter | solution.py:120
  140.5 3.1 copy-start.10
  140.5 41.1 %copy-start.1 = (bf16[1,16,2048]{2,1,0:T(8,128)(2,1)S(1)}, bf16[1,16,2048]{2,1,0:T(8,128)(2,1)}, u32[]{:S(2)}) copy-start(bf16[1,16,2048]{2,1,0:T(8,128)(2,1)} %param.19) | copy-start | bytes 196612
  140.6 43.2 %copy-start.5 = (f32[2048]{0:T(1024)S(1)}, f32[2048]{0:T(1024)}, u32[]{:S(2)}) copy-start(f32[2048]{0:T(1024)} %param.20) | copy-start | bytes 24580
  143.6 120.1 %all-gather.8.cloned.1.call-start = ((), (), s32[]{:S(2)}) async-start(), calls=%async_computation.6 | async-start | bytes 5013504 | tf_op jit(solution)/shard_map/all_gather | solution.py:135
  279.5 18.4 %copy-start.8 = (f32[1,16]{1,0:T(1,128)S(1)}, f32[1,16]{1,0:T(1,128)}, u32[]{:S(2)}) copy-start(f32[1,16]{1,0:T(1,128)} %param.23) | copy-start | bytes 196
  279.5 18.4 %copy-start.9 = (s32[1,16]{1,0:T(1,128)S(1)}, s32[1,16]{1,0:T(1,128)}, u32[]{:S(2)}) copy-start(s32[1,16]{1,0:T(1,128)} %param.24) | copy-start | bytes 196
  279.5 120.5 %copy-start.7 = (s32[32]{0:T(128)S(1)}, s32[32]{0:T(128)}, u32[]{:S(2)}) copy-start(s32[32]{0:T(128)} %param.25) | copy-start | bytes 388
  283.2 14.3 %all-to-all-start.2 = ((f32[64,1,48]{2,1,0:T(1,128)}), f32[64,1,48]{2,1,0:T(1,128)S(1)}, u32[]{:S(2)}, u32[]{:S(2)}) async-start(f32[64,1,48]{2,1,0:T(1,128)} %bitcast.27), calls=%async_computation.3 | async-start | bytes 65536 | tf_op jit(solution)/shard_map/all_to_all | solution.py:160
  297.7 102.8 %copy-start.6 = (f32[16]{0:T(128)}, f32[16]{0:T(128)S(1)}, u32[]{:S(2)}) copy-start(f32[16]{0:T(128)S(1)} %get-tuple-element.10) | copy-start | bytes 196
Sparse Core Ops, SparseCore 0:
  10.1 130.4 all-gather.5
  143.8 37.8 reduce-scatter.1
  201.7 62.0 all-gather.7

commit v4 on v3

--- a/solution.py
+++ b/solution.py
@@ -171,7 +171,11 @@
         jnp.float32
     )
     partial_sums = jnp.sum(member * token_ratio[:, None], axis=0)
-    seq_total = lax.psum(partial_sums, ("head", "ga", "gb"))
+    seq_total = partial_sums
+    for axes in (("head", "gb"), "ga"):
+        width = lax.axis_size(axes)
+        spread = jnp.broadcast_to(seq_total[None, :], (width, seq_count))
+        seq_total = jnp.sum(lax.all_to_all(spread, axes, 0, 0, tiled=True), axis=0)
     seq_ratio = seq_total / seq_lengths.astype(jnp.float32)
     return (seq_ratio, state_norms, own_max[None, :])
 

time: 409 us -> 342 us (0.84)
  blocking collectives: 118 us -> 27.7 us
  waiting for transfers between devices: 197 us -> 209 us
  starting transfers between devices: 32.2 us -> 43.2 us
    psum x1 -> x0, blocking collectives: 102 us -> none  [per_device(): seq_total = lax.psum(partial_sums, ('head', 'ga', 'gb'))]
    all_to_all x0 -> x1, blocking collectives: none -> 12.2 us  [per_device(): seq_total = jnp.sum(lax.all_to_all(spread, axes, 0, 0, tiled=True), axis=0)]
    all_to_all x0 -> x1, starting transfers between devices: none -> 11 us  [per_device(): seq_total = jnp.sum(lax.all_to_all(spread, axes, 0, 0, tiled=True), axis=0)]
    all_to_all x0 -> x1, waiting for transfers between devices: none -> 9.9 us  [per_device(): seq_total = jnp.sum(lax.all_to_all(spread, axes, 0, 0, tiled=True), axis=0)]
  transfers between devices with their start and end apart: 6 -> 7, of which waited for: 6 -> 7; matrix products, arithmetic and copies ran while one was open for 4% -> 4% of each run, Pallas kernels for 0% -> 0%
where the time goes in v4:
time: 342 us; the launch traced here: 341 us
  waiting for transfers between devices  209 us (61%)
  starting transfers between devices  43.2 us (13%)
  blocking collectives  27.7 us (8%)
  between operations  17.3 us (5%)
  local copies, waits for them, and re-layouts  15.9 us (5%)
  other arithmetic  15.1 us (4%)
  matrix products  13.6 us (4%)
    all_gather x1, waiting for transfers between devices, per_device(): gathered = lax.all_gather(lax.all_gather(hidden_ext, 'head'), 'gb')  62 us
    all_to_all x1, waiting for transfers between devices, per_device(): received = lax.all_to_all(payload, ('ga', 'gb'), 0, 0, tiled=True)  45.2 us
    all_to_all x1, waiting for transfers between devices, per_device(): lax.all_to_all(slices_out, ('ga', 'gb'), 0, 0, tiled=True)  42.8 us
    reduce_scatter x1, waiting for transfers between devices, per_device(): lax.psum_scatter(jnp.dot(gated_out, out_weight, preferred_element_type=jn...  37.8 us
    all_to_all x1, starting transfers between devices, per_device(): received = lax.all_to_all(payload, ('ga', 'gb'), 0, 0, tiled=True)  19.3 us
    all_gather x1, blocking collectives, per_device(): gathered = lax.all_gather(lax.all_gather(hidden_ext, 'head'), 'gb')  15.6 us
    all_to_all x1, blocking collectives, per_device(): seq_total = jnp.sum(lax.all_to_all(spread, axes, 0, 0, tiled=True), axis=0)  12.2 us
    all_to_all x1, starting transfers between devices, per_device(): seq_total = jnp.sum(lax.all_to_all(spread, axes, 0, 0, tiled=True), axis=0)  11 us
  transfers between devices with their start and end apart: 7, of which 7 were waited for; matrix products, arithmetic and copies ran while one was open for 4% of the time, Pallas kernels for 0%

profile of v4, /device:TPU:1, one launch (start us, length us, event | category | flops | bytes accessed | tf_op | source)
XLA Modules:
  0.0 341.4 jit_solution(15336843613685963073)
XLA Ops:
  7.2 0.7 all-gather.6.cloned.1.call-update
  7.9 0.7 copy.58
  8.7 0.1 reduce.9
  8.8 0.7 sub.100
  9.5 0.1 slice.49
  9.6 0.1 compare_reduce_fusion
  9.7 0.1 convert_reduce_fusion
  9.8 0.6 fusion.53
  10.4 0.8 copy.59
  11.2 0.2 reduce_window_sum.18
  11.3 0.5 slice.63
  11.8 0.1 reduce.10
  11.9 1.9 select_multiply_fusion
  13.8 1.4 fusion.19
  15.2 1.3 fusion.52
  17.1 0.2 reshape.424
  18.1 1.2 all_to_all.28
  19.3 19.3 %all-to-all-start = ((f32[64,1,2176]{2,1,0:T(1,128)}), f32[64,1,2176]{2,1,0:T(1,128)S(1)}, u32[]{:S(2)}, u32[]{:S(2)}) async-start(f32[64,1,2176]{2,1,0:T(1,128)} %all_to_all.28), calls=%async_computation | async-start | bytes 1114112 | tf_op jit(solution)/shard_map/all_to_all | solution.py:89
  38.5 45.2 %all-to-all-done = f32[64,1,2176]{2,1,0:T(1,128)S(1)} async-done(((f32[64,1,2176]{2,1,0:T(1,128)}), f32[64,1,2176]{2,1,0:T(1,128)S(1)}, u32[]{:S(2)}, u32[]{:S(2)}) %all-to-all-start) | async-done | bytes 557088 | tf_op jit(solution)/shard_map/all_to_all | solution.py:89
  83.8 0.1 slice_reduce_fusion
  83.9 1.2 select_reduce_fusion.1
  85.0 0.6 convolution_bitcast_fusion
  85.6 1.3 copy.60
  86.9 6.3 %all-to-all-start.1 = ((f32[64,1,2048]{2,1,0:T(1,128)}), f32[64,1,2048]{2,1,0:T(1,128)S(1)}, u32[]{:S(2)}, u32[]{:S(2)}) async-start(f32[64,1,2048]{2,1,0:T(1,128)} %copy.60), calls=%async_computation.1 | async-start | bytes 1048576 | tf_op jit(solution)/shard_map/all_to_all | solution.py:97
  93.3 0.4 convolution_bitcast_fusion.2
  93.7 42.8 %all-to-all-done.1 = f32[64,1,2048]{2,1,0:T(1,128)S(1)} async-done(((f32[64,1,2048]{2,1,0:T(1,128)}), f32[64,1,2048]{2,1,0:T(1,128)S(1)}, u32[]{:S(2)}, u32[]{:S(2)}) %all-to-all-start.1) | async-done | bytes 524320 | tf_op jit(solution)/shard_map/all_to_all | solution.py:97
  136.4 1.2 reduce.12
  137.7 0.1 reshape.425
  137.8 2.7 all-gather.6.cloned.1.call-done
  140.6 0.4 fusion.54
  141.0 0.2 multiply_reduce_fusion.1
  141.2 2.4 fusion.14
  143.7 0.1 fusion.44
  143.8 37.8 %reduce-scatter.2.cloned.1.call-done = f32[16,2048]{1,0:T(8,128)} async-done(((f32[128,2048]{1,0:T(8,128)}), f32[16,2048]{1,0:T(8,128)}) %reduce-scatter.2.cloned.1.call-update) | async-done | bytes 131088 | tf_op jit(solution)/shard_map/reduce_scatter | solution.py:120
  181.6 1.0 fusion.30
  182.7 1.1 multiply_reduce_fusion.2
  183.8 1.0 multiply_convert_fusion
  184.8 15.6 %all-gather.2 = bf16[8,17,2048]{2,1,0:T(8,128)(2,1)S(1)} all-gather(bf16[1,17,2048]{2,1,0:T(8,128)(2,1)S(1)} %maximum_bitcast_fusion), channel_id=2, replica_groups=mesh['head'=8,'ga'=8,'gb'=8] {'head'}, dimensions={0}, use_global_device_ids=true | all-gather | bytes 626688 | tf_op jit(solution)/shard_map/all_gather | solution.py:135
  200.4 1.1 copy.62
  201.6 0.1 iota_add_fusion
  201.6 0.1 add.145
  201.8 62.0 %all-gather.8.cloned.1.call-done = bf16[64,17,2048]{2,0,1:T(8,128)(2,1)} async-done(((bf16[8,17,2048]{2,0,1:T(8,128)(2,1)}), bf16[64,17,2048]{2,0,1:T(8,128)(2,1)}) %all-gather.8.cloned.1.call-update) | async-done | bytes 4456464 | tf_op jit(solution)/shard_map/all_gather | solution.py:135
  263.7 4.9 %copy.63 = bf16[64,17,2048]{2,1,0:T(8,128)(2,1)S(1)} copy(bf16[64,17,2048]{2,0,1:T(8,128)(2,1)} %all-gather.8.cloned.1.call-done) | data formatting | bytes 8912896 | tf_op jit(solution)/shard_map/all_gather | solution.py:135
  268.7 2.3 slice.66
  271.0 0.1 slice_add_fusion
  271.1 0.1 eq.99
  271.2 8.3 %fusion.55 = (f32[1024]{0:T(1024)S(1)}, f32[1024,768]{0,1:T(8,128)}) fusion(bf16[1024,2048]{1,0:T(8,128)(2,1)} %bitcast.129, bf16[768,2048]{1,0:T(8,128)(2,1)} %all-gather.6.cloned.1.call-done), kind=kOutput, calls=%fused_computation.109 | convolution fusion | flops 3222010880 | bytes 10489856 | tf_op jit(solution)/shard_map/dot_general | solution.py:149
  279.5 0.1 stack.12
  279.6 2.6 exponential_reduce_fusion
  282.2 0.1 stack.13
  282.5 0.7 all_to_all.33
  283.2 6.5 %all-to-all-start.2 = ((f32[64,1,48]{2,1,0:T(1,128)}), f32[64,1,48]{2,1,0:T(1,128)S(1)}, u32[]{:S(2)}, u32[]{:S(2)}) async-start(f32[64,1,48]{2,1,0:T(1,128)} %bitcast.27), calls=%async_computation.3 | async-start | bytes 65536 | tf_op jit(solution)/shard_map/all_to_all | solution.py:160
  289.7 0.2 convert_reduce_fusion.1
  289.9 7.6 %all-to-all-done.2 = f32[64,1,48]{2,1,0:T(1,128)S(1)} async-done(((f32[64,1,48]{2,1,0:T(1,128)}), f32[64,1,48]{2,1,0:T(1,128)S(1)}, u32[]{:S(2)}, u32[]{:S(2)}) %all-to-all-start.2) | async-done | bytes 12320 | tf_op jit(solution)/shard_map/all_to_all | solution.py:160
  297.6 0.1 slice_reduce_fusion.1
  297.7 0.2 fusion.40
  297.9 0.1 select_reduce_fusion.2
  298.0 12.2 %all_to_all.42 = f32[64,1,32]{2,1,0:T(1,128)S(1)} all-to-all(f32[64,1,32]{2,1,0:T(1,128)S(1)} %broadcast_in_dim.49), channel_id=1, replica_groups=mesh['head'=8,'ga'=8,'gb'=8] {'head','gb'}, dimensions={0} | all-to-all | bytes 16384 | tf_op jit(solution)/shard_map/all_to_all | solution.py:178
  310.2 0.1 reduce_sum.137
  310.3 0.6 broadcast_in_dim.50
  310.9 11.0 %all-to-all-start.4 = ((f32[8,1,32]{2,1,0:T(1,128)}), f32[8,1,32]{2,1,0:T(1,128)S(1)}, u32[]{:S(2)}, u32[]{:S(2)}) async-start(f32[8,1,32]{2,1,0:T(1,128)} %broadcast_in_dim.50), calls=%async_computation.5 | async-start | bytes 8192 | tf_op jit(solution)/shard_map/all_to_all | solution.py:178
  321.9 0.7 multiply_reduce_fusion
  323.3 9.9 %all-to-all-done.4 = f32[8,1,32]{2,1,0:T(1,128)S(1)} async-done(((f32[8,1,32]{2,1,0:T(1,128)}), f32[8,1,32]{2,1,0:T(1,128)S(1)}, u32[]{:S(2)}, u32[]{:S(2)}) %all-to-all-start.4) | async-done | bytes 1056 | tf_op jit(solution)/shard_map/all_to_all | solution.py:178
  333.3 0.5 convert_divide_fusion
  (50 shorter events, 0.8 us)
Async XLA Ops:
  7.2 134.0 %copy-start = (bf16[512,2048]{1,0:T(8,128)(2,1)S(1)}, bf16[512,2048]{1,0:T(8,128)(2,1)}, u32[]{:S(2)}) copy-start(bf16[512,2048]{1,0:T(8,128)(2,1)} %param.18) | copy-start | bytes 6291460
  7.2 133.4 %all-gather.6.cloned.1.call-start = ((), (), s32[]{:S(2)}) async-start(), calls=%async_computation.6 | async-start | bytes 3538944 | tf_op jit(solution)/shard_map/all_gather | solution.py:101
  18.0 75.2 %copy-start.2 = (bf16[128,512]{1,0:T(8,128)(2,1)S(1)}, bf16[128,512]{1,0:T(8,128)(2,1)}, u32[]{:S(2)}) copy-start(bf16[128,512]{1,0:T(8,128)(2,1)} %param.15) | copy-start | bytes 393220
  18.0 75.2 %copy-start.3 = (bf16[128,256]{1,0:T(8,128)(2,1)S(1)}, bf16[128,256]{1,0:T(8,128)(2,1)}, u32[]{:S(2)}) copy-start(bf16[128,256]{1,0:T(8,128)(2,1)} %param.14) | copy-start | bytes 196612
  18.1 75.2 %copy-start.4 = (bf16[128,256]{1,0:T(8,128)(2,1)S(1)}, bf16[128,256]{1,0:T(8,128)(2,1)}, u32[]{:S(2)}) copy-start(bf16[128,256]{1,0:T(8,128)(2,1)} %param.13) | copy-start | bytes 196612
  19.3 64.5 %all-to-all-start = ((f32[64,1,2176]{2,1,0:T(1,128)}), f32[64,1,2176]{2,1,0:T(1,128)S(1)}, u32[]{:S(2)}, u32[]{:S(2)}) async-start(f32[64,1,2176]{2,1,0:T(1,128)} %all_to_all.28), calls=%async_computation | async-start | bytes 1114112 | tf_op jit(solution)/shard_map/all_to_all | solution.py:89
  86.9 49.5 %all-to-all-start.1 = ((f32[64,1,2048]{2,1,0:T(1,128)}), f32[64,1,2048]{2,1,0:T(1,128)S(1)}, u32[]{:S(2)}, u32[]{:S(2)}) async-start(f32[64,1,2048]{2,1,0:T(1,128)} %copy.60), calls=%async_computation.1 | async-start | bytes 1048576 | tf_op jit(solution)/shard_map/all_to_all | solution.py:97
  93.2 88.4 %reduce-scatter.2.cloned.1.call-start = ((), (), s32[]{:S(2)}) async-start(), calls=%async_computation.7 | async-start | bytes 1179648 | tf_op jit(solution)/shard_map/reduce_scatter | solution.py:120
  140.5 3.1 copy-start.10
  140.5 41.1 %copy-start.1 = (bf16[1,16,2048]{2,1,0:T(8,128)(2,1)S(1)}, bf16[1,16,2048]{2,1,0:T(8,128)(2,1)}, u32[]{:S(2)}) copy-start(bf16[1,16,2048]{2,1,0:T(8,128)(2,1)} %param.19) | copy-start | bytes 196612
  140.6 43.2 %copy-start.5 = (f32[2048]{0:T(1024)S(1)}, f32[2048]{0:T(1024)}, u32[]{:S(2)}) copy-start(f32[2048]{0:T(1024)} %param.20) | copy-start | bytes 24580
  143.6 120.1 %all-gather.8.cloned.1.call-start = ((), (), s32[]{:S(2)}) async-start(), calls=%async_computation.8 | async-start | bytes 5013504 | tf_op jit(solution)/shard_map/all_gather | solution.py:135
  279.5 18.4 %copy-start.8 = (f32[1,16]{1,0:T(1,128)S(1)}, f32[1,16]{1,0:T(1,128)}, u32[]{:S(2)}) copy-start(f32[1,16]{1,0:T(1,128)} %param.23) | copy-start | bytes 196
  279.5 18.4 %copy-start.9 = (s32[1,16]{1,0:T(1,128)S(1)}, s32[1,16]{1,0:T(1,128)}, u32[]{:S(2)}) copy-start(s32[1,16]{1,0:T(1,128)} %param.24) | copy-start | bytes 196
  279.5 53.7 %copy-start.7 = (s32[32]{0:T(128)S(1)}, s32[32]{0:T(128)}, u32[]{:S(2)}) copy-start(s32[32]{0:T(128)} %param.25) | copy-start | bytes 388
  283.2 14.3 %all-to-all-start.2 = ((f32[64,1,48]{2,1,0:T(1,128)}), f32[64,1,48]{2,1,0:T(1,128)S(1)}, u32[]{:S(2)}, u32[]{:S(2)}) async-start(f32[64,1,48]{2,1,0:T(1,128)} %bitcast.27), calls=%async_computation.3 | async-start | bytes 65536 | tf_op jit(solution)/shard_map/all_to_all | solution.py:160
  297.7 36.1 %copy-start.6 = (f32[16]{0:T(128)}, f32[16]{0:T(128)S(1)}, u32[]{:S(2)}) copy-start(f32[16]{0:T(128)S(1)} %get-tuple-element.10) | copy-start | bytes 196
  310.9 22.4 %all-to-all-start.4 = ((f32[8,1,32]{2,1,0:T(1,128)}), f32[8,1,32]{2,1,0:T(1,128)S(1)}, u32[]{:S(2)}, u32[]{:S(2)}) async-start(f32[8,1,32]{2,1,0:T(1,128)} %broadcast_in_dim.50), calls=%async_computation.5 | async-start | bytes 8192 | tf_op jit(solution)/shard_map/all_to_all | solution.py:178
Sparse Core Ops, SparseCore 0:
  10.1 130.4 all-gather.5
  143.8 37.8 reduce-scatter.1
  201.7 62.0 all-gather.7

commit v5 on v4

--- a/solution.py
+++ b/solution.py
@@ -133,7 +133,6 @@
     code_row = jnp.pad(code, (0, hidden.shape[1] - code.shape[0]))[None, :]
     hidden_ext = jnp.concatenate([hidden, code_row], axis=0)
     gathered = lax.all_gather(lax.all_gather(hidden_ext, "head"), "gb")
-    hidden_all = gathered[:, :, :slice_rows, :].reshape(-1, hidden.shape[1])
     code_all = gathered[:, :, slice_rows, : 2 * slice_rows].astype(jnp.int32)
     all_targets = (code_all[..., :slice_rows] * 256 + code_all[..., slice_rows:]).reshape(-1)
     part_count = lax.axis_size("ga")
@@ -147,10 +146,12 @@
         + jnp.arange(vocab_here, dtype=jnp.int32)[None, :]
     ).reshape(-1)
     logits = lax.dot_general(
-        hidden_all,
+        gathered.reshape(-1, hidden.shape[1]),
         vocab_rows,
         (((1,), (1,)), ((), ())),
         preferred_element_type=jnp.float32,
+    ).reshape(head_count * sub, slice_rows + 1, -1)[:, :slice_rows, :].reshape(
+        head_count * sub * slice_rows, -1
     )
     top = jnp.max(logits, axis=1)
     exp_total = jnp.sum(jnp.exp(logits - top[:, None]), axis=1)

time: 342 us -> 335 us (0.980)
  local copies, waits for them, and re-layouts: 15.9 us -> 8.84 us
    slice x0 -> x1, matrix products: none -> 8.45 us  [per_device(): lax.dot_general(gathered.reshape(-1, hidden.shape[1]), vocab_rows, (((1,)...]
    dot_general x1 -> x0, matrix products: 8.35 us -> none  [per_device(): lax.dot_general(hidden_all, vocab_rows, (((1,), (1,)), ((), ())), preferr...]
    all_gather x2 -> x1, local copies, waits for them, and re-layouts: 6.03 us -> 1.13 us  [per_device(): gathered = lax.all_gather(lax.all_gather(hidden_ext, 'head'), 'gb')]
  transfers between devices with their start and end apart: 7 -> 7, of which waited for: 7 -> 7; matrix products, arithmetic and copies ran while one was open for 4% -> 5% of each run, Pallas kernels for 0% -> 0%
where the time goes in v5:
time: 335 us
  waiting for transfers between devices  208 us (62%)
  starting transfers between devices  43.7 us (13%)
  blocking collectives  27.8 us (8%)
  between operations  17.4 us (5%)
  other arithmetic  15.8 us (5%)
  matrix products  13.7 us (4%)
  local copies, waits for them, and re-layouts  8.84 us (3%)
    all_gather x1, waiting for transfers between devices, per_device(): gathered = lax.all_gather(lax.all_gather(hidden_ext, 'head'), 'gb')  61.8 us
    all_to_all x1, waiting for transfers between devices, per_device(): received = lax.all_to_all(payload, ('ga', 'gb'), 0, 0, tiled=True)  45.4 us
    all_to_all x1, waiting for transfers between devices, per_device(): lax.all_to_all(slices_out, ('ga', 'gb'), 0, 0, tiled=True)  44.1 us
    reduce_scatter x1, waiting for transfers between devices, per_device(): lax.psum_scatter(jnp.dot(gated_out, out_weight, preferred_element_type=jn...  36.6 us
    all_to_all x1, starting transfers between devices, per_device(): received = lax.all_to_all(payload, ('ga', 'gb'), 0, 0, tiled=True)  19.3 us
    all_gather x1, blocking collectives, per_device(): gathered = lax.all_gather(lax.all_gather(hidden_ext, 'head'), 'gb')  15.6 us
    all_to_all x1, blocking collectives, per_device(): seq_total = jnp.sum(lax.all_to_all(spread, axes, 0, 0, tiled=True), axis=0)  12.2 us
    all_to_all x1, starting transfers between devices, per_device(): seq_total = jnp.sum(lax.all_to_all(spread, axes, 0, 0, tiled=True), axis=0)  11 us
  transfers between devices with their start and end apart: 7, of which 7 were waited for; matrix products, arithmetic and copies ran while one was open for 5% of the time, Pallas kernels for 0%

profile of v5, /device:TPU:1, one launch (start us, length us, event | category | flops | bytes accessed | tf_op | source)
XLA Modules:
  0.0 334.8 jit_solution(16525486086320937027)
XLA Ops:
  7.2 0.7 all-gather.6.cloned.1.call-update
  7.9 0.7 copy.68
  8.7 0.1 reduce.12
  8.8 0.7 sub.101
  9.5 0.1 slice.49
  9.6 0.1 compare_reduce_fusion
  9.7 0.1 convert_reduce_fusion
  9.8 0.6 fusion.57
  10.4 0.8 copy.69
  11.2 0.2 reduce_window_sum.18
  11.3 0.6 slice.63
  11.9 0.1 reduce.13
  12.0 2.0 select_multiply_fusion
  14.0 1.4 fusion.21
  15.5 1.3 fusion.56
  17.5 0.2 reshape.448
  18.5 1.2 all_to_all.28
  19.7 19.3 %all-to-all-start = ((f32[64,1,2176]{2,1,0:T(1,128)}), f32[64,1,2176]{2,1,0:T(1,128)S(1)}, u32[]{:S(2)}, u32[]{:S(2)}) async-start(f32[64,1,2176]{2,1,0:T(1,128)} %all_to_all.28), calls=%async_computation | async-start | bytes 1114112 | tf_op jit(solution)/shard_map/all_to_all | solution.py:89
  38.9 45.4 %all-to-all-done = f32[64,1,2176]{2,1,0:T(1,128)S(1)} async-done(((f32[64,1,2176]{2,1,0:T(1,128)}), f32[64,1,2176]{2,1,0:T(1,128)S(1)}, u32[]{:S(2)}, u32[]{:S(2)}) %all-to-all-start) | async-done | bytes 557088 | tf_op jit(solution)/shard_map/all_to_all | solution.py:89
  84.3 0.1 slice_reduce_fusion
  84.5 1.2 select_reduce_fusion.1
  85.6 0.6 convolution_bitcast_fusion
  86.2 1.3 copy.70
  87.5 6.8 %all-to-all-start.1 = ((f32[64,1,2048]{2,1,0:T(1,128)}), f32[64,1,2048]{2,1,0:T(1,128)S(1)}, u32[]{:S(2)}, u32[]{:S(2)}) async-start(f32[64,1,2048]{2,1,0:T(1,128)} %copy.70), calls=%async_computation.1 | async-start | bytes 1048576 | tf_op jit(solution)/shard_map/all_to_all | solution.py:97
  94.4 0.4 convolution_bitcast_fusion.2
  94.8 44.1 %all-to-all-done.1 = f32[64,1,2048]{2,1,0:T(1,128)S(1)} async-done(((f32[64,1,2048]{2,1,0:T(1,128)}), f32[64,1,2048]{2,1,0:T(1,128)S(1)}, u32[]{:S(2)}, u32[]{:S(2)}) %all-to-all-start.1) | async-done | bytes 524320 | tf_op jit(solution)/shard_map/all_to_all | solution.py:97
  138.9 1.2 reduce.15
  140.2 0.1 reshape.449
  140.3 1.4 all-gather.6.cloned.1.call-done
  141.8 0.4 fusion.58
  142.2 0.2 multiply_reduce_fusion.1
  142.4 2.4 fusion.16
  145.0 0.1 fusion.48
  145.0 36.6 %reduce-scatter.2.cloned.1.call-done = f32[16,2048]{1,0:T(8,128)} async-done(((f32[128,2048]{1,0:T(8,128)}), f32[16,2048]{1,0:T(8,128)}) %reduce-scatter.2.cloned.1.call-update) | async-done | bytes 131088 | tf_op jit(solution)/shard_map/reduce_scatter | solution.py:120
  181.6 1.0 fusion.32
  182.7 1.1 multiply_reduce_fusion.2
  183.8 1.0 multiply_convert_fusion
  184.8 15.6 %all-gather.2 = bf16[8,17,2048]{2,1,0:T(8,128)(2,1)S(1)} all-gather(bf16[1,17,2048]{2,1,0:T(8,128)(2,1)S(1)} %maximum_bitcast_fusion), channel_id=2, replica_groups=mesh['head'=8,'ga'=8,'gb'=8] {'head'}, dimensions={0}, use_global_device_ids=true | all-gather | bytes 626688 | tf_op jit(solution)/shard_map/all_gather | solution.py:135
  200.4 1.1 copy.72
  201.6 0.1 iota_add_fusion
  201.7 0.1 add.145
  201.8 61.8 %all-gather.8.cloned.1.call-done = bf16[64,17,2048]{2,0,1:T(8,128)(2,1)} async-done(((bf16[8,17,2048]{2,0,1:T(8,128)(2,1)}), bf16[64,17,2048]{2,0,1:T(8,128)(2,1)}) %all-gather.8.cloned.1.call-update) | async-done | bytes 4456464 | tf_op jit(solution)/shard_map/all_gather | solution.py:135
  263.6 8.5 %fusion.59 = (f32[64,16]{0,1:T(8,128)S(1)}, f32[64,16,768]{2,0,1:T(8,128)}) fusion(bf16[64,17,2048]{2,0,1:T(8,128)(2,1)} %all-gather.8.cloned.1.call-done, bf16[768,2048]{1,0:T(8,128)(2,1)} %all-gather.6.cloned.1.call-done), kind=kOutput, calls=%fused_computation.113 | convolution fusion | flops 3222010880 | bytes 10752000 | tf_op jit(solution)/shard_map/slice | solution.py:148
  272.1 0.1 copy.73
  272.2 0.7 fusion.41
  272.9 0.1 fusion.33
  273.0 2.5 exponential_reduce_fusion
  275.5 0.1 copy.74
  275.6 0.1 copy.76
  275.7 0.1 copy.77
  275.8 0.7 all_to_all.33
  276.5 6.5 %all-to-all-start.2 = ((f32[64,1,48]{2,1,0:T(1,128)}), f32[64,1,48]{2,1,0:T(1,128)S(1)}, u32[]{:S(2)}, u32[]{:S(2)}) async-start(f32[64,1,48]{2,1,0:T(1,128)} %bitcast.32), calls=%async_computation.3 | async-start | bytes 65536 | tf_op jit(solution)/shard_map/all_to_all | solution.py:161
  283.0 0.2 convert_reduce_fusion.1
  283.2 7.6 %all-to-all-done.2 = f32[64,1,48]{2,1,0:T(1,128)S(1)} async-done(((f32[64,1,48]{2,1,0:T(1,128)}), f32[64,1,48]{2,1,0:T(1,128)S(1)}, u32[]{:S(2)}, u32[]{:S(2)}) %all-to-all-start.2) | async-done | bytes 12320 | tf_op jit(solution)/shard_map/all_to_all | solution.py:161
  290.9 0.1 slice_reduce_fusion.1
  291.0 0.2 fusion.44
  291.2 0.1 select_reduce_fusion.2
  291.4 12.2 %all_to_all.42 = f32[64,1,32]{2,1,0:T(1,128)S(1)} all-to-all(f32[64,1,32]{2,1,0:T(1,128)S(1)} %broadcast_in_dim.49), channel_id=1, replica_groups=mesh['head'=8,'ga'=8,'gb'=8] {'head','gb'}, dimensions={0} | all-to-all | bytes 16384 | tf_op jit(solution)/shard_map/all_to_all | solution.py:179
  303.5 0.1 reduce_sum.137
  303.6 0.6 broadcast_in_dim.50
  304.2 11.0 %all-to-all-start.4 = ((f32[8,1,32]{2,1,0:T(1,128)}), f32[8,1,32]{2,1,0:T(1,128)S(1)}, u32[]{:S(2)}, u32[]{:S(2)}) async-start(f32[8,1,32]{2,1,0:T(1,128)} %broadcast_in_dim.50), calls=%async_computation.5 | async-start | bytes 8192 | tf_op jit(solution)/shard_map/all_to_all | solution.py:179
  315.2 0.7 multiply_reduce_fusion
  316.7 9.9 %all-to-all-done.4 = f32[8,1,32]{2,1,0:T(1,128)S(1)} async-done(((f32[8,1,32]{2,1,0:T(1,128)}), f32[8,1,32]{2,1,0:T(1,128)S(1)}, u32[]{:S(2)}, u32[]{:S(2)}) %all-to-all-start.4) | async-done | bytes 1056 | tf_op jit(solution)/shard_map/all_to_all | solution.py:179
  326.6 0.5 convert_divide_fusion
  (48 shorter events, 0.6 us)
Async XLA Ops:
  7.2 135.2 %copy-start = (bf16[512,2048]{1,0:T(8,128)(2,1)S(1)}, bf16[512,2048]{1,0:T(8,128)(2,1)}, u32[]{:S(2)}) copy-start(bf16[512,2048]{1,0:T(8,128)(2,1)} %param.18) | copy-start | bytes 6291460
  7.2 134.6 %all-gather.6.cloned.1.call-start = ((), (), s32[]{:S(2)}) async-start(), calls=%async_computation.6 | async-start | bytes 3538944 | tf_op jit(solution)/shard_map/all_gather | solution.py:101
  18.4 75.9 %copy-start.2 = (bf16[128,512]{1,0:T(8,128)(2,1)S(1)}, bf16[128,512]{1,0:T(8,128)(2,1)}, u32[]{:S(2)}) copy-start(bf16[128,512]{1,0:T(8,128)(2,1)} %param.15) | copy-start | bytes 393220
  18.5 75.9 %copy-start.3 = (bf16[128,256]{1,0:T(8,128)(2,1)S(1)}, bf16[128,256]{1,0:T(8,128)(2,1)}, u32[]{:S(2)}) copy-start(bf16[128,256]{1,0:T(8,128)(2,1)} %param.14) | copy-start | bytes 196612
  18.5 75.9 %copy-start.4 = (bf16[128,256]{1,0:T(8,128)(2,1)S(1)}, bf16[128,256]{1,0:T(8,128)(2,1)}, u32[]{:S(2)}) copy-start(bf16[128,256]{1,0:T(8,128)(2,1)} %param.13) | copy-start | bytes 196612
  19.7 64.7 %all-to-all-start = ((f32[64,1,2176]{2,1,0:T(1,128)}), f32[64,1,2176]{2,1,0:T(1,128)S(1)}, u32[]{:S(2)}, u32[]{:S(2)}) async-start(f32[64,1,2176]{2,1,0:T(1,128)} %all_to_all.28), calls=%async_computation | async-start | bytes 1114112 | tf_op jit(solution)/shard_map/all_to_all | solution.py:89
  87.5 51.4 %all-to-all-start.1 = ((f32[64,1,2048]{2,1,0:T(1,128)}), f32[64,1,2048]{2,1,0:T(1,128)S(1)}, u32[]{:S(2)}, u32[]{:S(2)}) async-start(f32[64,1,2048]{2,1,0:T(1,128)} %copy.70), calls=%async_computation.1 | async-start | bytes 1048576 | tf_op jit(solution)/shard_map/all_to_all | solution.py:97
  94.3 87.3 %reduce-scatter.2.cloned.1.call-start = ((), (), s32[]{:S(2)}) async-start(), calls=%async_computation.7 | async-start | bytes 1179648 | tf_op jit(solution)/shard_map/reduce_scatter | solution.py:120
  141.8 3.2 copy-start.10
  141.8 39.9 %copy-start.1 = (bf16[1,16,2048]{2,1,0:T(8,128)(2,1)S(1)}, bf16[1,16,2048]{2,1,0:T(8,128)(2,1)}, u32[]{:S(2)}) copy-start(bf16[1,16,2048]{2,1,0:T(8,128)(2,1)} %param.19) | copy-start | bytes 196612
  141.8 42.0 %copy-start.5 = (f32[2048]{0:T(1024)S(1)}, f32[2048]{0:T(1024)}, u32[]{:S(2)}) copy-start(f32[2048]{0:T(1024)} %param.20) | copy-start | bytes 24580
  144.9 118.8 %all-gather.8.cloned.1.call-start = ((), (), s32[]{:S(2)}) async-start(), calls=%async_computation.8 | async-start | bytes 5013504 | tf_op jit(solution)/shard_map/all_gather | solution.py:135
  272.1 19.1 %copy-start.8 = (f32[1,16]{1,0:T(1,128)S(1)}, f32[1,16]{1,0:T(1,128)}, u32[]{:S(2)}) copy-start(f32[1,16]{1,0:T(1,128)} %param.23) | copy-start | bytes 196
  272.1 19.1 %copy-start.9 = (s32[1,16]{1,0:T(1,128)S(1)}, s32[1,16]{1,0:T(1,128)}, u32[]{:S(2)}) copy-start(s32[1,16]{1,0:T(1,128)} %param.24) | copy-start | bytes 196
  272.1 54.5 %copy-start.7 = (s32[32]{0:T(128)S(1)}, s32[32]{0:T(128)}, u32[]{:S(2)}) copy-start(s32[32]{0:T(128)} %param.25) | copy-start | bytes 388
  276.5 14.3 %all-to-all-start.2 = ((f32[64,1,48]{2,1,0:T(1,128)}), f32[64,1,48]{2,1,0:T(1,128)S(1)}, u32[]{:S(2)}, u32[]{:S(2)}) async-start(f32[64,1,48]{2,1,0:T(1,128)} %bitcast.32), calls=%async_computation.3 | async-start | bytes 65536 | tf_op jit(solution)/shard_map/all_to_all | solution.py:161
  291.0 36.1 %copy-start.6 = (f32[16]{0:T(128)}, f32[16]{0:T(128)S(1)}, u32[]{:S(2)}) copy-start(f32[16]{0:T(128)S(1)} %get-tuple-element.10) | copy-start | bytes 196
  304.2 22.4 %all-to-all-start.4 = ((f32[8,1,32]{2,1,0:T(1,128)}), f32[8,1,32]{2,1,0:T(1,128)S(1)}, u32[]{:S(2)}, u32[]{:S(2)}) async-start(f32[8,1,32]{2,1,0:T(1,128)} %broadcast_in_dim.50), calls=%async_computation.5 | async-start | bytes 8192 | tf_op jit(solution)/shard_map/all_to_all | solution.py:179
Sparse Core Ops, SparseCore 0:
  10.1 131.6 all-gather.5
  145.0 36.5 reduce-scatter.1
  201.7 61.8 all-gather.7

commit v6 on v5

--- a/solution.py
+++ b/solution.py
@@ -117,11 +117,12 @@
         .astype(jnp.bfloat16)
         .reshape(tok_count, heads_here * value_width)
     )
-    own_branch = lax.psum_scatter(
-        jnp.dot(gated_out, out_weight, preferred_element_type=jnp.float32),
-        "head",
-        scatter_dimension=0,
-        tiled=True,
+    branch_parts = jnp.dot(gated_out, out_weight, preferred_element_type=jnp.float32)
+    own_branch = jnp.sum(
+        lax.all_to_all(
+            branch_parts.reshape(head_count, slice_rows, -1), "head", 0, 0, tiled=True
+        ),
+        axis=0,
     )
     stream = residual[0].astype(jnp.float32) + own_branch
     hidden = (layer_norm(stream, 1e-05) * norm_gain).astype(jnp.bfloat16)

time: 335 us -> 313 us (0.934)
  waiting for transfers between devices: 208 us -> 182 us
  starting transfers between devices: 43.7 us -> 49.3 us
    reduce_scatter x1 -> x0, waiting for transfers between devices: 36.6 us -> none  [per_device(): lax.psum_scatter(jnp.dot(gated_out, out_weight, preferred_element_type=jn...]
    all_to_all x0 -> x1, waiting for transfers between devices: none -> 15 us  [per_device(): lax.all_to_all(branch_parts.reshape(head_count, slice_rows, -1), 'head',...]
    all_to_all x0 -> x1, starting transfers between devices: none -> 5.72 us  [per_device(): lax.all_to_all(branch_parts.reshape(head_count, slice_rows, -1), 'head',...]
    all_gather x1, waiting for transfers between devices: 61.8 us -> 58 us  [per_device(): gathered = lax.all_gather(lax.all_gather(hidden_ext, 'head'), 'gb')]
where the time goes in v6:
time: 313 us
  waiting for transfers between devices  182 us (58%)
  starting transfers between devices  49.3 us (16%)
  blocking collectives  26.5 us (8%)
  between operations  17.7 us (6%)
  other arithmetic  15.4 us (5%)
  matrix products  12.8 us (4%)
  local copies, waits for them, and re-layouts  8.84 us (3%)
    all_gather x1, waiting for transfers between devices, per_device(): gathered = lax.all_gather(lax.all_gather(hidden_ext, 'head'), 'gb')  58 us
    all_to_all x1, waiting for transfers between devices, per_device(): received = lax.all_to_all(payload, ('ga', 'gb'), 0, 0, tiled=True)  45.4 us
    all_to_all x1, waiting for transfers between devices, per_device(): lax.all_to_all(slices_out, ('ga', 'gb'), 0, 0, tiled=True)  44.2 us
    all_to_all x1, starting transfers between devices, per_device(): received = lax.all_to_all(payload, ('ga', 'gb'), 0, 0, tiled=True)  19.3 us
    all_to_all x1, waiting for transfers between devices, per_device(): lax.all_to_all(branch_parts.reshape(head_count, slice_rows, -1), 'head',...  15 us
    all_gather x1, blocking collectives, per_device(): gathered = lax.all_gather(lax.all_gather(hidden_ext, 'head'), 'gb')  14.4 us
    all_to_all x1, blocking collectives, per_device(): seq_total = jnp.sum(lax.all_to_all(spread, axes, 0, 0, tiled=True), axis=0)  12.2 us
    all_to_all x1, starting transfers between devices, per_device(): seq_total = jnp.sum(lax.all_to_all(spread, axes, 0, 0, tiled=True), axis=0)  11 us
  transfers between devices with their start and end apart: 7, of which 7 were waited for; matrix products, arithmetic and copies ran while one was open for 5% of the time, Pallas kernels for 0%

profile of v6, /device:TPU:1, one launch (start us, length us, event | category | flops | bytes accessed | tf_op | source)
XLA Modules:
  0.0 312.8 jit_solution(8365897815198594580)
XLA Ops:
  7.2 0.7 all-gather.6.cloned.1.call-update
  7.9 0.7 copy.62
  8.7 0.1 reduce.12
  8.8 0.7 sub.101
  9.6 0.1 compare_reduce_fusion
  9.7 0.1 convert_reduce_fusion
  9.8 0.6 fusion.53
  10.4 0.8 copy.63
  11.2 0.2 reduce_window_sum.18
  11.3 0.6 slice.63
  11.9 0.1 reduce.13
  12.0 2.0 select_multiply_fusion
  14.0 1.4 fusion.18
  15.5 1.3 fusion.52
  17.5 0.2 reshape.449
  18.5 1.2 all_to_all.31
  19.7 19.3 %all-to-all-start = ((f32[64,1,2176]{2,1,0:T(1,128)}), f32[64,1,2176]{2,1,0:T(1,128)S(1)}, u32[]{:S(2)}, u32[]{:S(2)}) async-start(f32[64,1,2176]{2,1,0:T(1,128)} %all_to_all.31), calls=%async_computation | async-start | bytes 1114112 | tf_op jit(solution)/shard_map/all_to_all | solution.py:89
  38.9 45.4 %all-to-all-done = f32[64,1,2176]{2,1,0:T(1,128)S(1)} async-done(((f32[64,1,2176]{2,1,0:T(1,128)}), f32[64,1,2176]{2,1,0:T(1,128)S(1)}, u32[]{:S(2)}, u32[]{:S(2)}) %all-to-all-start) | async-done | bytes 557088 | tf_op jit(solution)/shard_map/all_to_all | solution.py:89
  84.3 0.1 slice_reduce_fusion
  84.5 1.2 select_reduce_fusion.1
  85.6 0.6 convolution_bitcast_fusion
  86.2 1.3 copy.64
  87.5 6.8 %all-to-all-start.1 = ((f32[64,1,2048]{2,1,0:T(1,128)}), f32[64,1,2048]{2,1,0:T(1,128)S(1)}, u32[]{:S(2)}, u32[]{:S(2)}) async-start(f32[64,1,2048]{2,1,0:T(1,128)} %copy.64), calls=%async_computation.1 | async-start | bytes 1048576 | tf_op jit(solution)/shard_map/all_to_all | solution.py:97
  94.4 0.4 convolution_bitcast_fusion.2
  94.8 44.2 %all-to-all-done.1 = f32[64,1,2048]{2,1,0:T(1,128)S(1)} async-done(((f32[64,1,2048]{2,1,0:T(1,128)}), f32[64,1,2048]{2,1,0:T(1,128)S(1)}, u32[]{:S(2)}, u32[]{:S(2)}) %all-to-all-start.1) | async-done | bytes 524320 | tf_op jit(solution)/shard_map/all_to_all | solution.py:97
  138.9 1.2 reduce.15
  140.2 0.1 reshape.450
  140.3 1.4 all-gather.6.cloned.1.call-done
  141.8 0.4 fusion.54
  142.2 0.2 multiply_reduce_fusion.1
  142.4 1.1 fusion.17
  143.5 1.5 fusion.2
  145.0 5.7 %all-to-all-start.2 = ((f32[8,16,2048]{2,1,0:T(8,128)}), f32[8,16,2048]{2,1,0:T(8,128)}, u32[]{:S(2)}, u32[]{:S(2)}) async-start(f32[8,16,2048]{2,1,0:T(8,128)} %fusion.2), calls=%async_computation.2 | async-start | bytes 2097152 | tf_op jit(solution)/shard_map/all_to_all | solution.py:122
  150.7 0.1 fusion.45
  150.8 15.0 %all-to-all-done.2 = f32[8,16,2048]{2,1,0:T(8,128)} async-done(((f32[8,16,2048]{2,1,0:T(8,128)}), f32[8,16,2048]{2,1,0:T(8,128)}, u32[]{:S(2)}, u32[]{:S(2)}) %all-to-all-start.2) | async-done | bytes 1048608 | tf_op jit(solution)/shard_map/all_to_all | solution.py:122
  165.8 1.3 reduce_sum.139
  167.1 0.1 fusion.29
  167.3 0.2 multiply_reduce_fusion.2
  167.5 0.1 multiply_convert_fusion
  167.6 14.4 %all-gather.2 = bf16[8,17,2048]{2,1,0:T(8,128)(2,1)S(1)} all-gather(bf16[1,17,2048]{2,1,0:T(8,128)(2,1)S(1)} %maximum_bitcast_fusion), channel_id=2, replica_groups=mesh['head'=8,'ga'=8,'gb'=8] {'head'}, dimensions={0}, use_global_device_ids=true | all-gather | bytes 626688 | tf_op jit(solution)/shard_map/all_gather | solution.py:136
  182.0 1.1 copy.65
  183.2 0.1 add.143
  183.4 58.0 %all-gather.8.cloned.1.call-done = bf16[64,17,2048]{2,0,1:T(8,128)(2,1)} async-done(((bf16[8,17,2048]{2,0,1:T(8,128)(2,1)}), bf16[64,17,2048]{2,0,1:T(8,128)(2,1)}) %all-gather.8.cloned.1.call-update) | async-done | bytes 4456464 | tf_op jit(solution)/shard_map/all_gather | solution.py:136
  241.3 8.5 %fusion.55 = (f32[64,16]{0,1:T(8,128)S(1)}, f32[64,16,768]{2,0,1:T(8,128)}) fusion(bf16[64,17,2048]{2,0,1:T(8,128)(2,1)} %all-gather.8.cloned.1.call-done, bf16[768,2048]{1,0:T(8,128)(2,1)} %all-gather.6.cloned.1.call-done), kind=kOutput, calls=%fused_computation.110 | convolution fusion | flops 3222010880 | bytes 10752000 | tf_op jit(solution)/shard_map/slice | solution.py:149
  249.8 0.1 copy.66
  249.9 0.7 fusion.38
  250.6 0.1 fusion.30
  250.7 2.5 exponential_reduce_fusion
  253.2 0.1 copy.67
  253.3 0.1 copy.69
  253.5 0.7 all_to_all.37
  254.2 6.5 %all-to-all-start.3 = ((f32[64,1,48]{2,1,0:T(1,128)}), f32[64,1,48]{2,1,0:T(1,128)S(1)}, u32[]{:S(2)}, u32[]{:S(2)}) async-start(f32[64,1,48]{2,1,0:T(1,128)} %bitcast.33), calls=%async_computation.3 | async-start | bytes 65536 | tf_op jit(solution)/shard_map/all_to_all | solution.py:162
  260.7 0.2 convert_reduce_fusion.1
  260.9 7.6 %all-to-all-done.3 = f32[64,1,48]{2,1,0:T(1,128)S(1)} async-done(((f32[64,1,48]{2,1,0:T(1,128)}), f32[64,1,48]{2,1,0:T(1,128)S(1)}, u32[]{:S(2)}, u32[]{:S(2)}) %all-to-all-start.3) | async-done | bytes 12320 | tf_op jit(solution)/shard_map/all_to_all | solution.py:162
  268.6 0.1 slice_reduce_fusion.1
  268.7 0.2 fusion.41
  268.9 0.1 select_reduce_fusion.2
  269.0 12.2 %all_to_all.47 = f32[64,1,32]{2,1,0:T(1,128)S(1)} all-to-all(f32[64,1,32]{2,1,0:T(1,128)S(1)} %broadcast_in_dim.49), channel_id=1, replica_groups=mesh['head'=8,'ga'=8,'gb'=8] {'head','gb'}, dimensions={0} | all-to-all | bytes 16384 | tf_op jit(solution)/shard_map/all_to_all | solution.py:180
  281.2 0.1 reduce_sum.147
  281.3 0.6 broadcast_in_dim.50
  281.9 11.0 %all-to-all-start.5 = ((f32[8,1,32]{2,1,0:T(1,128)}), f32[8,1,32]{2,1,0:T(1,128)S(1)}, u32[]{:S(2)}, u32[]{:S(2)}) async-start(f32[8,1,32]{2,1,0:T(1,128)} %broadcast_in_dim.50), calls=%async_computation.5 | async-start | bytes 8192 | tf_op jit(solution)/shard_map/all_to_all | solution.py:180
  292.9 0.7 multiply_reduce_fusion
  294.3 9.9 %all-to-all-done.5 = f32[8,1,32]{2,1,0:T(1,128)S(1)} async-done(((f32[8,1,32]{2,1,0:T(1,128)}), f32[8,1,32]{2,1,0:T(1,128)S(1)}, u32[]{:S(2)}, u32[]{:S(2)}) %all-to-all-start.5) | async-done | bytes 1056 | tf_op jit(solution)/shard_map/all_to_all | solution.py:180
  304.3 0.5 convert_divide_fusion
  (49 shorter events, 0.8 us)
Async XLA Ops:
  7.2 136.3 %copy-start = (bf16[512,2048]{1,0:T(8,128)(2,1)S(1)}, bf16[512,2048]{1,0:T(8,128)(2,1)}, u32[]{:S(2)}) copy-start(bf16[512,2048]{1,0:T(8,128)(2,1)} %param.18) | copy-start | bytes 6291460
  7.2 134.6 %all-gather.6.cloned.1.call-start = ((), (), s32[]{:S(2)}) async-start(), calls=%async_computation.6 | async-start | bytes 3538944 | tf_op jit(solution)/shard_map/all_gather | solution.py:101
  18.4 75.9 %copy-start.2 = (bf16[128,512]{1,0:T(8,128)(2,1)S(1)}, bf16[128,512]{1,0:T(8,128)(2,1)}, u32[]{:S(2)}) copy-start(bf16[128,512]{1,0:T(8,128)(2,1)} %param.15) | copy-start | bytes 393220
  18.5 75.9 %copy-start.3 = (bf16[128,256]{1,0:T(8,128)(2,1)S(1)}, bf16[128,256]{1,0:T(8,128)(2,1)}, u32[]{:S(2)}) copy-start(bf16[128,256]{1,0:T(8,128)(2,1)} %param.14) | copy-start | bytes 196612
  18.5 75.9 %copy-start.4 = (bf16[128,256]{1,0:T(8,128)(2,1)S(1)}, bf16[128,256]{1,0:T(8,128)(2,1)}, u32[]{:S(2)}) copy-start(bf16[128,256]{1,0:T(8,128)(2,1)} %param.13) | copy-start | bytes 196612
  19.7 64.7 %all-to-all-start = ((f32[64,1,2176]{2,1,0:T(1,128)}), f32[64,1,2176]{2,1,0:T(1,128)S(1)}, u32[]{:S(2)}, u32[]{:S(2)}) async-start(f32[64,1,2176]{2,1,0:T(1,128)} %all_to_all.31), calls=%async_computation | async-start | bytes 1114112 | tf_op jit(solution)/shard_map/all_to_all | solution.py:89
  87.5 51.4 %all-to-all-start.1 = ((f32[64,1,2048]{2,1,0:T(1,128)}), f32[64,1,2048]{2,1,0:T(1,128)S(1)}, u32[]{:S(2)}, u32[]{:S(2)}) async-start(f32[64,1,2048]{2,1,0:T(1,128)} %copy.64), calls=%async_computation.1 | async-start | bytes 1048576 | tf_op jit(solution)/shard_map/all_to_all | solution.py:97
  142.2 8.5 %copy-start.10 = (s32[1,16]{1,0:T(1,128)S(1)}, s32[1,16]{1,0:T(1,128)}, u32[]{:S(2)}) copy-start(s32[1,16]{1,0:T(1,128)} %param.22) | copy-start | bytes 196
  143.5 23.6 %copy-start.1 = (bf16[1,16,2048]{2,1,0:T(8,128)(2,1)S(1)}, bf16[1,16,2048]{2,1,0:T(8,128)(2,1)}, u32[]{:S(2)}) copy-start(bf16[1,16,2048]{2,1,0:T(8,128)(2,1)} %param.19) | copy-start | bytes 196612
  143.5 24.0 %copy-start.5 = (f32[2048]{0:T(1024)S(1)}, f32[2048]{0:T(1024)}, u32[]{:S(2)}) copy-start(f32[2048]{0:T(1024)} %param.20) | copy-start | bytes 24580
  145.0 20.8 %all-to-all-start.2 = ((f32[8,16,2048]{2,1,0:T(8,128)}), f32[8,16,2048]{2,1,0:T(8,128)}, u32[]{:S(2)}, u32[]{:S(2)}) async-start(f32[8,16,2048]{2,1,0:T(8,128)} %fusion.2), calls=%async_computation.2 | async-start | bytes 2097152 | tf_op jit(solution)/shard_map/all_to_all | solution.py:122
  150.7 90.6 %all-gather.8.cloned.1.call-start = ((), (), s32[]{:S(2)}) async-start(), calls=%async_computation.7 | async-start | bytes 5013504 | tf_op jit(solution)/shard_map/all_gather | solution.py:136
  249.8 19.1 %copy-start.8 = (f32[1,16]{1,0:T(1,128)S(1)}, f32[1,16]{1,0:T(1,128)}, u32[]{:S(2)}) copy-start(f32[1,16]{1,0:T(1,128)} %param.23) | copy-start | bytes 196
  249.8 19.1 %copy-start.9 = (s32[1,16]{1,0:T(1,128)S(1)}, s32[1,16]{1,0:T(1,128)}, u32[]{:S(2)}) copy-start(s32[1,16]{1,0:T(1,128)} %param.24) | copy-start | bytes 196
  249.8 54.5 %copy-start.7 = (s32[32]{0:T(128)S(1)}, s32[32]{0:T(128)}, u32[]{:S(2)}) copy-start(s32[32]{0:T(128)} %param.25) | copy-start | bytes 388
  254.2 14.3 %all-to-all-start.3 = ((f32[64,1,48]{2,1,0:T(1,128)}), f32[64,1,48]{2,1,0:T(1,128)S(1)}, u32[]{:S(2)}, u32[]{:S(2)}) async-start(f32[64,1,48]{2,1,0:T(1,128)} %bitcast.33), calls=%async_computation.3 | async-start | bytes 65536 | tf_op jit(solution)/shard_map/all_to_all | solution.py:162
  268.7 36.1 %copy-start.6 = (f32[16]{0:T(128)}, f32[16]{0:T(128)S(1)}, u32[]{:S(2)}) copy-start(f32[16]{0:T(128)S(1)} %get-tuple-element.10) | copy-start | bytes 196
  281.9 22.4 %all-to-all-start.5 = ((f32[8,1,32]{2,1,0:T(1,128)}), f32[8,1,32]{2,1,0:T(1,128)S(1)}, u32[]{:S(2)}, u32[]{:S(2)}) async-start(f32[8,1,32]{2,1,0:T(1,128)} %broadcast_in_dim.50), calls=%async_computation.5 | async-start | bytes 8192 | tf_op jit(solution)/shard_map/all_to_all | solution.py:180
Sparse Core Ops, SparseCore 0:
  10.1 131.6 all-gather.5
  183.3 58.0 all-gather.7

commit v7 on v6

--- a/solution.py
+++ b/solution.py
@@ -174,7 +174,7 @@
     )
     partial_sums = jnp.sum(member * token_ratio[:, None], axis=0)
     seq_total = partial_sums
-    for axes in (("head", "gb"), "ga"):
+    for axes in (("head", "ga", "gb"),):
         width = lax.axis_size(axes)
         spread = jnp.broadcast_to(seq_total[None, :], (width, seq_count))
         seq_total = jnp.sum(lax.all_to_all(spread, axes, 0, 0, tiled=True), axis=0)

time: 313 us -> 320 us (1.022)
  waiting for transfers between devices: 182 us -> 195 us
  blocking collectives: 26.5 us -> 14.4 us
  starting transfers between devices: 49.3 us -> 54.4 us
    all_to_all x1, waiting for transfers between devices: 9.9 us -> 22.5 us  [per_device(): seq_total = jnp.sum(lax.all_to_all(spread, axes, 0, 0, tiled=True), axis=0)]
    all_to_all x1 -> x0, blocking collectives: 12.2 us -> none  [per_device(): seq_total = jnp.sum(lax.all_to_all(spread, axes, 0, 0, tiled=True), axis=0)]
    all_to_all x1, starting transfers between devices: 11 us -> 16.1 us  [per_device(): seq_total = jnp.sum(lax.all_to_all(spread, axes, 0, 0, tiled=True), axis=0)]
where the time goes in v7:
time: 320 us; the launch traced here: 319 us
  waiting for transfers between devices  195 us (61%)
  starting transfers between devices  54.4 us (17%)
  between operations  17.7 us (6%)
  other arithmetic  15.9 us (5%)
  blocking collectives  14.4 us (4%)
  matrix products  12.8 us (4%)
  local copies, waits for them, and re-layouts  9.05 us (3%)
    all_gather x1, waiting for transfers between devices, per_device(): gathered = lax.all_gather(lax.all_gather(hidden_ext, 'head'), 'gb')  58 us
    all_to_all x1, waiting for transfers between devices, per_device(): received = lax.all_to_all(payload, ('ga', 'gb'), 0, 0, tiled=True)  45.4 us
    all_to_all x1, waiting for transfers between devices, per_device(): lax.all_to_all(slices_out, ('ga', 'gb'), 0, 0, tiled=True)  44.2 us
    all_to_all x1, waiting for transfers between devices, per_device(): seq_total = jnp.sum(lax.all_to_all(spread, axes, 0, 0, tiled=True), axis=0)  22.5 us
    all_to_all x1, starting transfers between devices, per_device(): received = lax.all_to_all(payload, ('ga', 'gb'), 0, 0, tiled=True)  19.3 us
    all_to_all x1, starting transfers between devices, per_device(): seq_total = jnp.sum(lax.all_to_all(spread, axes, 0, 0, tiled=True), axis=0)  16.1 us
    all_to_all x1, waiting for transfers between devices, per_device(): lax.all_to_all(branch_parts.reshape(head_count, slice_rows, -1), 'head',...  15 us
    all_gather x1, blocking collectives, per_device(): gathered = lax.all_gather(lax.all_gather(hidden_ext, 'head'), 'gb')  14.4 us
  transfers between devices with their start and end apart: 7, of which 7 were waited for; matrix products, arithmetic and copies ran while one was open for 5% of the time, Pallas kernels for 0%

profile of v7, /device:TPU:1, one launch (start us, length us, event | category | flops | bytes accessed | tf_op | source)
XLA Modules:
  0.0 318.9 jit_solution(9817885055343412136)
XLA Ops:
  7.2 0.7 all-gather.6.cloned.1.call-update
  7.9 0.7 copy.62
  8.7 0.1 reduce.11
  8.8 0.7 sub.101
  9.5 0.1 slice.49
  9.6 0.1 compare_reduce_fusion
  9.7 0.1 convert_reduce_fusion
  9.8 0.6 fusion.53
  10.4 0.8 copy.63
  11.2 0.2 reduce_window_sum.18
  11.3 0.6 slice.63
  11.9 0.1 reduce.12
  12.0 2.0 select_multiply_fusion
  14.0 1.4 fusion.18
  15.5 1.3 fusion.52
  17.5 0.2 reshape.443
  18.5 1.2 all_to_all.27
  19.7 19.3 %all-to-all-start = ((f32[64,1,2176]{2,1,0:T(1,128)}), f32[64,1,2176]{2,1,0:T(1,128)S(1)}, u32[]{:S(2)}, u32[]{:S(2)}) async-start(f32[64,1,2176]{2,1,0:T(1,128)} %all_to_all.27), calls=%async_computation | async-start | bytes 1114112 | tf_op jit(solution)/shard_map/all_to_all | solution.py:89
  38.9 45.4 %all-to-all-done = f32[64,1,2176]{2,1,0:T(1,128)S(1)} async-done(((f32[64,1,2176]{2,1,0:T(1,128)}), f32[64,1,2176]{2,1,0:T(1,128)S(1)}, u32[]{:S(2)}, u32[]{:S(2)}) %all-to-all-start) | async-done | bytes 557088 | tf_op jit(solution)/shard_map/all_to_all | solution.py:89
  84.3 0.1 slice_reduce_fusion
  84.5 1.2 select_reduce_fusion.1
  85.6 0.6 convolution_bitcast_fusion
  86.2 1.3 copy.64
  87.5 6.8 %all-to-all-start.1 = ((f32[64,1,2048]{2,1,0:T(1,128)}), f32[64,1,2048]{2,1,0:T(1,128)S(1)}, u32[]{:S(2)}, u32[]{:S(2)}) async-start(f32[64,1,2048]{2,1,0:T(1,128)} %copy.64), calls=%async_computation.1 | async-start | bytes 1048576 | tf_op jit(solution)/shard_map/all_to_all | solution.py:97
  94.4 0.4 convolution_bitcast_fusion.2
  94.8 44.2 %all-to-all-done.1 = f32[64,1,2048]{2,1,0:T(1,128)S(1)} async-done(((f32[64,1,2048]{2,1,0:T(1,128)}), f32[64,1,2048]{2,1,0:T(1,128)S(1)}, u32[]{:S(2)}, u32[]{:S(2)}) %all-to-all-start.1) | async-done | bytes 524320 | tf_op jit(solution)/shard_map/all_to_all | solution.py:97
  138.9 1.2 reduce.14
  140.2 0.1 reshape.444
  140.3 1.4 all-gather.6.cloned.1.call-done
  141.8 0.4 fusion.54
  142.2 0.2 multiply_reduce_fusion.1
  142.4 1.1 fusion.17
  143.5 1.5 fusion.2
  145.0 5.7 %all-to-all-start.2 = ((f32[8,16,2048]{2,1,0:T(8,128)}), f32[8,16,2048]{2,1,0:T(8,128)}, u32[]{:S(2)}, u32[]{:S(2)}) async-start(f32[8,16,2048]{2,1,0:T(8,128)} %fusion.2), calls=%async_computation.2 | async-start | bytes 2097152 | tf_op jit(solution)/shard_map/all_to_all | solution.py:122
  150.7 0.1 fusion.45
  150.8 15.0 %all-to-all-done.2 = f32[8,16,2048]{2,1,0:T(8,128)} async-done(((f32[8,16,2048]{2,1,0:T(8,128)}), f32[8,16,2048]{2,1,0:T(8,128)}, u32[]{:S(2)}, u32[]{:S(2)}) %all-to-all-start.2) | async-done | bytes 1048608 | tf_op jit(solution)/shard_map/all_to_all | solution.py:122
  165.8 1.3 reduce_sum.130
  167.1 0.1 fusion.29
  167.3 0.2 multiply_reduce_fusion.2
  167.5 0.1 multiply_convert_fusion
  167.6 14.4 %all-gather.2 = bf16[8,17,2048]{2,1,0:T(8,128)(2,1)S(1)} all-gather(bf16[1,17,2048]{2,1,0:T(8,128)(2,1)S(1)} %maximum_bitcast_fusion), channel_id=2, replica_groups=mesh['head'=8,'ga'=8,'gb'=8] {'head'}, dimensions={0}, use_global_device_ids=true | all-gather | bytes 626688 | tf_op jit(solution)/shard_map/all_gather | solution.py:136
  182.0 1.1 copy.65
  183.2 0.1 add.143
  183.4 58.0 %all-gather.8.cloned.1.call-done = bf16[64,17,2048]{2,0,1:T(8,128)(2,1)} async-done(((bf16[8,17,2048]{2,0,1:T(8,128)(2,1)}), bf16[64,17,2048]{2,0,1:T(8,128)(2,1)}) %all-gather.8.cloned.1.call-update) | async-done | bytes 4456464 | tf_op jit(solution)/shard_map/all_gather | solution.py:136
  241.3 8.5 %fusion.55 = (f32[64,16]{0,1:T(8,128)S(1)}, f32[64,16,768]{2,0,1:T(8,128)}) fusion(bf16[64,17,2048]{2,0,1:T(8,128)(2,1)} %all-gather.8.cloned.1.call-done, bf16[768,2048]{1,0:T(8,128)(2,1)} %all-gather.6.cloned.1.call-done), kind=kOutput, calls=%fused_computation.110 | convolution fusion | flops 3222010880 | bytes 10752000 | tf_op jit(solution)/shard_map/slice | solution.py:149
  249.8 0.1 copy.66
  249.9 0.7 fusion.38
  250.6 0.1 fusion.30
  250.7 2.5 exponential_reduce_fusion
  253.2 0.1 copy.67
  253.3 0.1 copy.69
  253.5 0.7 all_to_all.33
  254.2 6.5 %all-to-all-start.3 = ((f32[64,1,48]{2,1,0:T(1,128)}), f32[64,1,48]{2,1,0:T(1,128)S(1)}, u32[]{:S(2)}, u32[]{:S(2)}) async-start(f32[64,1,48]{2,1,0:T(1,128)} %bitcast.33), calls=%async_computation.3 | async-start | bytes 65536 | tf_op jit(solution)/shard_map/all_to_all | solution.py:162
  260.7 0.2 convert_reduce_fusion.1
  260.9 7.6 %all-to-all-done.3 = f32[64,1,48]{2,1,0:T(1,128)S(1)} async-done(((f32[64,1,48]{2,1,0:T(1,128)}), f32[64,1,48]{2,1,0:T(1,128)S(1)}, u32[]{:S(2)}, u32[]{:S(2)}) %all-to-all-start.3) | async-done | bytes 12320 | tf_op jit(solution)/shard_map/all_to_all | solution.py:162
  268.6 0.1 slice_reduce_fusion.1
  268.7 0.2 fusion.41
  268.9 0.1 select_reduce_fusion.2
  269.0 0.8 broadcast_in_dim.47
  269.8 16.1 %all-to-all-start.4 = ((f32[512,1,32]{2,1,0:T(1,128)}), f32[512,1,32]{2,1,0:T(1,128)S(1)}, u32[]{:S(2)}, u32[]{:S(2)}) async-start(f32[512,1,32]{2,1,0:T(1,128)} %broadcast_in_dim.47), calls=%async_computation.4 | async-start | bytes 524288 | tf_op jit(solution)/shard_map/all_to_all | solution.py:180
  285.9 0.7 multiply_reduce_fusion
  287.4 22.5 %all-to-all-done.4 = f32[512,1,32]{2,1,0:T(1,128)S(1)} async-done(((f32[512,1,32]{2,1,0:T(1,128)}), f32[512,1,32]{2,1,0:T(1,128)S(1)}, u32[]{:S(2)}, u32[]{:S(2)}) %all-to-all-start.4) | async-done | bytes 65568 | tf_op jit(solution)/shard_map/all_to_all | solution.py:180
  309.9 0.6 reduce_sum.138
  310.4 0.5 convert_divide_fusion
  (46 shorter events, 0.7 us)
Async XLA Ops:
  7.2 136.3 %copy-start = (bf16[512,2048]{1,0:T(8,128)(2,1)S(1)}, bf16[512,2048]{1,0:T(8,128)(2,1)}, u32[]{:S(2)}) copy-start(bf16[512,2048]{1,0:T(8,128)(2,1)} %param.18) | copy-start | bytes 6291460
  7.2 134.6 %all-gather.6.cloned.1.call-start = ((), (), s32[]{:S(2)}) async-start(), calls=%async_computation.5 | async-start | bytes 3538944 | tf_op jit(solution)/shard_map/all_gather | solution.py:101
  18.4 75.9 %copy-start.2 = (bf16[128,512]{1,0:T(8,128)(2,1)S(1)}, bf16[128,512]{1,0:T(8,128)(2,1)}, u32[]{:S(2)}) copy-start(bf16[128,512]{1,0:T(8,128)(2,1)} %param.15) | copy-start | bytes 393220
  18.5 75.9 %copy-start.3 = (bf16[128,256]{1,0:T(8,128)(2,1)S(1)}, bf16[128,256]{1,0:T(8,128)(2,1)}, u32[]{:S(2)}) copy-start(bf16[128,256]{1,0:T(8,128)(2,1)} %param.14) | copy-start | bytes 196612
  18.5 75.9 %copy-start.4 = (bf16[128,256]{1,0:T(8,128)(2,1)S(1)}, bf16[128,256]{1,0:T(8,128)(2,1)}, u32[]{:S(2)}) copy-start(bf16[128,256]{1,0:T(8,128)(2,1)} %param.13) | copy-start | bytes 196612
  19.7 64.7 %all-to-all-start = ((f32[64,1,2176]{2,1,0:T(1,128)}), f32[64,1,2176]{2,1,0:T(1,128)S(1)}, u32[]{:S(2)}, u32[]{:S(2)}) async-start(f32[64,1,2176]{2,1,0:T(1,128)} %all_to_all.27), calls=%async_computation | async-start | bytes 1114112 | tf_op jit(solution)/shard_map/all_to_all | solution.py:89
  87.5 51.4 %all-to-all-start.1 = ((f32[64,1,2048]{2,1,0:T(1,128)}), f32[64,1,2048]{2,1,0:T(1,128)S(1)}, u32[]{:S(2)}, u32[]{:S(2)}) async-start(f32[64,1,2048]{2,1,0:T(1,128)} %copy.64), calls=%async_computation.1 | async-start | bytes 1048576 | tf_op jit(solution)/shard_map/all_to_all | solution.py:97
  142.2 8.5 %copy-start.10 = (s32[1,16]{1,0:T(1,128)S(1)}, s32[1,16]{1,0:T(1,128)}, u32[]{:S(2)}) copy-start(s32[1,16]{1,0:T(1,128)} %param.22) | copy-start | bytes 196
  143.5 23.6 %copy-start.1 = (bf16[1,16,2048]{2,1,0:T(8,128)(2,1)S(1)}, bf16[1,16,2048]{2,1,0:T(8,128)(2,1)}, u32[]{:S(2)}) copy-start(bf16[1,16,2048]{2,1,0:T(8,128)(2,1)} %param.19) | copy-start | bytes 196612
  143.5 24.0 %copy-start.5 = (f32[2048]{0:T(1024)S(1)}, f32[2048]{0:T(1024)}, u32[]{:S(2)}) copy-start(f32[2048]{0:T(1024)} %param.20) | copy-start | bytes 24580
  145.0 20.8 %all-to-all-start.2 = ((f32[8,16,2048]{2,1,0:T(8,128)}), f32[8,16,2048]{2,1,0:T(8,128)}, u32[]{:S(2)}, u32[]{:S(2)}) async-start(f32[8,16,2048]{2,1,0:T(8,128)} %fusion.2), calls=%async_computation.2 | async-start | bytes 2097152 | tf_op jit(solution)/shard_map/all_to_all | solution.py:122
  150.7 90.6 %all-gather.8.cloned.1.call-start = ((), (), s32[]{:S(2)}) async-start(), calls=%async_computation.6 | async-start | bytes 5013504 | tf_op jit(solution)/shard_map/all_gather | solution.py:136
  249.8 19.1 %copy-start.8 = (f32[1,16]{1,0:T(1,128)S(1)}, f32[1,16]{1,0:T(1,128)}, u32[]{:S(2)}) copy-start(f32[1,16]{1,0:T(1,128)} %param.23) | copy-start | bytes 196
  249.8 19.1 %copy-start.9 = (s32[1,16]{1,0:T(1,128)S(1)}, s32[1,16]{1,0:T(1,128)}, u32[]{:S(2)}) copy-start(s32[1,16]{1,0:T(1,128)} %param.24) | copy-start | bytes 196
  249.8 60.6 %copy-start.7 = (s32[32]{0:T(128)S(1)}, s32[32]{0:T(128)}, u32[]{:S(2)}) copy-start(s32[32]{0:T(128)} %param.25) | copy-start | bytes 388
  254.2 14.3 %all-to-all-start.3 = ((f32[64,1,48]{2,1,0:T(1,128)}), f32[64,1,48]{2,1,0:T(1,128)S(1)}, u32[]{:S(2)}, u32[]{:S(2)}) async-start(f32[64,1,48]{2,1,0:T(1,128)} %bitcast.33), calls=%async_computation.3 | async-start | bytes 65536 | tf_op jit(solution)/shard_map/all_to_all | solution.py:162
  268.7 42.2 %copy-start.6 = (f32[16]{0:T(128)}, f32[16]{0:T(128)S(1)}, u32[]{:S(2)}) copy-start(f32[16]{0:T(128)S(1)} %get-tuple-element.10) | copy-start | bytes 196
  269.8 40.0 %all-to-all-start.4 = ((f32[512,1,32]{2,1,0:T(1,128)}), f32[512,1,32]{2,1,0:T(1,128)S(1)}, u32[]{:S(2)}, u32[]{:S(2)}) async-start(f32[512,1,32]{2,1,0:T(1,128)} %broadcast_in_dim.47), calls=%async_computation.4 | async-start | bytes 524288 | tf_op jit(solution)/shard_map/all_to_all | solution.py:180
Sparse Core Ops, SparseCore 0:
  10.1 131.6 all-gather.5
  183.3 58.0 all-gather.7

commit v8 on v6

--- a/solution.py
+++ b/solution.py
@@ -75,26 +75,45 @@
     block_decay = jnp.where(jnp.all(continuation_flags), jnp.exp(cumulative_decay[-1]), 0.0)
 
     assert heads_here == 1
-    chunk = key_width * value_width // group_count
-    extras = block_decay
-    extra_width = 128 * pl_cdiv(extras.shape[0], 128)
-    extras = jnp.pad(extras, (0, extra_width - extras.shape[0]))
+    sub = lax.axis_size("gb")
+    part_count = lax.axis_size("ga")
+    state_size = key_width * value_width
+    pad = jnp.zeros((127,), jnp.float32)
+    chunk = state_size // sub
+    extras = jnp.concatenate([block_decay, pad])
     payload = jnp.concatenate(
         [
-            block_total_sum.reshape(group_count, chunk),
-            jnp.broadcast_to(extras[None, :], (group_count, extra_width)),
+            block_total_sum.reshape(sub, chunk),
+            jnp.broadcast_to(extras[None, :], (sub, 128)),
         ],
         axis=1,
     )
-    received = lax.all_to_all(payload, ("ga", "gb"), 0, 0, tiled=True)
+    received = lax.all_to_all(payload, "gb", 0, 0, tiled=True)
     slices_in = received[:, :chunk]
-    decay_all = received[:, chunk]
-    blk = jnp.arange(group_count, dtype=jnp.int32)
-    between = (blk[None, None, :] > blk[None, :, None]) & (blk[None, None, :] < blk[:, None, None])
-    weights = jnp.prod(jnp.where(between, decay_all[None, None, :], 1.0), axis=2)
-    weights = jnp.where(blk[None, :] < blk[:, None], weights, 0.0)
-    slices_out = jnp.dot(weights, slices_in, precision=highest_precision)
-    carried_state = lax.all_to_all(slices_out, ("ga", "gb"), 0, 0, tiled=True).reshape(
+    decay_in = received[:, chunk]
+    local_in = jnp.dot(decay_weights(decay_in), slices_in, precision=highest_precision)
+    tail_weights = decay_weights(jnp.concatenate([decay_in, jnp.ones((1,), jnp.float32)]))[
+        sub, :sub
+    ]
+    octet_total = jnp.dot(tail_weights, slices_in, precision=highest_precision)
+    octet_decay = jnp.prod(decay_in)
+    lead_decay = jnp.cumprod(jnp.concatenate([jnp.ones((1,), jnp.float32), decay_in[:-1]]))
+    piece = chunk // part_count
+    extras = jnp.concatenate([octet_decay[None], pad])
+    payload = jnp.concatenate(
+        [
+            octet_total.reshape(part_count, piece),
+            jnp.broadcast_to(extras[None, :], (part_count, 128)),
+        ],
+        axis=1,
+    )
+    received = lax.all_to_all(payload, "ga", 0, 0, tiled=True)
+    octet_in = jnp.dot(
+        decay_weights(received[:, piece]), received[:, :piece], precision=highest_precision
+    )
+    octet_in = lax.all_to_all(octet_in, "ga", 0, 0, tiled=True).reshape(chunk)
+    slices_out = local_in + lead_decay[:, None] * octet_in[None, :]
+    carried_state = lax.all_to_all(slices_out, "gb", 0, 0, tiled=True).reshape(
         heads_here, key_width, value_width
     )
 
@@ -127,7 +146,6 @@
     stream = residual[0].astype(jnp.float32) + own_branch
     hidden = (layer_norm(stream, 1e-05) * norm_gain).astype(jnp.bfloat16)
 
-    sub = lax.axis_size("gb")
     ga_index = lax.axis_index("ga")
     gb_index = lax.axis_index("gb")
     code = jnp.concatenate([targets[0] // 256, targets[0] % 256]).astype(jnp.bfloat16)
@@ -136,7 +154,6 @@
     gathered = lax.all_gather(lax.all_gather(hidden_ext, "head"), "gb")
     code_all = gathered[:, :, slice_rows, : 2 * slice_rows].astype(jnp.int32)
     all_targets = (code_all[..., :slice_rows] * 256 + code_all[..., slice_rows:]).reshape(-1)
-    part_count = lax.axis_size("ga")
     entry_ids = (
         (
             head_index * group_count
@@ -182,8 +199,12 @@
     return (seq_ratio, state_norms, own_max[None, :])
 
 
-def pl_cdiv(a, b):
-    return (a + b - 1) // b
+def decay_weights(decay):
+    count = decay.shape[0]
+    at = jnp.arange(count, dtype=jnp.int32)
+    between = (at[None, None, :] > at[None, :, None]) & (at[None, None, :] < at[:, None, None])
+    weights = jnp.prod(jnp.where(between, decay[None, None, :], 1.0), axis=2)
+    return jnp.where(at[None, :] < at[:, None], weights, 0.0)
 
 
 def solution(mesh):

time: 313 us -> 296 us (0.946)
  waiting for transfers between devices: 182 us -> 157 us
  starting transfers between devices: 49.3 us -> 53.8 us
    all_to_all x2 -> x4, waiting for transfers between devices: 89.5 us -> 53.4 us  [the longest x1 18.3 us: per_device(): lax.all_to_all(slices_out, 'gb', 0, 0, tiled=True)]
    all_gather x1, waiting for transfers between devices: 1.44 us -> 12.8 us  [per_device(): vocab_rows = lax.all_gather(vocab_weight, 'ga', axis=0, tiled=True)]
    all_to_all x2 -> x4, starting transfers between devices: 26.1 us -> 31 us  [the longest x1 14.5 us: per_device(): received = lax.all_to_all(payload, 'ga', 0, 0, tiled=True)]
  transfers between devices with their start and end apart: 7 -> 9, of which waited for: 7 -> 9; matrix products, arithmetic and copies ran while one was open for 5% -> 3% of each run, Pallas kernels for 0% -> 0%
where the time goes in v8:
time: 296 us; the launch traced here: 295 us
  waiting for transfers between devices  157 us (53%)
  starting transfers between devices  53.8 us (18%)
  blocking collectives  26.5 us (9%)
  between operations  17.7 us (6%)
  other arithmetic  16.5 us (6%)
  matrix products  13.5 us (5%)
  local copies, waits for them, and re-layouts  10.3 us (3%)
    all_gather x1, waiting for transfers between devices, per_device(): gathered = lax.all_gather(lax.all_gather(hidden_ext, 'head'), 'gb')  57.6 us
    all_to_all x1, waiting for transfers between devices, per_device(): lax.all_to_all(slices_out, 'gb', 0, 0, tiled=True)  18.3 us
    all_to_all x1, waiting for transfers between devices, per_device(): octet_in = lax.all_to_all(octet_in, 'ga', 0, 0, tiled=True).reshape(chunk)  15.6 us
    all_to_all x1, waiting for transfers between devices, per_device(): lax.all_to_all(branch_parts.reshape(head_count, slice_rows, -1), 'head',...  15 us
    all_to_all x1, starting transfers between devices, per_device(): received = lax.all_to_all(payload, 'ga', 0, 0, tiled=True)  14.5 us
    all_gather x1, blocking collectives, per_device(): gathered = lax.all_gather(lax.all_gather(hidden_ext, 'head'), 'gb')  14.4 us
    all_to_all x1, waiting for transfers between devices, per_device(): received = lax.all_to_all(payload, 'ga', 0, 0, tiled=True)  13.2 us
    all_gather x1, waiting for transfers between devices, per_device(): vocab_rows = lax.all_gather(vocab_weight, 'ga', axis=0, tiled=True)  12.8 us
  transfers between devices with their start and end apart: 9, of which 9 were waited for; matrix products, arithmetic and copies ran while one was open for 3% of the time, Pallas kernels for 0%

profile of v8, /device:TPU:1, one launch (start us, length us, event | category | flops | bytes accessed | tf_op | source)
XLA Modules:
  0.0 295.4 jit_solution(14432298140862876262)
XLA Ops:
  7.2 0.9 copy.65
  8.1 0.1 reduce.13
  8.3 0.7 sub.101
  9.2 0.6 fusion.66
  9.8 0.8 copy.66
  10.6 0.2 reduce_window_sum.18
  10.7 0.6 slice.84
  12.1 0.1 reduce.14
  12.2 1.3 fusion.64
  14.0 2.0 select_multiply_fusion
  16.0 1.4 fusion.18
  17.6 1.2 all_to_all.45
  18.8 6.4 %all-to-all-start = ((f32[8,1,16512]{2,1,0:T(1,128)}), f32[8,1,16512]{2,1,0:T(1,128)S(1)}, u32[]{:S(2)}, u32[]{:S(2)}) async-start(f32[8,1,16512]{2,1,0:T(1,128)} %all_to_all.45), calls=%async_computation | async-start | bytes 1056768 | tf_op jit(solution)/shard_map/all_to_all | solution.py:91
  25.2 0.7 all-gather.6.cloned.1.call-update
  25.9 6.4 %all-to-all-done = f32[8,1,16512]{2,1,0:T(1,128)S(1)} async-done(((f32[8,1,16512]{2,1,0:T(1,128)}), f32[8,1,16512]{2,1,0:T(1,128)S(1)}, u32[]{:S(2)}, u32[]{:S(2)}) %all-to-all-start) | async-done | bytes 528416 | tf_op jit(solution)/shard_map/all_to_all | solution.py:91
  32.4 0.7 slice_reduce_fusion.4
  33.2 0.2 select_reduce_fusion.1
  33.4 0.6 fusion.53
  34.0 0.7 pad_select_fusion.1
  34.7 0.7 all_to_all.48
  35.4 14.5 %all-to-all-start.1 = ((f32[8,1,2176]{2,1,0:T(1,128)}), f32[8,1,2176]{2,1,0:T(1,128)S(1)}, u32[]{:S(2)}, u32[]{:S(2)}) async-start(f32[8,1,2176]{2,1,0:T(1,128)} %all_to_all.48), calls=%async_computation.1 | async-start | bytes 139264 | tf_op jit(solution)/shard_map/all_to_all | solution.py:110
  49.9 13.2 %all-to-all-done.1 = f32[8,1,2176]{2,1,0:T(1,128)S(1)} async-done(((f32[8,1,2176]{2,1,0:T(1,128)}), f32[8,1,2176]{2,1,0:T(1,128)S(1)}, u32[]{:S(2)}, u32[]{:S(2)}) %all-to-all-start.1) | async-done | bytes 69664 | tf_op jit(solution)/shard_map/all_to_all | solution.py:110
  63.1 0.1 slice_reduce_fusion.2
  63.2 0.3 fusion.31
  63.6 0.2 convolution_bitcast_fusion
  63.8 0.7 copy.67
  64.4 3.3 %all-to-all-start.2 = ((f32[8,1,2048]{2,1,0:T(1,128)}), f32[8,1,2048]{2,1,0:T(1,128)S(1)}, u32[]{:S(2)}, u32[]{:S(2)}) async-start(f32[8,1,2048]{2,1,0:T(1,128)} %copy.67), calls=%async_computation.2 | async-start | bytes 131072 | tf_op jit(solution)/shard_map/all_to_all | solution.py:114
  67.8 0.1 slice_reduce_fusion.3
  68.0 0.2 reduce-window.18
  68.2 15.6 %all-to-all-done.2 = f32[8,1,2048]{2,1,0:T(1,128)S(1)} async-done(((f32[8,1,2048]{2,1,0:T(1,128)}), f32[8,1,2048]{2,1,0:T(1,128)S(1)}, u32[]{:S(2)}, u32[]{:S(2)}) %all-to-all-start.2) | async-done | bytes 65568 | tf_op jit(solution)/shard_map/all_to_all | solution.py:114
  83.7 0.6 fusion
  84.3 1.3 copy.68
  85.6 6.8 %all-to-all-start.3 = ((f32[8,1,16384]{2,1,0:T(1,128)}), f32[8,1,16384]{2,1,0:T(1,128)S(1)}, u32[]{:S(2)}, u32[]{:S(2)}) async-start(f32[8,1,16384]{2,1,0:T(1,128)} %copy.68), calls=%async_computation.3 | async-start | bytes 1048576 | tf_op jit(solution)/shard_map/all_to_all | solution.py:116
  92.4 0.4 convolution_bitcast_fusion.2
  92.8 18.3 %all-to-all-done.3 = f32[8,1,16384]{2,1,0:T(1,128)S(1)} async-done(((f32[8,1,16384]{2,1,0:T(1,128)}), f32[8,1,16384]{2,1,0:T(1,128)S(1)}, u32[]{:S(2)}, u32[]{:S(2)}) %all-to-all-start.3) | async-done | bytes 524320 | tf_op jit(solution)/shard_map/all_to_all | solution.py:116
  111.1 1.2 reduce.18
  112.5 12.8 %all-gather.6.cloned.1.call-done = bf16[768,2048]{1,0:T(8,128)(2,1)} async-done(((bf16[96,2048]{1,0:T(8,128)(2,1)}), bf16[768,2048]{1,0:T(8,128)(2,1)}) %all-gather.6.cloned.1.call-update) | async-done | bytes 3145744 | tf_op jit(solution)/shard_map/all_gather | solution.py:120
  125.3 0.4 fusion.67
  125.7 0.2 multiply_reduce_fusion.1
  125.9 1.1 fusion.17
  127.0 1.5 fusion.3
  128.5 5.3 %all-to-all-start.4 = ((f32[8,16,2048]{2,1,0:T(8,128)}), f32[8,16,2048]{2,1,0:T(8,128)}, u32[]{:S(2)}, u32[]{:S(2)}) async-start(f32[8,16,2048]{2,1,0:T(8,128)} %fusion.3), calls=%async_computation.4 | async-start | bytes 2097152 | tf_op jit(solution)/shard_map/all_to_all | solution.py:141
  133.9 15.0 %all-to-all-done.4 = f32[8,16,2048]{2,1,0:T(8,128)} async-done(((f32[8,16,2048]{2,1,0:T(8,128)}), f32[8,16,2048]{2,1,0:T(8,128)}, u32[]{:S(2)}, u32[]{:S(2)}) %all-to-all-start.4) | async-done | bytes 1048608 | tf_op jit(solution)/shard_map/all_to_all | solution.py:141
  148.8 1.3 reduce_sum.139
  150.1 0.1 fusion.30
  150.3 0.2 multiply_reduce_fusion.2
  150.6 14.4 %all-gather.2 = bf16[8,17,2048]{2,1,0:T(8,128)(2,1)S(1)} all-gather(bf16[1,17,2048]{2,1,0:T(8,128)(2,1)S(1)} %maximum_bitcast_fusion), channel_id=2, replica_groups=mesh['head'=8,'ga'=8,'gb'=8] {'head'}, dimensions={0}, use_global_device_ids=true | all-gather | bytes 626688 | tf_op jit(solution)/shard_map/all_gather | solution.py:154
  165.0 1.1 copy.69
  166.4 57.6 %all-gather.8.cloned.1.call-done = bf16[64,17,2048]{2,0,1:T(8,128)(2,1)} async-done(((bf16[8,17,2048]{2,0,1:T(8,128)(2,1)}), bf16[64,17,2048]{2,0,1:T(8,128)(2,1)}) %all-gather.8.cloned.1.call-update) | async-done | bytes 4456464 | tf_op jit(solution)/shard_map/all_gather | solution.py:154
  223.9 8.5 %fusion.68 = (f32[64,16]{0,1:T(8,128)S(1)}, f32[64,16,768]{2,0,1:T(8,128)}) fusion(bf16[64,17,2048]{2,0,1:T(8,128)(2,1)} %all-gather.8.cloned.1.call-done, bf16[768,2048]{1,0:T(8,128)(2,1)} %all-gather.6.cloned.1.call-done), kind=kOutput, calls=%fused_computation.138 | convolution fusion | flops 3222010880 | bytes 10752000 | tf_op jit(solution)/shard_map/slice | solution.py:166
  232.5 0.7 fusion.40
  233.4 2.5 exponential_reduce_fusion
  236.1 0.7 all_to_all.56
  236.8 6.5 %all-to-all-start.5 = ((f32[64,1,48]{2,1,0:T(1,128)}), f32[64,1,48]{2,1,0:T(1,128)S(1)}, u32[]{:S(2)}, u32[]{:S(2)}) async-start(f32[64,1,48]{2,1,0:T(1,128)} %bitcast.43), calls=%async_computation.5 | async-start | bytes 65536 | tf_op jit(solution)/shard_map/all_to_all | solution.py:179
  243.3 0.2 convert_reduce_fusion.1
  243.5 7.6 %all-to-all-done.5 = f32[64,1,48]{2,1,0:T(1,128)S(1)} async-done(((f32[64,1,48]{2,1,0:T(1,128)}), f32[64,1,48]{2,1,0:T(1,128)S(1)}, u32[]{:S(2)}, u32[]{:S(2)}) %all-to-all-start.5) | async-done | bytes 12320 | tf_op jit(solution)/shard_map/all_to_all | solution.py:179
  251.2 0.1 slice_reduce_fusion
  251.3 0.2 fusion.42
  251.7 12.2 %all_to_all.68 = f32[64,1,32]{2,1,0:T(1,128)S(1)} all-to-all(f32[64,1,32]{2,1,0:T(1,128)S(1)} %broadcast_in_dim.86), channel_id=1, replica_groups=mesh['head'=8,'ga'=8,'gb'=8] {'head','gb'}, dimensions={0} | all-to-all | bytes 16384 | tf_op jit(solution)/shard_map/all_to_all | solution.py:197
  263.9 0.6 broadcast_in_dim.87
  264.5 11.0 %all-to-all-start.7 = ((f32[8,1,32]{2,1,0:T(1,128)}), f32[8,1,32]{2,1,0:T(1,128)S(1)}, u32[]{:S(2)}, u32[]{:S(2)}) async-start(f32[8,1,32]{2,1,0:T(1,128)} %broadcast_in_dim.87), calls=%async_computation.7 | async-start | bytes 8192 | tf_op jit(solution)/shard_map/all_to_all | solution.py:197
  275.5 0.7 multiply_reduce_fusion
  277.0 9.9 %all-to-all-done.7 = f32[8,1,32]{2,1,0:T(1,128)S(1)} async-done(((f32[8,1,32]{2,1,0:T(1,128)}), f32[8,1,32]{2,1,0:T(1,128)S(1)}, u32[]{:S(2)}, u32[]{:S(2)}) %all-to-all-start.7) | async-done | bytes 1056 | tf_op jit(solution)/shard_map/all_to_all | solution.py:197
  286.9 0.5 convert_divide_fusion
  (69 shorter events, 2.1 us)
Async XLA Ops:
  7.2 119.8 %copy-start = (bf16[512,2048]{1,0:T(8,128)(2,1)S(1)}, bf16[512,2048]{1,0:T(8,128)(2,1)}, u32[]{:S(2)}) copy-start(bf16[512,2048]{1,0:T(8,128)(2,1)} %param.18) | copy-start | bytes 6291460
  18.8 13.5 %all-to-all-start = ((f32[8,1,16512]{2,1,0:T(1,128)}), f32[8,1,16512]{2,1,0:T(1,128)S(1)}, u32[]{:S(2)}, u32[]{:S(2)}) async-start(f32[8,1,16512]{2,1,0:T(1,128)} %all_to_all.45), calls=%async_computation | async-start | bytes 1056768 | tf_op jit(solution)/shard_map/all_to_all | solution.py:91
  25.2 100.1 %all-gather.6.cloned.1.call-start = ((), (), s32[]{:S(2)}) async-start(), calls=%async_computation.8 | async-start | bytes 3538944 | tf_op jit(solution)/shard_map/all_gather | solution.py:120
  32.3 60.1 %copy-start.2 = (bf16[128,512]{1,0:T(8,128)(2,1)S(1)}, bf16[128,512]{1,0:T(8,128)(2,1)}, u32[]{:S(2)}) copy-start(bf16[128,512]{1,0:T(8,128)(2,1)} %param.15) | copy-start | bytes 393220
  32.4 60.1 %copy-start.3 = (bf16[128,256]{1,0:T(8,128)(2,1)S(1)}, bf16[128,256]{1,0:T(8,128)(2,1)}, u32[]{:S(2)}) copy-start(bf16[128,256]{1,0:T(8,128)(2,1)} %param.14) | copy-start | bytes 196612
  32.4 60.1 %copy-start.4 = (bf16[128,256]{1,0:T(8,128)(2,1)S(1)}, bf16[128,256]{1,0:T(8,128)(2,1)}, u32[]{:S(2)}) copy-start(bf16[128,256]{1,0:T(8,128)(2,1)} %param.13) | copy-start | bytes 196612
  35.4 27.7 %all-to-all-start.1 = ((f32[8,1,2176]{2,1,0:T(1,128)}), f32[8,1,2176]{2,1,0:T(1,128)S(1)}, u32[]{:S(2)}, u32[]{:S(2)}) async-start(f32[8,1,2176]{2,1,0:T(1,128)} %all_to_all.48), calls=%async_computation.1 | async-start | bytes 139264 | tf_op jit(solution)/shard_map/all_to_all | solution.py:110
  64.4 19.3 %all-to-all-start.2 = ((f32[8,1,2048]{2,1,0:T(1,128)}), f32[8,1,2048]{2,1,0:T(1,128)S(1)}, u32[]{:S(2)}, u32[]{:S(2)}) async-start(f32[8,1,2048]{2,1,0:T(1,128)} %copy.67), calls=%async_computation.2 | async-start | bytes 131072 | tf_op jit(solution)/shard_map/all_to_all | solution.py:114
  85.6 25.5 %all-to-all-start.3 = ((f32[8,1,16384]{2,1,0:T(1,128)}), f32[8,1,16384]{2,1,0:T(1,128)S(1)}, u32[]{:S(2)}, u32[]{:S(2)}) async-start(f32[8,1,16384]{2,1,0:T(1,128)} %copy.68), calls=%async_computation.3 | async-start | bytes 1048576 | tf_op jit(solution)/shard_map/all_to_all | solution.py:116
  125.7 8.1 %copy-start.10 = (s32[1,16]{1,0:T(1,128)S(1)}, s32[1,16]{1,0:T(1,128)}, u32[]{:S(2)}) copy-start(s32[1,16]{1,0:T(1,128)} %param.22) | copy-start | bytes 196
  127.0 23.1 %copy-start.1 = (bf16[1,16,2048]{2,1,0:T(8,128)(2,1)S(1)}, bf16[1,16,2048]{2,1,0:T(8,128)(2,1)}, u32[]{:S(2)}) copy-start(bf16[1,16,2048]{2,1,0:T(8,128)(2,1)} %param.19) | copy-start | bytes 196612
  127.0 23.5 %copy-start.5 = (f32[2048]{0:T(1024)S(1)}, f32[2048]{0:T(1024)}, u32[]{:S(2)}) copy-start(f32[2048]{0:T(1024)} %param.20) | copy-start | bytes 24580
  128.5 20.3 %all-to-all-start.4 = ((f32[8,16,2048]{2,1,0:T(8,128)}), f32[8,16,2048]{2,1,0:T(8,128)}, u32[]{:S(2)}, u32[]{:S(2)}) async-start(f32[8,16,2048]{2,1,0:T(8,128)} %fusion.3), calls=%async_computation.4 | async-start | bytes 2097152 | tf_op jit(solution)/shard_map/all_to_all | solution.py:141
  133.8 90.2 %all-gather.8.cloned.1.call-start = ((), (), s32[]{:S(2)}) async-start(), calls=%async_computation.9 | async-start | bytes 5013504 | tf_op jit(solution)/shard_map/all_gather | solution.py:154
  232.4 19.1 %copy-start.8 = (f32[1,16]{1,0:T(1,128)S(1)}, f32[1,16]{1,0:T(1,128)}, u32[]{:S(2)}) copy-start(f32[1,16]{1,0:T(1,128)} %param.23) | copy-start | bytes 196
  232.4 19.1 %copy-start.9 = (s32[1,16]{1,0:T(1,128)S(1)}, s32[1,16]{1,0:T(1,128)}, u32[]{:S(2)}) copy-start(s32[1,16]{1,0:T(1,128)} %param.24) | copy-start | bytes 196
  232.4 54.5 %copy-start.7 = (s32[32]{0:T(128)S(1)}, s32[32]{0:T(128)}, u32[]{:S(2)}) copy-start(s32[32]{0:T(128)} %param.25) | copy-start | bytes 388
  236.8 14.3 %all-to-all-start.5 = ((f32[64,1,48]{2,1,0:T(1,128)}), f32[64,1,48]{2,1,0:T(1,128)S(1)}, u32[]{:S(2)}, u32[]{:S(2)}) async-start(f32[64,1,48]{2,1,0:T(1,128)} %bitcast.43), calls=%async_computation.5 | async-start | bytes 65536 | tf_op jit(solution)/shard_map/all_to_all | solution.py:179
  251.3 36.1 %copy-start.6 = (f32[16]{0:T(128)}, f32[16]{0:T(128)S(1)}, u32[]{:S(2)}) copy-start(f32[16]{0:T(128)S(1)} %get-tuple-element.12) | copy-start | bytes 196
  264.5 22.4 %all-to-all-start.7 = ((f32[8,1,32]{2,1,0:T(1,128)}), f32[8,1,32]{2,1,0:T(1,128)S(1)}, u32[]{:S(2)}, u32[]{:S(2)}) async-start(f32[8,1,32]{2,1,0:T(1,128)} %broadcast_in_dim.87), calls=%async_computation.7 | async-start | bytes 8192 | tf_op jit(solution)/shard_map/all_to_all | solution.py:197
Sparse Core Ops, SparseCore 0:
  28.0 97.1 all-gather.5
  166.3 57.6 all-gather.7

commit v9 on v8

--- a/solution.py
+++ b/solution.py
@@ -151,7 +151,7 @@
     code = jnp.concatenate([targets[0] // 256, targets[0] % 256]).astype(jnp.bfloat16)
     code_row = jnp.pad(code, (0, hidden.shape[1] - code.shape[0]))[None, :]
     hidden_ext = jnp.concatenate([hidden, code_row], axis=0)
-    gathered = lax.all_gather(lax.all_gather(hidden_ext, "head"), "gb")
+    gathered = lax.all_gather(lax.all_gather(hidden_ext, "gb"), "head")
     code_all = gathered[:, :, slice_rows, : 2 * slice_rows].astype(jnp.int32)
     all_targets = (code_all[..., :slice_rows] * 256 + code_all[..., slice_rows:]).reshape(-1)
     entry_ids = (
@@ -174,8 +174,8 @@
     top = jnp.max(logits, axis=1)
     exp_total = jnp.sum(jnp.exp(logits - top[:, None]), axis=1)
     picked = jnp.sum(jnp.where(entry_ids[None, :] == all_targets[:, None], logits, 0.0), axis=1)
-    outgoing = jnp.stack([top, exp_total, picked]).reshape(3, sub, head_count, slice_rows)
-    outgoing = jnp.transpose(outgoing, (2, 1, 0, 3)).reshape(head_count * sub, 3 * slice_rows)
+    outgoing = jnp.stack([top, exp_total, picked]).reshape(3, head_count, sub, slice_rows)
+    outgoing = jnp.transpose(outgoing, (1, 2, 0, 3)).reshape(head_count * sub, 3 * slice_rows)
     incoming = lax.all_to_all(outgoing, ("head", "gb"), 0, 0, tiled=True).reshape(
         head_count * sub, 3, slice_rows
     )

time: 296 us -> 291 us (0.983)
  waiting for transfers between devices: 157 us -> 140 us
  blocking collectives: 26.5 us -> 37.5 us
    all_gather x1, waiting for transfers between devices: 57.6 us -> 40.9 us  [per_device(): gathered = lax.all_gather(lax.all_gather(hidden_ext, 'gb'), 'head')]
    all_gather x1, blocking collectives: 14.4 us -> 25.3 us  [per_device(): gathered = lax.all_gather(lax.all_gather(hidden_ext, 'gb'), 'head')]
where the time goes in v9:
time: 291 us; the launch traced here: 290 us
  waiting for transfers between devices  140 us (48%)
  starting transfers between devices  54.5 us (19%)
  blocking collectives  37.5 us (13%)
  between operations  17.7 us (6%)
  other arithmetic  16.5 us (6%)
  matrix products  13.5 us (5%)
  local copies, waits for them, and re-layouts  10.3 us (4%)
    all_gather x1, waiting for transfers between devices, per_device(): gathered = lax.all_gather(lax.all_gather(hidden_ext, 'gb'), 'head')  40.9 us
    all_gather x1, blocking collectives, per_device(): gathered = lax.all_gather(lax.all_gather(hidden_ext, 'gb'), 'head')  25.3 us
    all_to_all x1, waiting for transfers between devices, per_device(): lax.all_to_all(slices_out, 'gb', 0, 0, tiled=True)  18.3 us
    all_to_all x1, waiting for transfers between devices, per_device(): octet_in = lax.all_to_all(octet_in, 'ga', 0, 0, tiled=True).reshape(chunk)  15.6 us
    all_to_all x1, waiting for transfers between devices, per_device(): lax.all_to_all(branch_parts.reshape(head_count, slice_rows, -1), 'head',...  15 us
    all_to_all x1, starting transfers between devices, per_device(): received = lax.all_to_all(payload, 'ga', 0, 0, tiled=True)  14.5 us
    all_to_all x1, waiting for transfers between devices, per_device(): received = lax.all_to_all(payload, 'ga', 0, 0, tiled=True)  13.2 us
    all_gather x1, waiting for transfers between devices, per_device(): vocab_rows = lax.all_gather(vocab_weight, 'ga', axis=0, tiled=True)  12.8 us
  transfers between devices with their start and end apart: 9, of which 9 were waited for; matrix products, arithmetic and copies ran while one was open for 3% of the time, Pallas kernels for 0%

profile of v9, /device:TPU:1, one launch (start us, length us, event | category | flops | bytes accessed | tf_op | source)
XLA Modules:
  0.0 290.4 jit_solution(12553107043667105414)
XLA Ops:
  7.2 0.9 copy.72
  8.1 0.1 reduce.13
  8.3 0.7 sub.101
  9.2 0.6 fusion.66
  9.8 0.8 copy.73
  10.6 0.2 reduce_window_sum.18
  10.7 0.6 slice.84
  12.1 0.1 reduce.14
  12.2 1.3 fusion.64
  14.0 2.0 select_multiply_fusion
  16.0 1.4 fusion.18
  17.6 1.2 all_to_all.45
  18.8 6.4 %all-to-all-start = ((f32[8,1,16512]{2,1,0:T(1,128)}), f32[8,1,16512]{2,1,0:T(1,128)S(1)}, u32[]{:S(2)}, u32[]{:S(2)}) async-start(f32[8,1,16512]{2,1,0:T(1,128)} %all_to_all.45), calls=%async_computation | async-start | bytes 1056768 | tf_op jit(solution)/shard_map/all_to_all | solution.py:91
  25.2 0.7 all-gather.6.cloned.1.call-update
  25.9 6.4 %all-to-all-done = f32[8,1,16512]{2,1,0:T(1,128)S(1)} async-done(((f32[8,1,16512]{2,1,0:T(1,128)}), f32[8,1,16512]{2,1,0:T(1,128)S(1)}, u32[]{:S(2)}, u32[]{:S(2)}) %all-to-all-start) | async-done | bytes 528416 | tf_op jit(solution)/shard_map/all_to_all | solution.py:91
  32.4 0.7 slice_reduce_fusion.4
  33.2 0.2 select_reduce_fusion.1
  33.4 0.6 fusion.53
  34.0 0.7 pad_select_fusion.1
  34.7 0.7 all_to_all.48
  35.4 14.5 %all-to-all-start.1 = ((f32[8,1,2176]{2,1,0:T(1,128)}), f32[8,1,2176]{2,1,0:T(1,128)S(1)}, u32[]{:S(2)}, u32[]{:S(2)}) async-start(f32[8,1,2176]{2,1,0:T(1,128)} %all_to_all.48), calls=%async_computation.1 | async-start | bytes 139264 | tf_op jit(solution)/shard_map/all_to_all | solution.py:110
  49.9 13.2 %all-to-all-done.1 = f32[8,1,2176]{2,1,0:T(1,128)S(1)} async-done(((f32[8,1,2176]{2,1,0:T(1,128)}), f32[8,1,2176]{2,1,0:T(1,128)S(1)}, u32[]{:S(2)}, u32[]{:S(2)}) %all-to-all-start.1) | async-done | bytes 69664 | tf_op jit(solution)/shard_map/all_to_all | solution.py:110
  63.1 0.1 slice_reduce_fusion.2
  63.2 0.3 fusion.31
  63.6 0.2 convolution_bitcast_fusion
  63.8 0.7 copy.74
  64.4 3.3 %all-to-all-start.2 = ((f32[8,1,2048]{2,1,0:T(1,128)}), f32[8,1,2048]{2,1,0:T(1,128)S(1)}, u32[]{:S(2)}, u32[]{:S(2)}) async-start(f32[8,1,2048]{2,1,0:T(1,128)} %copy.74), calls=%async_computation.2 | async-start | bytes 131072 | tf_op jit(solution)/shard_map/all_to_all | solution.py:114
  67.8 0.1 slice_reduce_fusion.3
  68.0 0.2 reduce-window.18
  68.2 15.6 %all-to-all-done.2 = f32[8,1,2048]{2,1,0:T(1,128)S(1)} async-done(((f32[8,1,2048]{2,1,0:T(1,128)}), f32[8,1,2048]{2,1,0:T(1,128)S(1)}, u32[]{:S(2)}, u32[]{:S(2)}) %all-to-all-start.2) | async-done | bytes 65568 | tf_op jit(solution)/shard_map/all_to_all | solution.py:114
  83.7 0.6 fusion
  84.3 1.3 copy.75
  85.6 6.8 %all-to-all-start.3 = ((f32[8,1,16384]{2,1,0:T(1,128)}), f32[8,1,16384]{2,1,0:T(1,128)S(1)}, u32[]{:S(2)}, u32[]{:S(2)}) async-start(f32[8,1,16384]{2,1,0:T(1,128)} %copy.75), calls=%async_computation.3 | async-start | bytes 1048576 | tf_op jit(solution)/shard_map/all_to_all | solution.py:116
  92.4 0.4 convolution_bitcast_fusion.2
  92.8 18.3 %all-to-all-done.3 = f32[8,1,16384]{2,1,0:T(1,128)S(1)} async-done(((f32[8,1,16384]{2,1,0:T(1,128)}), f32[8,1,16384]{2,1,0:T(1,128)S(1)}, u32[]{:S(2)}, u32[]{:S(2)}) %all-to-all-start.3) | async-done | bytes 524320 | tf_op jit(solution)/shard_map/all_to_all | solution.py:116
  111.1 1.2 reduce.18
  112.5 12.8 %all-gather.6.cloned.1.call-done = bf16[768,2048]{1,0:T(8,128)(2,1)} async-done(((bf16[96,2048]{1,0:T(8,128)(2,1)}), bf16[768,2048]{1,0:T(8,128)(2,1)}) %all-gather.6.cloned.1.call-update) | async-done | bytes 3145744 | tf_op jit(solution)/shard_map/all_gather | solution.py:120
  125.3 0.4 fusion.67
  125.7 0.2 multiply_reduce_fusion.1
  125.9 1.1 fusion.17
  127.0 1.5 fusion.3
  128.5 5.3 %all-to-all-start.4 = ((f32[8,16,2048]{2,1,0:T(8,128)}), f32[8,16,2048]{2,1,0:T(8,128)}, u32[]{:S(2)}, u32[]{:S(2)}) async-start(f32[8,16,2048]{2,1,0:T(8,128)} %fusion.3), calls=%async_computation.4 | async-start | bytes 2097152 | tf_op jit(solution)/shard_map/all_to_all | solution.py:141
  133.9 15.0 %all-to-all-done.4 = f32[8,16,2048]{2,1,0:T(8,128)} async-done(((f32[8,16,2048]{2,1,0:T(8,128)}), f32[8,16,2048]{2,1,0:T(8,128)}, u32[]{:S(2)}, u32[]{:S(2)}) %all-to-all-start.4) | async-done | bytes 1048608 | tf_op jit(solution)/shard_map/all_to_all | solution.py:141
  148.8 1.3 reduce_sum.139
  150.1 0.1 fusion.30
  150.3 0.2 multiply_reduce_fusion.2
  150.6 25.3 %all-gather.2 = bf16[8,17,2048]{2,1,0:T(8,128)(2,1)S(1)} all-gather(bf16[1,17,2048]{2,1,0:T(8,128)(2,1)S(1)} %maximum_bitcast_fusion), channel_id=2, replica_groups=mesh['head'=8,'ga'=8,'gb'=8] {'gb'}, dimensions={0}, use_global_device_ids=true | all-gather | bytes 626688 | tf_op jit(solution)/shard_map/all_gather | solution.py:154
  176.0 1.1 copy.76
  177.3 40.9 %all-gather.8.cloned.1.call-done = bf16[64,17,2048]{2,0,1:T(8,128)(2,1)} async-done(((bf16[8,17,2048]{2,0,1:T(8,128)(2,1)}), bf16[64,17,2048]{2,0,1:T(8,128)(2,1)}) %all-gather.8.cloned.1.call-update) | async-done | bytes 4456464 | tf_op jit(solution)/shard_map/all_gather | solution.py:154
  218.2 8.5 %fusion.68 = (f32[64,16]{0,1:T(8,128)S(1)}, f32[64,16,768]{2,0,1:T(8,128)}) fusion(bf16[64,17,2048]{2,0,1:T(8,128)(2,1)} %all-gather.8.cloned.1.call-done, bf16[768,2048]{1,0:T(8,128)(2,1)} %all-gather.6.cloned.1.call-done), kind=kOutput, calls=%fused_computation.138 | convolution fusion | flops 3222010880 | bytes 10752000 | tf_op jit(solution)/shard_map/slice | solution.py:166
  226.8 0.7 fusion.40
  227.6 2.5 exponential_reduce_fusion
  230.4 0.7 all_to_all.56
  231.1 7.2 %all-to-all-start.5 = ((f32[64,1,48]{2,1,0:T(1,128)}), f32[64,1,48]{2,1,0:T(1,128)S(1)}, u32[]{:S(2)}, u32[]{:S(2)}) async-start(f32[64,1,48]{2,1,0:T(1,128)} %bitcast.43), calls=%async_computation.5 | async-start | bytes 65536 | tf_op jit(solution)/shard_map/all_to_all | solution.py:179
  238.4 0.2 convert_reduce_fusion.1
  238.5 7.6 %all-to-all-done.5 = f32[64,1,48]{2,1,0:T(1,128)S(1)} async-done(((f32[64,1,48]{2,1,0:T(1,128)}), f32[64,1,48]{2,1,0:T(1,128)S(1)}, u32[]{:S(2)}, u32[]{:S(2)}) %all-to-all-start.5) | async-done | bytes 12320 | tf_op jit(solution)/shard_map/all_to_all | solution.py:179
  246.2 0.1 slice_reduce_fusion
  246.3 0.2 fusion.42
  246.7 12.2 %all_to_all.68 = f32[64,1,32]{2,1,0:T(1,128)S(1)} all-to-all(f32[64,1,32]{2,1,0:T(1,128)S(1)} %broadcast_in_dim.86), channel_id=1, replica_groups=mesh['head'=8,'ga'=8,'gb'=8] {'head','gb'}, dimensions={0} | all-to-all | bytes 16384 | tf_op jit(solution)/shard_map/all_to_all | solution.py:197
  258.9 0.6 broadcast_in_dim.87
  259.5 11.0 %all-to-all-start.7 = ((f32[8,1,32]{2,1,0:T(1,128)}), f32[8,1,32]{2,1,0:T(1,128)S(1)}, u32[]{:S(2)}, u32[]{:S(2)}) async-start(f32[8,1,32]{2,1,0:T(1,128)} %broadcast_in_dim.87), calls=%async_computation.7 | async-start | bytes 8192 | tf_op jit(solution)/shard_map/all_to_all | solution.py:197
  270.5 0.7 multiply_reduce_fusion
  272.0 9.9 %all-to-all-done.7 = f32[8,1,32]{2,1,0:T(1,128)S(1)} async-done(((f32[8,1,32]{2,1,0:T(1,128)}), f32[8,1,32]{2,1,0:T(1,128)S(1)}, u32[]{:S(2)}, u32[]{:S(2)}) %all-to-all-start.7) | async-done | bytes 1056 | tf_op jit(solution)/shard_map/all_to_all | solution.py:197
  281.9 0.5 convert_divide_fusion
  (69 shorter events, 2.1 us)
Async XLA Ops:
  7.2 119.8 %copy-start = (bf16[512,2048]{1,0:T(8,128)(2,1)S(1)}, bf16[512,2048]{1,0:T(8,128)(2,1)}, u32[]{:S(2)}) copy-start(bf16[512,2048]{1,0:T(8,128)(2,1)} %param.18) | copy-start | bytes 6291460
  18.8 13.5 %all-to-all-start = ((f32[8,1,16512]{2,1,0:T(1,128)}), f32[8,1,16512]{2,1,0:T(1,128)S(1)}, u32[]{:S(2)}, u32[]{:S(2)}) async-start(f32[8,1,16512]{2,1,0:T(1,128)} %all_to_all.45), calls=%async_computation | async-start | bytes 1056768 | tf_op jit(solution)/shard_map/all_to_all | solution.py:91
  25.2 100.1 %all-gather.6.cloned.1.call-start = ((), (), s32[]{:S(2)}) async-start(), calls=%async_computation.8 | async-start | bytes 3538944 | tf_op jit(solution)/shard_map/all_gather | solution.py:120
  32.3 60.1 %copy-start.2 = (bf16[128,512]{1,0:T(8,128)(2,1)S(1)}, bf16[128,512]{1,0:T(8,128)(2,1)}, u32[]{:S(2)}) copy-start(bf16[128,512]{1,0:T(8,128)(2,1)} %param.15) | copy-start | bytes 393220
  32.4 60.1 %copy-start.3 = (bf16[128,256]{1,0:T(8,128)(2,1)S(1)}, bf16[128,256]{1,0:T(8,128)(2,1)}, u32[]{:S(2)}) copy-start(bf16[128,256]{1,0:T(8,128)(2,1)} %param.14) | copy-start | bytes 196612
  32.4 60.1 %copy-start.4 = (bf16[128,256]{1,0:T(8,128)(2,1)S(1)}, bf16[128,256]{1,0:T(8,128)(2,1)}, u32[]{:S(2)}) copy-start(bf16[128,256]{1,0:T(8,128)(2,1)} %param.13) | copy-start | bytes 196612
  35.4 27.7 %all-to-all-start.1 = ((f32[8,1,2176]{2,1,0:T(1,128)}), f32[8,1,2176]{2,1,0:T(1,128)S(1)}, u32[]{:S(2)}, u32[]{:S(2)}) async-start(f32[8,1,2176]{2,1,0:T(1,128)} %all_to_all.48), calls=%async_computation.1 | async-start | bytes 139264 | tf_op jit(solution)/shard_map/all_to_all | solution.py:110
  64.4 19.3 %all-to-all-start.2 = ((f32[8,1,2048]{2,1,0:T(1,128)}), f32[8,1,2048]{2,1,0:T(1,128)S(1)}, u32[]{:S(2)}, u32[]{:S(2)}) async-start(f32[8,1,2048]{2,1,0:T(1,128)} %copy.74), calls=%async_computation.2 | async-start | bytes 131072 | tf_op jit(solution)/shard_map/all_to_all | solution.py:114
  85.6 25.5 %all-to-all-start.3 = ((f32[8,1,16384]{2,1,0:T(1,128)}), f32[8,1,16384]{2,1,0:T(1,128)S(1)}, u32[]{:S(2)}, u32[]{:S(2)}) async-start(f32[8,1,16384]{2,1,0:T(1,128)} %copy.75), calls=%async_computation.3 | async-start | bytes 1048576 | tf_op jit(solution)/shard_map/all_to_all | solution.py:116
  125.7 8.1 %copy-start.10 = (s32[1,16]{1,0:T(1,128)S(1)}, s32[1,16]{1,0:T(1,128)}, u32[]{:S(2)}) copy-start(s32[1,16]{1,0:T(1,128)} %param.22) | copy-start | bytes 196
  127.0 23.1 %copy-start.1 = (bf16[1,16,2048]{2,1,0:T(8,128)(2,1)S(1)}, bf16[1,16,2048]{2,1,0:T(8,128)(2,1)}, u32[]{:S(2)}) copy-start(bf16[1,16,2048]{2,1,0:T(8,128)(2,1)} %param.19) | copy-start | bytes 196612
  127.0 23.5 %copy-start.5 = (f32[2048]{0:T(1024)S(1)}, f32[2048]{0:T(1024)}, u32[]{:S(2)}) copy-start(f32[2048]{0:T(1024)} %param.20) | copy-start | bytes 24580
  128.5 20.3 %all-to-all-start.4 = ((f32[8,16,2048]{2,1,0:T(8,128)}), f32[8,16,2048]{2,1,0:T(8,128)}, u32[]{:S(2)}, u32[]{:S(2)}) async-start(f32[8,16,2048]{2,1,0:T(8,128)} %fusion.3), calls=%async_computation.4 | async-start | bytes 2097152 | tf_op jit(solution)/shard_map/all_to_all | solution.py:141
  133.8 84.5 %all-gather.8.cloned.1.call-start = ((), (), s32[]{:S(2)}) async-start(), calls=%async_computation.9 | async-start | bytes 5013504 | tf_op jit(solution)/shard_map/all_gather | solution.py:154
  226.7 19.8 %copy-start.8 = (f32[1,16]{1,0:T(1,128)S(1)}, f32[1,16]{1,0:T(1,128)}, u32[]{:S(2)}) copy-start(f32[1,16]{1,0:T(1,128)} %param.23) | copy-start | bytes 196
  226.7 19.8 %copy-start.9 = (s32[1,16]{1,0:T(1,128)S(1)}, s32[1,16]{1,0:T(1,128)}, u32[]{:S(2)}) copy-start(s32[1,16]{1,0:T(1,128)} %param.24) | copy-start | bytes 196
  226.7 55.2 %copy-start.7 = (s32[32]{0:T(128)S(1)}, s32[32]{0:T(128)}, u32[]{:S(2)}) copy-start(s32[32]{0:T(128)} %param.25) | copy-start | bytes 388
  231.1 15.0 %all-to-all-start.5 = ((f32[64,1,48]{2,1,0:T(1,128)}), f32[64,1,48]{2,1,0:T(1,128)S(1)}, u32[]{:S(2)}, u32[]{:S(2)}) async-start(f32[64,1,48]{2,1,0:T(1,128)} %bitcast.43), calls=%async_computation.5 | async-start | bytes 65536 | tf_op jit(solution)/shard_map/all_to_all | solution.py:179
  246.3 36.1 %copy-start.6 = (f32[16]{0:T(128)}, f32[16]{0:T(128)S(1)}, u32[]{:S(2)}) copy-start(f32[16]{0:T(128)S(1)} %get-tuple-element.12) | copy-start | bytes 196
  259.5 22.4 %all-to-all-start.7 = ((f32[8,1,32]{2,1,0:T(1,128)}), f32[8,1,32]{2,1,0:T(1,128)S(1)}, u32[]{:S(2)}, u32[]{:S(2)}) async-start(f32[8,1,32]{2,1,0:T(1,128)} %broadcast_in_dim.87), calls=%async_computation.7 | async-start | bytes 8192 | tf_op jit(solution)/shard_map/all_to_all | solution.py:197
Sparse Core Ops, SparseCore 0:
  28.0 97.1 all-gather.5
  177.2 40.9 all-gather.7

commit v10 on v9

--- a/solution.py
+++ b/solution.py
@@ -151,7 +151,8 @@
     code = jnp.concatenate([targets[0] // 256, targets[0] % 256]).astype(jnp.bfloat16)
     code_row = jnp.pad(code, (0, hidden.shape[1] - code.shape[0]))[None, :]
     hidden_ext = jnp.concatenate([hidden, code_row], axis=0)
-    gathered = lax.all_gather(lax.all_gather(hidden_ext, "gb"), "head")
+    spread = jnp.broadcast_to(hidden_ext[None], (sub,) + hidden_ext.shape)
+    gathered = lax.all_gather(lax.all_to_all(spread, "gb", 0, 0, tiled=True), "head")
     code_all = gathered[:, :, slice_rows, : 2 * slice_rows].astype(jnp.int32)
     all_targets = (code_all[..., :slice_rows] * 256 + code_all[..., slice_rows:]).reshape(-1)
     entry_ids = (

time: 291 us -> 277 us (0.952)
  blocking collectives: 37.5 us -> 28.6 us
  waiting for transfers between devices: 140 us -> 134 us
    all_gather x1 -> x0, blocking collectives: 25.3 us -> none  [per_device(): gathered = lax.all_gather(lax.all_gather(hidden_ext, 'gb'), 'head')]
    all_to_all x0 -> x1, blocking collectives: none -> 16.5 us  [per_device(): lax.all_to_all(spread, 'gb', 0, 0, tiled=True)]
    all_gather x1, waiting for transfers between devices: 40.9 us -> 35 us  [per_device(): lax.all_gather(lax.all_to_all(spread, 'gb', 0, 0, tiled=True), 'head')]
where the time goes in v10:
time: 277 us; the launch traced here: 276 us
  waiting for transfers between devices  134 us (48%)
  starting transfers between devices  54.5 us (20%)
  blocking collectives  28.6 us (10%)
  between operations  17.7 us (6%)
  other arithmetic  16.5 us (6%)
  matrix products  13.5 us (5%)
  local copies, waits for them, and re-layouts  10.4 us (4%)
    all_gather x1, waiting for transfers between devices, per_device(): lax.all_gather(lax.all_to_all(spread, 'gb', 0, 0, tiled=True), 'head')  35 us
    all_to_all x1, waiting for transfers between devices, per_device(): lax.all_to_all(slices_out, 'gb', 0, 0, tiled=True)  18.3 us
    all_to_all x1, blocking collectives, per_device(): lax.all_to_all(spread, 'gb', 0, 0, tiled=True)  16.5 us
    all_to_all x1, waiting for transfers between devices, per_device(): octet_in = lax.all_to_all(octet_in, 'ga', 0, 0, tiled=True).reshape(chunk)  15.6 us
    all_to_all x1, waiting for transfers between devices, per_device(): lax.all_to_all(branch_parts.reshape(head_count, slice_rows, -1), 'head',...  15 us
    all_to_all x1, starting transfers between devices, per_device(): received = lax.all_to_all(payload, 'ga', 0, 0, tiled=True)  14.5 us
    all_to_all x1, waiting for transfers between devices, per_device(): received = lax.all_to_all(payload, 'ga', 0, 0, tiled=True)  13.2 us
    all_gather x1, waiting for transfers between devices, per_device(): vocab_rows = lax.all_gather(vocab_weight, 'ga', axis=0, tiled=True)  12.8 us
  transfers between devices with their start and end apart: 9, of which 9 were waited for; matrix products, arithmetic and copies ran while one was open for 3% of the time, Pallas kernels for 0%

profile of v10, /device:TPU:1, one launch (start us, length us, event | category | flops | bytes accessed | tf_op | source)
XLA Modules:
  0.0 275.7 jit_solution(8955163061083523556)
XLA Ops:
  7.2 0.9 copy.70
  8.1 0.1 reduce.13
  8.3 0.7 sub.101
  9.2 0.6 fusion.66
  9.8 0.8 copy.71
  10.6 0.2 reduce_window_sum.18
  10.7 0.6 slice.84
  12.1 0.1 reduce.14
  12.2 1.3 fusion.64
  14.0 2.0 select_multiply_fusion
  16.0 1.4 fusion.18
  17.6 1.2 all_to_all.48
  18.8 6.4 %all-to-all-start = ((f32[8,1,16512]{2,1,0:T(1,128)}), f32[8,1,16512]{2,1,0:T(1,128)S(1)}, u32[]{:S(2)}, u32[]{:S(2)}) async-start(f32[8,1,16512]{2,1,0:T(1,128)} %all_to_all.48), calls=%async_computation | async-start | bytes 1056768 | tf_op jit(solution)/shard_map/all_to_all | solution.py:91
  25.2 0.7 all-gather.4.cloned.1.call-update
  25.9 6.4 %all-to-all-done = f32[8,1,16512]{2,1,0:T(1,128)S(1)} async-done(((f32[8,1,16512]{2,1,0:T(1,128)}), f32[8,1,16512]{2,1,0:T(1,128)S(1)}, u32[]{:S(2)}, u32[]{:S(2)}) %all-to-all-start) | async-done | bytes 528416 | tf_op jit(solution)/shard_map/all_to_all | solution.py:91
  32.4 0.7 slice_reduce_fusion.4
  33.2 0.2 select_reduce_fusion.1
  33.4 0.6 fusion.53
  34.0 0.7 pad_select_fusion.1
  34.7 0.7 all_to_all.51
  35.4 14.5 %all-to-all-start.1 = ((f32[8,1,2176]{2,1,0:T(1,128)}), f32[8,1,2176]{2,1,0:T(1,128)S(1)}, u32[]{:S(2)}, u32[]{:S(2)}) async-start(f32[8,1,2176]{2,1,0:T(1,128)} %all_to_all.51), calls=%async_computation.1 | async-start | bytes 139264 | tf_op jit(solution)/shard_map/all_to_all | solution.py:110
  49.9 13.2 %all-to-all-done.1 = f32[8,1,2176]{2,1,0:T(1,128)S(1)} async-done(((f32[8,1,2176]{2,1,0:T(1,128)}), f32[8,1,2176]{2,1,0:T(1,128)S(1)}, u32[]{:S(2)}, u32[]{:S(2)}) %all-to-all-start.1) | async-done | bytes 69664 | tf_op jit(solution)/shard_map/all_to_all | solution.py:110
  63.1 0.1 slice_reduce_fusion.2
  63.2 0.3 fusion.31
  63.6 0.2 convolution_bitcast_fusion
  63.8 0.7 copy.72
  64.4 3.3 %all-to-all-start.2 = ((f32[8,1,2048]{2,1,0:T(1,128)}), f32[8,1,2048]{2,1,0:T(1,128)S(1)}, u32[]{:S(2)}, u32[]{:S(2)}) async-start(f32[8,1,2048]{2,1,0:T(1,128)} %copy.72), calls=%async_computation.2 | async-start | bytes 131072 | tf_op jit(solution)/shard_map/all_to_all | solution.py:114
  67.8 0.1 slice_reduce_fusion.3
  68.0 0.2 reduce-window.18
  68.2 15.6 %all-to-all-done.2 = f32[8,1,2048]{2,1,0:T(1,128)S(1)} async-done(((f32[8,1,2048]{2,1,0:T(1,128)}), f32[8,1,2048]{2,1,0:T(1,128)S(1)}, u32[]{:S(2)}, u32[]{:S(2)}) %all-to-all-start.2) | async-done | bytes 65568 | tf_op jit(solution)/shard_map/all_to_all | solution.py:114
  83.7 0.6 fusion
  84.3 1.3 copy.73
  85.6 6.8 %all-to-all-start.3 = ((f32[8,1,16384]{2,1,0:T(1,128)}), f32[8,1,16384]{2,1,0:T(1,128)S(1)}, u32[]{:S(2)}, u32[]{:S(2)}) async-start(f32[8,1,16384]{2,1,0:T(1,128)} %copy.73), calls=%async_computation.3 | async-start | bytes 1048576 | tf_op jit(solution)/shard_map/all_to_all | solution.py:116
  92.4 0.4 convolution_bitcast_fusion.2
  92.8 18.3 %all-to-all-done.3 = f32[8,1,16384]{2,1,0:T(1,128)S(1)} async-done(((f32[8,1,16384]{2,1,0:T(1,128)}), f32[8,1,16384]{2,1,0:T(1,128)S(1)}, u32[]{:S(2)}, u32[]{:S(2)}) %all-to-all-start.3) | async-done | bytes 524320 | tf_op jit(solution)/shard_map/all_to_all | solution.py:116
  111.1 1.2 reduce.18
  112.5 12.8 %all-gather.4.cloned.1.call-done = bf16[768,2048]{1,0:T(8,128)(2,1)} async-done(((bf16[96,2048]{1,0:T(8,128)(2,1)}), bf16[768,2048]{1,0:T(8,128)(2,1)}) %all-gather.4.cloned.1.call-update) | async-done | bytes 3145744 | tf_op jit(solution)/shard_map/all_gather | solution.py:120
  125.3 0.4 fusion.67
  125.7 0.2 multiply_reduce_fusion.1
  125.9 1.1 fusion.17
  127.0 1.5 fusion.3
  128.5 5.3 %all-to-all-start.4 = ((f32[8,16,2048]{2,1,0:T(8,128)}), f32[8,16,2048]{2,1,0:T(8,128)}, u32[]{:S(2)}, u32[]{:S(2)}) async-start(f32[8,16,2048]{2,1,0:T(8,128)} %fusion.3), calls=%async_computation.4 | async-start | bytes 2097152 | tf_op jit(solution)/shard_map/all_to_all | solution.py:141
  133.9 15.0 %all-to-all-done.4 = f32[8,16,2048]{2,1,0:T(8,128)} async-done(((f32[8,16,2048]{2,1,0:T(8,128)}), f32[8,16,2048]{2,1,0:T(8,128)}, u32[]{:S(2)}, u32[]{:S(2)}) %all-to-all-start.4) | async-done | bytes 1048608 | tf_op jit(solution)/shard_map/all_to_all | solution.py:141
  148.8 1.3 reduce_sum.139
  150.1 0.1 fusion.30
  150.3 0.2 multiply_reduce_fusion.2
  150.7 16.5 %all_to_all.73 = bf16[8,17,2048]{2,1,0:T(8,128)(2,1)S(1)} all-to-all(bf16[8,17,2048]{2,1,0:T(8,128)(2,1)S(1)} %broadcast_in_dim.87), channel_id=1, replica_groups=mesh['head'=8,'ga'=8,'gb'=8] {'gb'}, dimensions={0} | all-to-all | bytes 1114112 | tf_op jit(solution)/shard_map/all_to_all | solution.py:155
  167.2 1.1 copy.74
  168.6 35.0 %all-gather.6.cloned.1.call-done = bf16[64,17,2048]{2,0,1:T(8,128)(2,1)} async-done(((bf16[8,17,2048]{2,0,1:T(8,128)(2,1)}), bf16[64,17,2048]{2,0,1:T(8,128)(2,1)}) %all-gather.6.cloned.1.call-update) | async-done | bytes 4456464 | tf_op jit(solution)/shard_map/all_gather | solution.py:155
  203.5 8.5 %fusion.68 = (f32[64,16]{0,1:T(8,128)S(1)}, f32[64,16,768]{2,0,1:T(8,128)}) fusion(bf16[64,17,2048]{2,0,1:T(8,128)(2,1)} %all-gather.6.cloned.1.call-done, bf16[768,2048]{1,0:T(8,128)(2,1)} %all-gather.4.cloned.1.call-done), kind=kOutput, calls=%fused_computation.138 | convolution fusion | flops 3222010880 | bytes 10752000 | tf_op jit(solution)/shard_map/slice | solution.py:167
  212.1 0.7 fusion.40
  213.0 2.5 exponential_reduce_fusion
  215.7 0.7 all_to_all.60
  216.4 7.2 %all-to-all-start.6 = ((f32[64,1,48]{2,1,0:T(1,128)}), f32[64,1,48]{2,1,0:T(1,128)S(1)}, u32[]{:S(2)}, u32[]{:S(2)}) async-start(f32[64,1,48]{2,1,0:T(1,128)} %bitcast.42), calls=%async_computation.6 | async-start | bytes 65536 | tf_op jit(solution)/shard_map/all_to_all | solution.py:180
  223.7 0.2 convert_reduce_fusion.1
  223.8 7.6 %all-to-all-done.6 = f32[64,1,48]{2,1,0:T(1,128)S(1)} async-done(((f32[64,1,48]{2,1,0:T(1,128)}), f32[64,1,48]{2,1,0:T(1,128)S(1)}, u32[]{:S(2)}, u32[]{:S(2)}) %all-to-all-start.6) | async-done | bytes 12320 | tf_op jit(solution)/shard_map/all_to_all | solution.py:180
  231.5 0.1 slice_reduce_fusion
  231.6 0.2 fusion.42
  232.0 12.2 %all_to_all.74 = f32[64,1,32]{2,1,0:T(1,128)S(1)} all-to-all(f32[64,1,32]{2,1,0:T(1,128)S(1)} %broadcast_in_dim.89), channel_id=1, replica_groups=mesh['head'=8,'ga'=8,'gb'=8] {'head','gb'}, dimensions={0} | all-to-all | bytes 16384 | tf_op jit(solution)/shard_map/all_to_all | solution.py:198
  244.2 0.6 broadcast_in_dim.90
  244.8 11.0 %all-to-all-start.8 = ((f32[8,1,32]{2,1,0:T(1,128)}), f32[8,1,32]{2,1,0:T(1,128)S(1)}, u32[]{:S(2)}, u32[]{:S(2)}) async-start(f32[8,1,32]{2,1,0:T(1,128)} %broadcast_in_dim.90), calls=%async_computation.8 | async-start | bytes 8192 | tf_op jit(solution)/shard_map/all_to_all | solution.py:198
  255.8 0.7 multiply_reduce_fusion
  257.3 9.9 %all-to-all-done.8 = f32[8,1,32]{2,1,0:T(1,128)S(1)} async-done(((f32[8,1,32]{2,1,0:T(1,128)}), f32[8,1,32]{2,1,0:T(1,128)S(1)}, u32[]{:S(2)}, u32[]{:S(2)}) %all-to-all-start.8) | async-done | bytes 1056 | tf_op jit(solution)/shard_map/all_to_all | solution.py:198
  267.2 0.5 convert_divide_fusion
  (70 shorter events, 2.2 us)
Async XLA Ops:
  7.2 119.8 %copy-start = (bf16[512,2048]{1,0:T(8,128)(2,1)S(1)}, bf16[512,2048]{1,0:T(8,128)(2,1)}, u32[]{:S(2)}) copy-start(bf16[512,2048]{1,0:T(8,128)(2,1)} %param.18) | copy-start | bytes 6291460
  18.8 13.5 %all-to-all-start = ((f32[8,1,16512]{2,1,0:T(1,128)}), f32[8,1,16512]{2,1,0:T(1,128)S(1)}, u32[]{:S(2)}, u32[]{:S(2)}) async-start(f32[8,1,16512]{2,1,0:T(1,128)} %all_to_all.48), calls=%async_computation | async-start | bytes 1056768 | tf_op jit(solution)/shard_map/all_to_all | solution.py:91
  25.2 100.1 %all-gather.4.cloned.1.call-start = ((), (), s32[]{:S(2)}) async-start(), calls=%async_computation.9 | async-start | bytes 3538944 | tf_op jit(solution)/shard_map/all_gather | solution.py:120
  32.3 60.1 %copy-start.2 = (bf16[128,512]{1,0:T(8,128)(2,1)S(1)}, bf16[128,512]{1,0:T(8,128)(2,1)}, u32[]{:S(2)}) copy-start(bf16[128,512]{1,0:T(8,128)(2,1)} %param.15) | copy-start | bytes 393220
  32.4 60.1 %copy-start.3 = (bf16[128,256]{1,0:T(8,128)(2,1)S(1)}, bf16[128,256]{1,0:T(8,128)(2,1)}, u32[]{:S(2)}) copy-start(bf16[128,256]{1,0:T(8,128)(2,1)} %param.14) | copy-start | bytes 196612
  32.4 60.1 %copy-start.4 = (bf16[128,256]{1,0:T(8,128)(2,1)S(1)}, bf16[128,256]{1,0:T(8,128)(2,1)}, u32[]{:S(2)}) copy-start(bf16[128,256]{1,0:T(8,128)(2,1)} %param.13) | copy-start | bytes 196612
  35.4 27.7 %all-to-all-start.1 = ((f32[8,1,2176]{2,1,0:T(1,128)}), f32[8,1,2176]{2,1,0:T(1,128)S(1)}, u32[]{:S(2)}, u32[]{:S(2)}) async-start(f32[8,1,2176]{2,1,0:T(1,128)} %all_to_all.51), calls=%async_computation.1 | async-start | bytes 139264 | tf_op jit(solution)/shard_map/all_to_all | solution.py:110
  64.4 19.3 %all-to-all-start.2 = ((f32[8,1,2048]{2,1,0:T(1,128)}), f32[8,1,2048]{2,1,0:T(1,128)S(1)}, u32[]{:S(2)}, u32[]{:S(2)}) async-start(f32[8,1,2048]{2,1,0:T(1,128)} %copy.72), calls=%async_computation.2 | async-start | bytes 131072 | tf_op jit(solution)/shard_map/all_to_all | solution.py:114
  85.6 25.5 %all-to-all-start.3 = ((f32[8,1,16384]{2,1,0:T(1,128)}), f32[8,1,16384]{2,1,0:T(1,128)S(1)}, u32[]{:S(2)}, u32[]{:S(2)}) async-start(f32[8,1,16384]{2,1,0:T(1,128)} %copy.73), calls=%async_computation.3 | async-start | bytes 1048576 | tf_op jit(solution)/shard_map/all_to_all | solution.py:116
  125.7 8.1 %copy-start.10 = (s32[1,16]{1,0:T(1,128)S(1)}, s32[1,16]{1,0:T(1,128)}, u32[]{:S(2)}) copy-start(s32[1,16]{1,0:T(1,128)} %param.22) | copy-start | bytes 196
  127.0 23.1 %copy-start.1 = (bf16[1,16,2048]{2,1,0:T(8,128)(2,1)S(1)}, bf16[1,16,2048]{2,1,0:T(8,128)(2,1)}, u32[]{:S(2)}) copy-start(bf16[1,16,2048]{2,1,0:T(8,128)(2,1)} %param.19) | copy-start | bytes 196612
  127.0 23.5 %copy-start.5 = (f32[2048]{0:T(1024)S(1)}, f32[2048]{0:T(1024)}, u32[]{:S(2)}) copy-start(f32[2048]{0:T(1024)} %param.20) | copy-start | bytes 24580
  128.5 20.3 %all-to-all-start.4 = ((f32[8,16,2048]{2,1,0:T(8,128)}), f32[8,16,2048]{2,1,0:T(8,128)}, u32[]{:S(2)}, u32[]{:S(2)}) async-start(f32[8,16,2048]{2,1,0:T(8,128)} %fusion.3), calls=%async_computation.4 | async-start | bytes 2097152 | tf_op jit(solution)/shard_map/all_to_all | solution.py:141
  133.8 69.8 %all-gather.6.cloned.1.call-start = ((), (), s32[]{:S(2)}) async-start(), calls=%async_computation.10 | async-start | bytes 5013504 | tf_op jit(solution)/shard_map/all_gather | solution.py:155
  212.0 19.8 %copy-start.8 = (f32[1,16]{1,0:T(1,128)S(1)}, f32[1,16]{1,0:T(1,128)}, u32[]{:S(2)}) copy-start(f32[1,16]{1,0:T(1,128)} %param.23) | copy-start | bytes 196
  212.0 19.8 %copy-start.9 = (s32[1,16]{1,0:T(1,128)S(1)}, s32[1,16]{1,0:T(1,128)}, u32[]{:S(2)}) copy-start(s32[1,16]{1,0:T(1,128)} %param.24) | copy-start | bytes 196
  212.0 55.2 %copy-start.7 = (s32[32]{0:T(128)S(1)}, s32[32]{0:T(128)}, u32[]{:S(2)}) copy-start(s32[32]{0:T(128)} %param.25) | copy-start | bytes 388
  216.4 15.0 %all-to-all-start.6 = ((f32[64,1,48]{2,1,0:T(1,128)}), f32[64,1,48]{2,1,0:T(1,128)S(1)}, u32[]{:S(2)}, u32[]{:S(2)}) async-start(f32[64,1,48]{2,1,0:T(1,128)} %bitcast.42), calls=%async_computation.6 | async-start | bytes 65536 | tf_op jit(solution)/shard_map/all_to_all | solution.py:180
  231.6 36.1 %copy-start.6 = (f32[16]{0:T(128)}, f32[16]{0:T(128)S(1)}, u32[]{:S(2)}) copy-start(f32[16]{0:T(128)S(1)} %get-tuple-element.12) | copy-start | bytes 196
  244.8 22.4 %all-to-all-start.8 = ((f32[8,1,32]{2,1,0:T(1,128)}), f32[8,1,32]{2,1,0:T(1,128)S(1)}, u32[]{:S(2)}, u32[]{:S(2)}) async-start(f32[8,1,32]{2,1,0:T(1,128)} %broadcast_in_dim.90), calls=%async_computation.8 | async-start | bytes 8192 | tf_op jit(solution)/shard_map/all_to_all | solution.py:198
Sparse Core Ops, SparseCore 0:
  28.0 97.1 all-gather.3
  168.5 35.0 all-gather.5

commit v11 on v10

--- a/solution.py
+++ b/solution.py
@@ -118,7 +118,6 @@
     )
 
     vocab_rows = lax.all_gather(vocab_weight, "ga", axis=0, tiled=True)
-    vocab_rows, carried_state = lax.optimization_barrier((vocab_rows, carried_state))
     query_as_float = query_heads.astype(jnp.float32)
     state_contribution = (
         jnp.einsum("ugo,gow->ugw", query_as_float, carried_state, precision=highest_precision)
@@ -143,6 +142,7 @@
         ),
         axis=0,
     )
+    vocab_rows, own_branch = lax.optimization_barrier((vocab_rows, own_branch))
     stream = residual[0].astype(jnp.float32) + own_branch
     hidden = (layer_norm(stream, 1e-05) * norm_gain).astype(jnp.bfloat16)
 

time: 277 us -> 265 us (0.957)
  waiting for transfers between devices: 134 us -> 121 us
    all_gather x1, waiting for transfers between devices: 12.8 us -> 0.02 us  [per_device(): vocab_rows = lax.all_gather(vocab_weight, 'ga', axis=0, tiled=True)]
  transfers between devices with their start and end apart: 9 -> 9, of which waited for: 9 -> 8; matrix products, arithmetic and copies ran while one was open for 3% -> 5% of each run, Pallas kernels for 0% -> 0%
where the time goes in v11:
time: 265 us
  waiting for transfers between devices  121 us (46%)
  starting transfers between devices  56.8 us (21%)
  blocking collectives  29.1 us (11%)
  between operations  17.7 us (7%)
  other arithmetic  16 us (6%)
  matrix products  13.5 us (5%)
  local copies, waits for them, and re-layouts  10.4 us (4%)
    all_gather x1, waiting for transfers between devices, per_device(): lax.all_gather(lax.all_to_all(spread, 'gb', 0, 0, tiled=True), 'head')  33 us
    all_to_all x1, waiting for transfers between devices, per_device(): lax.all_to_all(slices_out, 'gb', 0, 0, tiled=True)  19.3 us
    all_to_all x1, blocking collectives, per_device(): lax.all_to_all(spread, 'gb', 0, 0, tiled=True)  16.9 us
    all_to_all x1, waiting for transfers between devices, per_device(): octet_in = lax.all_to_all(octet_in, 'ga', 0, 0, tiled=True).reshape(chunk)  15.5 us
    all_to_all x1, waiting for transfers between devices, per_device(): lax.all_to_all(branch_parts.reshape(head_count, slice_rows, -1), 'head',...  14.9 us
    all_to_all x1, starting transfers between devices, per_device(): received = lax.all_to_all(payload, 'ga', 0, 0, tiled=True)  14.5 us
    all_to_all x1, waiting for transfers between devices, per_device(): received = lax.all_to_all(payload, 'ga', 0, 0, tiled=True)  13.1 us
    all_to_all x1, blocking collectives, per_device(): seq_total = jnp.sum(lax.all_to_all(spread, axes, 0, 0, tiled=True), axis=0)  12.2 us
  transfers between devices with their start and end apart: 9, of which 8 were waited for; matrix products, arithmetic and copies ran while one was open for 5% of the time, Pallas kernels for 0%

profile of v11, /device:TPU:1, one launch (start us, length us, event | category | flops | bytes accessed | tf_op | source)
XLA Modules:
  0.0 264.6 jit_solution(4840612814224553165)
XLA Ops:
  7.2 0.9 copy.70
  8.1 0.1 reduce.14
  8.3 0.7 sub.101
  9.2 0.6 fusion.65
  9.8 0.8 copy.71
  10.6 0.2 reduce_window_sum.18
  10.7 0.6 slice.84
  11.3 0.1 reduce.15
  12.2 1.3 fusion.63
  13.5 2.0 select_multiply_fusion
  15.5 1.4 fusion.17
  16.9 0.1 reshape.517
  17.6 1.2 all_to_all.48
  18.8 6.4 %all-to-all-start = ((f32[8,1,16512]{2,1,0:T(1,128)}), f32[8,1,16512]{2,1,0:T(1,128)S(1)}, u32[]{:S(2)}, u32[]{:S(2)}) async-start(f32[8,1,16512]{2,1,0:T(1,128)} %all_to_all.48), calls=%async_computation | async-start | bytes 1056768 | tf_op jit(solution)/shard_map/all_to_all | solution.py:91
  25.2 0.7 all-gather.4.cloned.1.call-update
  25.9 6.4 %all-to-all-done = f32[8,1,16512]{2,1,0:T(1,128)S(1)} async-done(((f32[8,1,16512]{2,1,0:T(1,128)}), f32[8,1,16512]{2,1,0:T(1,128)S(1)}, u32[]{:S(2)}, u32[]{:S(2)}) %all-to-all-start) | async-done | bytes 528416 | tf_op jit(solution)/shard_map/all_to_all | solution.py:91
  32.4 0.7 slice_reduce_fusion.4
  33.1 0.2 select_reduce_fusion.1
  33.4 0.6 fusion.52
  34.0 0.7 pad_select_fusion.1
  34.7 0.7 all_to_all.51
  35.3 14.5 %all-to-all-start.1 = ((f32[8,1,2176]{2,1,0:T(1,128)}), f32[8,1,2176]{2,1,0:T(1,128)S(1)}, u32[]{:S(2)}, u32[]{:S(2)}) async-start(f32[8,1,2176]{2,1,0:T(1,128)} %all_to_all.51), calls=%async_computation.1 | async-start | bytes 139264 | tf_op jit(solution)/shard_map/all_to_all | solution.py:110
  49.9 13.1 %all-to-all-done.1 = f32[8,1,2176]{2,1,0:T(1,128)S(1)} async-done(((f32[8,1,2176]{2,1,0:T(1,128)}), f32[8,1,2176]{2,1,0:T(1,128)S(1)}, u32[]{:S(2)}, u32[]{:S(2)}) %all-to-all-start.1) | async-done | bytes 69664 | tf_op jit(solution)/shard_map/all_to_all | solution.py:110
  63.0 0.1 slice_reduce_fusion.2
  63.1 0.3 fusion.30
  63.5 0.2 convolution_bitcast_fusion
  63.7 0.7 copy.72
  64.3 3.4 %all-to-all-start.2 = ((f32[8,1,2048]{2,1,0:T(1,128)}), f32[8,1,2048]{2,1,0:T(1,128)S(1)}, u32[]{:S(2)}, u32[]{:S(2)}) async-start(f32[8,1,2048]{2,1,0:T(1,128)} %copy.72), calls=%async_computation.2 | async-start | bytes 131072 | tf_op jit(solution)/shard_map/all_to_all | solution.py:114
  67.8 0.1 slice_reduce_fusion.3
  68.0 0.2 reduce-window.18
  68.2 15.5 %all-to-all-done.2 = f32[8,1,2048]{2,1,0:T(1,128)S(1)} async-done(((f32[8,1,2048]{2,1,0:T(1,128)}), f32[8,1,2048]{2,1,0:T(1,128)S(1)}, u32[]{:S(2)}, u32[]{:S(2)}) %all-to-all-start.2) | async-done | bytes 65568 | tf_op jit(solution)/shard_map/all_to_all | solution.py:114
  83.6 0.6 fusion
  84.2 1.3 copy.73
  85.5 8.3 %all-to-all-start.3 = ((f32[8,1,16384]{2,1,0:T(1,128)}), f32[8,1,16384]{2,1,0:T(1,128)S(1)}, u32[]{:S(2)}, u32[]{:S(2)}) async-start(f32[8,1,16384]{2,1,0:T(1,128)} %copy.73), calls=%async_computation.3 | async-start | bytes 1048576 | tf_op jit(solution)/shard_map/all_to_all | solution.py:116
  93.8 0.4 convolution_bitcast_fusion.2
  94.2 19.3 %all-to-all-done.3 = f32[8,1,16384]{2,1,0:T(1,128)S(1)} async-done(((f32[8,1,16384]{2,1,0:T(1,128)}), f32[8,1,16384]{2,1,0:T(1,128)S(1)}, u32[]{:S(2)}, u32[]{:S(2)}) %all-to-all-start.3) | async-done | bytes 524320 | tf_op jit(solution)/shard_map/all_to_all | solution.py:116
  113.5 2.8 %multiply_reduce_fusion = (f32[]{:T(128)}, f32[8,16384]{1,0:T(8,128)S(1)}) fusion(f32[8,1,16384]{2,1,0:T(1,128)S(1)} %all-to-all-done.3), kind=kLoop, calls=%fused_computation.20 | loop fusion | flops 262143 | bytes 1048580 | tf_op jit(solution)/shard_map/reduce_sum | solution.py:129
  116.3 0.1 reshape.520
  116.4 0.4 fusion.66
  116.9 0.2 multiply_reduce_fusion.1
  117.1 1.1 fusion.16
  118.1 1.4 fusion.3
  119.6 5.9 %all-to-all-start.4 = ((f32[8,16,2048]{2,1,0:T(8,128)}), f32[8,16,2048]{2,1,0:T(8,128)S(1)}, u32[]{:S(2)}, u32[]{:S(2)}) async-start(f32[8,16,2048]{2,1,0:T(8,128)} %fusion.3), calls=%async_computation.4 | async-start | bytes 2097152 | tf_op jit(solution)/shard_map/all_to_all | solution.py:140
  125.6 14.9 %all-to-all-done.4 = f32[8,16,2048]{2,1,0:T(8,128)S(1)} async-done(((f32[8,16,2048]{2,1,0:T(8,128)}), f32[8,16,2048]{2,1,0:T(8,128)S(1)}, u32[]{:S(2)}, u32[]{:S(2)}) %all-to-all-start.4) | async-done | bytes 1048608 | tf_op jit(solution)/shard_map/all_to_all | solution.py:140
  140.5 0.1 fusion.29
  140.7 0.2 multiply_reduce_fusion.2
  140.9 0.1 multiply_convert_fusion
  141.1 16.9 %all_to_all.73 = bf16[8,17,2048]{2,1,0:T(8,128)(2,1)S(1)} all-to-all(bf16[8,17,2048]{2,1,0:T(8,128)(2,1)S(1)} %broadcast_in_dim.87), channel_id=1, replica_groups=mesh['head'=8,'ga'=8,'gb'=8] {'gb'}, dimensions={0} | all-to-all | bytes 1114112 | tf_op jit(solution)/shard_map/all_to_all | solution.py:155
  158.0 1.1 copy.74
  159.4 33.0 %all-gather.6.cloned.1.call-done = bf16[64,17,2048]{2,0,1:T(8,128)(2,1)} async-done(((bf16[8,17,2048]{2,0,1:T(8,128)(2,1)}), bf16[64,17,2048]{2,0,1:T(8,128)(2,1)}) %all-gather.6.cloned.1.call-update) | async-done | bytes 4456464 | tf_op jit(solution)/shard_map/all_gather | solution.py:155
  192.4 0.7 fusion.39
  193.3 8.5 %fusion.67 = (f32[64,16]{0,1:T(8,128)S(1)}, f32[64,16,768]{2,0,1:T(8,128)}) fusion(bf16[64,17,2048]{2,0,1:T(8,128)(2,1)} %all-gather.6.cloned.1.call-done, bf16[768,2048]{1,0:T(8,128)(2,1)} %all-gather.4.cloned.1.call-done), kind=kOutput, calls=%fused_computation.137 | convolution fusion | flops 3222010880 | bytes 10752000 | tf_op jit(solution)/shard_map/slice | solution.py:167
  201.8 2.4 exponential_reduce_fusion
  204.6 0.7 all_to_all.60
  205.3 7.2 %all-to-all-start.6 = ((f32[64,1,48]{2,1,0:T(1,128)}), f32[64,1,48]{2,1,0:T(1,128)S(1)}, u32[]{:S(2)}, u32[]{:S(2)}) async-start(f32[64,1,48]{2,1,0:T(1,128)} %bitcast.41), calls=%async_computation.6 | async-start | bytes 65536 | tf_op jit(solution)/shard_map/all_to_all | solution.py:180
  212.5 0.2 convert_reduce_fusion.1
  212.7 7.6 %all-to-all-done.6 = f32[64,1,48]{2,1,0:T(1,128)S(1)} async-done(((f32[64,1,48]{2,1,0:T(1,128)}), f32[64,1,48]{2,1,0:T(1,128)S(1)}, u32[]{:S(2)}, u32[]{:S(2)}) %all-to-all-start.6) | async-done | bytes 12320 | tf_op jit(solution)/shard_map/all_to_all | solution.py:180
  220.4 0.1 slice_reduce_fusion
  220.5 0.2 fusion.41
  220.8 12.2 %all_to_all.74 = f32[64,1,32]{2,1,0:T(1,128)S(1)} all-to-all(f32[64,1,32]{2,1,0:T(1,128)S(1)} %broadcast_in_dim.89), channel_id=1, replica_groups=mesh['head'=8,'ga'=8,'gb'=8] {'head','gb'}, dimensions={0} | all-to-all | bytes 16384 | tf_op jit(solution)/shard_map/all_to_all | solution.py:198
  233.1 0.6 broadcast_in_dim.90
  233.7 11.0 %all-to-all-start.8 = ((f32[8,1,32]{2,1,0:T(1,128)}), f32[8,1,32]{2,1,0:T(1,128)S(1)}, u32[]{:S(2)}, u32[]{:S(2)}) async-start(f32[8,1,32]{2,1,0:T(1,128)} %broadcast_in_dim.90), calls=%async_computation.8 | async-start | bytes 8192 | tf_op jit(solution)/shard_map/all_to_all | solution.py:198
  245.4 10.6 %all-to-all-done.8 = f32[8,1,32]{2,1,0:T(1,128)S(1)} async-done(((f32[8,1,32]{2,1,0:T(1,128)}), f32[8,1,32]{2,1,0:T(1,128)S(1)}, u32[]{:S(2)}, u32[]{:S(2)}) %all-to-all-start.8) | async-done | bytes 1056 | tf_op jit(solution)/shard_map/all_to_all | solution.py:198
  256.1 0.5 convert_divide_fusion
  (69 shorter events, 2.0 us)
Async XLA Ops:
  7.2 111.0 %copy-start = (bf16[512,2048]{1,0:T(8,128)(2,1)S(1)}, bf16[512,2048]{1,0:T(8,128)(2,1)}, u32[]{:S(2)}) copy-start(bf16[512,2048]{1,0:T(8,128)(2,1)} %param.18) | copy-start | bytes 6291460
  18.8 13.5 %all-to-all-start = ((f32[8,1,16512]{2,1,0:T(1,128)}), f32[8,1,16512]{2,1,0:T(1,128)S(1)}, u32[]{:S(2)}, u32[]{:S(2)}) async-start(f32[8,1,16512]{2,1,0:T(1,128)} %all_to_all.48), calls=%async_computation | async-start | bytes 1056768 | tf_op jit(solution)/shard_map/all_to_all | solution.py:91
  25.1 115.4 %all-gather.4.cloned.1.call-start = ((), (), s32[]{:S(2)}) async-start(), calls=%async_computation.9 | async-start | bytes 3538944 | tf_op jit(solution)/shard_map/all_gather | solution.py:120
  32.3 61.5 %copy-start.2 = (bf16[128,512]{1,0:T(8,128)(2,1)S(1)}, bf16[128,512]{1,0:T(8,128)(2,1)}, u32[]{:S(2)}) copy-start(bf16[128,512]{1,0:T(8,128)(2,1)} %param.15) | copy-start | bytes 393220
  32.3 61.5 %copy-start.3 = (bf16[128,256]{1,0:T(8,128)(2,1)S(1)}, bf16[128,256]{1,0:T(8,128)(2,1)}, u32[]{:S(2)}) copy-start(bf16[128,256]{1,0:T(8,128)(2,1)} %param.14) | copy-start | bytes 196612
  32.4 61.5 %copy-start.4 = (bf16[128,256]{1,0:T(8,128)(2,1)S(1)}, bf16[128,256]{1,0:T(8,128)(2,1)}, u32[]{:S(2)}) copy-start(bf16[128,256]{1,0:T(8,128)(2,1)} %param.13) | copy-start | bytes 196612
  35.3 27.6 %all-to-all-start.1 = ((f32[8,1,2176]{2,1,0:T(1,128)}), f32[8,1,2176]{2,1,0:T(1,128)S(1)}, u32[]{:S(2)}, u32[]{:S(2)}) async-start(f32[8,1,2176]{2,1,0:T(1,128)} %all_to_all.51), calls=%async_computation.1 | async-start | bytes 139264 | tf_op jit(solution)/shard_map/all_to_all | solution.py:110
  64.3 19.3 %all-to-all-start.2 = ((f32[8,1,2048]{2,1,0:T(1,128)}), f32[8,1,2048]{2,1,0:T(1,128)S(1)}, u32[]{:S(2)}, u32[]{:S(2)}) async-start(f32[8,1,2048]{2,1,0:T(1,128)} %copy.72), calls=%async_computation.2 | async-start | bytes 131072 | tf_op jit(solution)/shard_map/all_to_all | solution.py:114
  85.5 28.0 %all-to-all-start.3 = ((f32[8,1,16384]{2,1,0:T(1,128)}), f32[8,1,16384]{2,1,0:T(1,128)S(1)}, u32[]{:S(2)}, u32[]{:S(2)}) async-start(f32[8,1,16384]{2,1,0:T(1,128)} %copy.73), calls=%async_computation.3 | async-start | bytes 1048576 | tf_op jit(solution)/shard_map/all_to_all | solution.py:116
  116.8 8.6 %copy-start.10 = (s32[1,16]{1,0:T(1,128)S(1)}, s32[1,16]{1,0:T(1,128)}, u32[]{:S(2)}) copy-start(s32[1,16]{1,0:T(1,128)} %param.22) | copy-start | bytes 196
  118.1 22.4 %copy-start.1 = (bf16[1,16,2048]{2,1,0:T(8,128)(2,1)S(1)}, bf16[1,16,2048]{2,1,0:T(8,128)(2,1)}, u32[]{:S(2)}) copy-start(bf16[1,16,2048]{2,1,0:T(8,128)(2,1)} %param.19) | copy-start | bytes 196612
  118.1 22.8 %copy-start.5 = (f32[2048]{0:T(1024)S(1)}, f32[2048]{0:T(1024)}, u32[]{:S(2)}) copy-start(f32[2048]{0:T(1024)} %param.20) | copy-start | bytes 24580
  119.6 20.8 %all-to-all-start.4 = ((f32[8,16,2048]{2,1,0:T(8,128)}), f32[8,16,2048]{2,1,0:T(8,128)S(1)}, u32[]{:S(2)}, u32[]{:S(2)}) async-start(f32[8,16,2048]{2,1,0:T(8,128)} %fusion.3), calls=%async_computation.4 | async-start | bytes 2097152 | tf_op jit(solution)/shard_map/all_to_all | solution.py:140
  125.5 66.9 %all-gather.6.cloned.1.call-start = ((), (), s32[]{:S(2)}) async-start(), calls=%async_computation.10 | async-start | bytes 5013504 | tf_op jit(solution)/shard_map/all_gather | solution.py:155
  201.7 19.0 %copy-start.8 = (f32[1,16]{1,0:T(1,128)S(1)}, f32[1,16]{1,0:T(1,128)}, u32[]{:S(2)}) copy-start(f32[1,16]{1,0:T(1,128)} %param.23) | copy-start | bytes 196
  201.7 19.0 %copy-start.9 = (s32[1,16]{1,0:T(1,128)S(1)}, s32[1,16]{1,0:T(1,128)}, u32[]{:S(2)}) copy-start(s32[1,16]{1,0:T(1,128)} %param.24) | copy-start | bytes 196
  201.7 54.3 %copy-start.7 = (s32[32]{0:T(128)S(1)}, s32[32]{0:T(128)}, u32[]{:S(2)}) copy-start(s32[32]{0:T(128)} %param.25) | copy-start | bytes 388
  205.3 15.0 %all-to-all-start.6 = ((f32[64,1,48]{2,1,0:T(1,128)}), f32[64,1,48]{2,1,0:T(1,128)S(1)}, u32[]{:S(2)}, u32[]{:S(2)}) async-start(f32[64,1,48]{2,1,0:T(1,128)} %bitcast.41), calls=%async_computation.6 | async-start | bytes 65536 | tf_op jit(solution)/shard_map/all_to_all | solution.py:180
  220.5 36.1 %copy-start.6 = (f32[16]{0:T(128)}, f32[16]{0:T(128)S(1)}, u32[]{:S(2)}) copy-start(f32[16]{0:T(128)S(1)} %get-tuple-element.14) | copy-start | bytes 196
  233.7 22.4 %all-to-all-start.8 = ((f32[8,1,32]{2,1,0:T(1,128)}), f32[8,1,32]{2,1,0:T(1,128)S(1)}, u32[]{:S(2)}, u32[]{:S(2)}) async-start(f32[8,1,32]{2,1,0:T(1,128)} %broadcast_in_dim.90), calls=%async_computation.8 | async-start | bytes 8192 | tf_op jit(solution)/shard_map/all_to_all | solution.py:198
Sparse Core Ops, SparseCore 0:
  28.0 96.6 all-gather.3
  159.3 33.0 all-gather.5

commit v12 on v11

--- a/solution.py
+++ b/solution.py
@@ -98,20 +98,16 @@
     octet_total = jnp.dot(tail_weights, slices_in, precision=highest_precision)
     octet_decay = jnp.prod(decay_in)
     lead_decay = jnp.cumprod(jnp.concatenate([jnp.ones((1,), jnp.float32), decay_in[:-1]]))
-    piece = chunk // part_count
     extras = jnp.concatenate([octet_decay[None], pad])
-    payload = jnp.concatenate(
-        [
-            octet_total.reshape(part_count, piece),
-            jnp.broadcast_to(extras[None, :], (part_count, 128)),
-        ],
-        axis=1,
-    )
-    received = lax.all_to_all(payload, "ga", 0, 0, tiled=True)
+    payload = jnp.concatenate([octet_total, extras])
+    received = lax.all_to_all(
+        jnp.broadcast_to(payload[None, :], (part_count,) + payload.shape), "ga", 0, 0, tiled=True
+    )
     octet_in = jnp.dot(
-        decay_weights(received[:, piece]), received[:, :piece], precision=highest_precision
-    )
-    octet_in = lax.all_to_all(octet_in, "ga", 0, 0, tiled=True).reshape(chunk)
+        decay_weights(received[:, chunk])[lax.axis_index("ga")],
+        received[:, :chunk],
+        precision=highest_precision,
+    )
     slices_out = local_in + lead_decay[:, None] * octet_in[None, :]
     carried_state = lax.all_to_all(slices_out, "gb", 0, 0, tiled=True).reshape(
         heads_here, key_width, value_width

time: 265 us -> 273 us (1.030)
  starting transfers between devices: 56.8 us -> 63.1 us
  blocking collectives: 29.1 us -> 25.5 us
  waiting for transfers between devices: 121 us -> 124 us
    all_to_all x1, starting transfers between devices: 8.27 us -> 18.6 us  [per_device(): lax.all_to_all(slices_out, 'gb', 0, 0, tiled=True)]
    all_to_all x2 -> x1, waiting for transfers between devices: 28.6 us -> 19.2 us  [per_device(): lax.all_to_all(jnp.broadcast_to(payload[None, :], (part_count,) + payload...]
    all_gather x1, waiting for transfers between devices: 0.02 us -> 9.14 us  [per_device(): vocab_rows = lax.all_gather(vocab_weight, 'ga', axis=0, tiled=True)]
    all_gather x1, waiting for transfers between devices: 33 us -> 36.9 us  [per_device(): lax.all_gather(lax.all_to_all(spread, 'gb', 0, 0, tiled=True), 'head')]
    all_to_all x1, blocking collectives: 16.9 us -> 13.4 us  [per_device(): lax.all_to_all(spread, 'gb', 0, 0, tiled=True)]
    all_to_all x2 -> x1, starting transfers between devices: 18 us -> 14.6 us  [per_device(): lax.all_to_all(jnp.broadcast_to(payload[None, :], (part_count,) + payload...]
  transfers between devices with their start and end apart: 9 -> 8, of which waited for: 8 -> 8; matrix products, arithmetic and copies ran while one was open for 5% -> 4% of each run, Pallas kernels for 0% -> 0%
where the time goes in v12:
time: 273 us; the launch traced here: 272 us
  waiting for transfers between devices  124 us (45%)
  starting transfers between devices  63.1 us (23%)
  blocking collectives  25.5 us (9%)
  between operations  17.6 us (6%)
  matrix products  15.6 us (6%)
  other arithmetic  15.4 us (6%)
  local copies, waits for them, and re-layouts  10.8 us (4%)
    all_gather x1, waiting for transfers between devices, per_device(): lax.all_gather(lax.all_to_all(spread, 'gb', 0, 0, tiled=True), 'head')  36.9 us
    all_to_all x1, waiting for transfers between devices, per_device(): lax.all_to_all(jnp.broadcast_to(payload[None, :], (part_count,) + payload...  19.2 us
    all_to_all x1, starting transfers between devices, per_device(): lax.all_to_all(slices_out, 'gb', 0, 0, tiled=True)  18.6 us
    all_to_all x1, waiting for transfers between devices, per_device(): lax.all_to_all(slices_out, 'gb', 0, 0, tiled=True)  17.6 us
    all_to_all x1, waiting for transfers between devices, per_device(): lax.all_to_all(branch_parts.reshape(head_count, slice_rows, -1), 'head',...  14.9 us
    all_to_all x1, starting transfers between devices, per_device(): lax.all_to_all(jnp.broadcast_to(payload[None, :], (part_count,) + payload...  14.6 us
    all_to_all x1, blocking collectives, per_device(): lax.all_to_all(spread, 'gb', 0, 0, tiled=True)  13.4 us
    all_to_all x1, blocking collectives, per_device(): seq_total = jnp.sum(lax.all_to_all(spread, axes, 0, 0, tiled=True), axis=0)  12.2 us
  transfers between devices with their start and end apart: 8, of which 8 were waited for; matrix products, arithmetic and copies ran while one was open for 4% of the time, Pallas kernels for 0%

profile of v12, /device:TPU:1, one launch (start us, length us, event | category | flops | bytes accessed | tf_op | source)
XLA Modules:
  0.0 271.8 jit_solution(18056018524151156496)
XLA Ops:
  7.2 0.9 copy.67
  8.1 0.1 reduce.14
  8.3 0.7 sub.101
  9.0 0.1 compare_reduce_fusion
  9.1 0.1 convert_reduce_fusion
  9.2 0.6 fusion.68
  9.8 0.8 copy.68
  10.6 0.2 reduce_window_sum.18
  10.7 0.6 slice.84
  11.3 0.1 reduce.15
  12.2 1.3 fusion.67
  13.5 2.0 select_multiply_fusion
  15.5 1.4 fusion.22
  16.9 0.1 reshape.515
  17.6 1.2 all_to_all.40
  18.8 6.4 %all-to-all-start = ((f32[8,1,16512]{2,1,0:T(1,128)}), f32[8,1,16512]{2,1,0:T(1,128)S(1)}, u32[]{:S(2)}, u32[]{:S(2)}) async-start(f32[8,1,16512]{2,1,0:T(1,128)} %all_to_all.40), calls=%async_computation | async-start | bytes 1056768 | tf_op jit(solution)/shard_map/all_to_all | solution.py:91
  25.2 7.1 %all-to-all-done = f32[8,1,16512]{2,1,0:T(1,128)S(1)} async-done(((f32[8,1,16512]{2,1,0:T(1,128)}), f32[8,1,16512]{2,1,0:T(1,128)S(1)}, u32[]{:S(2)}, u32[]{:S(2)}) %all-to-all-start) | async-done | bytes 528416 | tf_op jit(solution)/shard_map/all_to_all | solution.py:91
  32.3 0.7 slice_reduce_fusion.4
  33.1 0.2 select_reduce_fusion.1
  33.3 0.6 fusion.13
  33.9 0.7 concatenate.27
  34.6 1.1 broadcast_in_dim.85
  35.7 14.6 %all-to-all-start.1 = ((f32[8,1,16512]{2,1,0:T(1,128)}), f32[8,1,16512]{2,1,0:T(1,128)S(1)}, u32[]{:S(2)}, u32[]{:S(2)}) async-start(f32[8,1,16512]{2,1,0:T(1,128)} %broadcast_in_dim.85), calls=%async_computation.1 | async-start | bytes 1056768 | tf_op jit(solution)/shard_map/all_to_all | solution.py:103
  50.4 0.7 all-gather.4.cloned.1.call-update
  51.1 0.1 slice_reduce_fusion.3
  51.3 0.2 reduce-window.18
  51.5 19.2 %all-to-all-done.1 = f32[8,1,16512]{2,1,0:T(1,128)S(1)} async-done(((f32[8,1,16512]{2,1,0:T(1,128)}), f32[8,1,16512]{2,1,0:T(1,128)S(1)}, u32[]{:S(2)}, u32[]{:S(2)}) %all-to-all-start.1) | async-done | bytes 528416 | tf_op jit(solution)/shard_map/all_to_all | solution.py:103
  70.7 0.1 slice_reduce_fusion.2
  70.8 0.3 fusion.34
  71.2 0.6 fusion.11
  71.7 0.6 fusion
  72.3 1.3 copy.69
  73.6 18.6 %all-to-all-start.2 = ((f32[8,1,16384]{2,1,0:T(1,128)}), f32[8,1,16384]{2,1,0:T(1,128)S(1)}, u32[]{:S(2)}, u32[]{:S(2)}) async-start(f32[8,1,16384]{2,1,0:T(1,128)} %copy.69), calls=%async_computation.2 | async-start | bytes 1048576 | tf_op jit(solution)/shard_map/all_to_all | solution.py:112
  92.3 1.3 convolution_bitcast_fusion.1
  93.6 17.6 %all-to-all-done.2 = f32[8,1,16384]{2,1,0:T(1,128)S(1)} async-done(((f32[8,1,16384]{2,1,0:T(1,128)}), f32[8,1,16384]{2,1,0:T(1,128)S(1)}, u32[]{:S(2)}, u32[]{:S(2)}) %all-to-all-start.2) | async-done | bytes 524320 | tf_op jit(solution)/shard_map/all_to_all | solution.py:112
  111.2 2.8 %multiply_reduce_fusion = (f32[]{:T(128)}, f32[8,16384]{1,0:T(8,128)S(1)}) fusion(f32[8,1,16384]{2,1,0:T(1,128)S(1)} %all-to-all-done.2), kind=kLoop, calls=%fused_computation.22 | loop fusion | flops 262143 | bytes 1048580 | tf_op jit(solution)/shard_map/reduce_sum | solution.py:125
  113.9 0.1 reshape.518
  114.0 1.3 fusion.69
  115.3 0.2 multiply_reduce_fusion.1
  115.5 1.1 fusion.21
  116.6 1.4 fusion.3
  118.1 5.2 %all-to-all-start.3 = ((f32[8,16,2048]{2,1,0:T(8,128)}), f32[8,16,2048]{2,1,0:T(8,128)S(1)}, u32[]{:S(2)}, u32[]{:S(2)}) async-start(f32[8,16,2048]{2,1,0:T(8,128)} %fusion.3), calls=%async_computation.3 | async-start | bytes 2097152 | tf_op jit(solution)/shard_map/all_to_all | solution.py:136
  123.4 14.9 %all-to-all-done.3 = f32[8,16,2048]{2,1,0:T(8,128)S(1)} async-done(((f32[8,16,2048]{2,1,0:T(8,128)}), f32[8,16,2048]{2,1,0:T(8,128)S(1)}, u32[]{:S(2)}, u32[]{:S(2)}) %all-to-all-start.3) | async-done | bytes 1048608 | tf_op jit(solution)/shard_map/all_to_all | solution.py:136
  138.3 9.1 %all-gather.4.cloned.1.call-done = bf16[768,2048]{1,0:T(8,128)(2,1)} async-done(((bf16[96,2048]{1,0:T(8,128)(2,1)}), bf16[768,2048]{1,0:T(8,128)(2,1)}) %all-gather.4.cloned.1.call-update) | async-done | bytes 3145744 | tf_op jit(solution)/shard_map/all_gather | solution.py:116
  147.4 0.1 fusion.33
  147.6 0.2 multiply_reduce_fusion.2
  147.8 0.1 multiply_convert_fusion
  148.0 13.4 %all_to_all.61 = bf16[8,17,2048]{2,1,0:T(8,128)(2,1)S(1)} all-to-all(bf16[8,17,2048]{2,1,0:T(8,128)(2,1)S(1)} %broadcast_in_dim.90), channel_id=1, replica_groups=mesh['head'=8,'ga'=8,'gb'=8] {'gb'}, dimensions={0} | all-to-all | bytes 1114112 | tf_op jit(solution)/shard_map/all_to_all | solution.py:151
  161.4 1.1 copy.70
  162.8 36.9 %all-gather.6.cloned.1.call-done = bf16[64,17,2048]{2,0,1:T(8,128)(2,1)} async-done(((bf16[8,17,2048]{2,0,1:T(8,128)(2,1)}), bf16[64,17,2048]{2,0,1:T(8,128)(2,1)}) %all-gather.6.cloned.1.call-update) | async-done | bytes 4456464 | tf_op jit(solution)/shard_map/all_gather | solution.py:151
  199.7 0.7 fusion.43
  200.5 8.5 %fusion.70 = (f32[64,16]{0,1:T(8,128)S(1)}, f32[64,16,768]{2,0,1:T(8,128)}) fusion(bf16[64,17,2048]{2,0,1:T(8,128)(2,1)} %all-gather.6.cloned.1.call-done, bf16[768,2048]{1,0:T(8,128)(2,1)} %all-gather.4.cloned.1.call-done), kind=kOutput, calls=%fused_computation.135 | convolution fusion | flops 3222010880 | bytes 10752000 | tf_op jit(solution)/shard_map/slice | solution.py:163
  209.1 2.4 exponential_reduce_fusion
  211.8 0.7 all_to_all.49
  212.5 7.2 %all-to-all-start.5 = ((f32[64,1,48]{2,1,0:T(1,128)}), f32[64,1,48]{2,1,0:T(1,128)S(1)}, u32[]{:S(2)}, u32[]{:S(2)}) async-start(f32[64,1,48]{2,1,0:T(1,128)} %bitcast.40), calls=%async_computation.5 | async-start | bytes 65536 | tf_op jit(solution)/shard_map/all_to_all | solution.py:176
  219.8 0.2 convert_reduce_fusion.1
  220.0 7.6 %all-to-all-done.5 = f32[64,1,48]{2,1,0:T(1,128)S(1)} async-done(((f32[64,1,48]{2,1,0:T(1,128)}), f32[64,1,48]{2,1,0:T(1,128)S(1)}, u32[]{:S(2)}, u32[]{:S(2)}) %all-to-all-start.5) | async-done | bytes 12320 | tf_op jit(solution)/shard_map/all_to_all | solution.py:176
  227.6 0.1 slice_reduce_fusion
  227.8 0.2 fusion.45
  228.1 12.2 %all_to_all.62 = f32[64,1,32]{2,1,0:T(1,128)S(1)} all-to-all(f32[64,1,32]{2,1,0:T(1,128)S(1)} %broadcast_in_dim.92), channel_id=1, replica_groups=mesh['head'=8,'ga'=8,'gb'=8] {'head','gb'}, dimensions={0} | all-to-all | bytes 16384 | tf_op jit(solution)/shard_map/all_to_all | solution.py:194
  240.3 0.6 broadcast_in_dim.93
  240.9 11.0 %all-to-all-start.7 = ((f32[8,1,32]{2,1,0:T(1,128)}), f32[8,1,32]{2,1,0:T(1,128)S(1)}, u32[]{:S(2)}, u32[]{:S(2)}) async-start(f32[8,1,32]{2,1,0:T(1,128)} %broadcast_in_dim.93), calls=%async_computation.7 | async-start | bytes 8192 | tf_op jit(solution)/shard_map/all_to_all | solution.py:194
  252.7 10.6 %all-to-all-done.7 = f32[8,1,32]{2,1,0:T(1,128)S(1)} async-done(((f32[8,1,32]{2,1,0:T(1,128)}), f32[8,1,32]{2,1,0:T(1,128)S(1)}, u32[]{:S(2)}, u32[]{:S(2)}) %all-to-all-start.7) | async-done | bytes 1056 | tf_op jit(solution)/shard_map/all_to_all | solution.py:194
  263.3 0.5 convert_divide_fusion
  (65 shorter events, 1.7 us)
Async XLA Ops:
  7.2 109.4 %copy-start = (bf16[512,2048]{1,0:T(8,128)(2,1)S(1)}, bf16[512,2048]{1,0:T(8,128)(2,1)}, u32[]{:S(2)}) copy-start(bf16[512,2048]{1,0:T(8,128)(2,1)} %param.18) | copy-start | bytes 6291460
  7.2 3.5 %copy-start.9 = (s32[128]{0:T(128)}, s32[128]{0:T(128)S(1)}, u32[]{:S(2)}) copy-start(s32[128]{0:T(128)S(1)} %iota_add_fusion.2) | copy-start | bytes 1540
  18.8 13.5 %all-to-all-start = ((f32[8,1,16512]{2,1,0:T(1,128)}), f32[8,1,16512]{2,1,0:T(1,128)S(1)}, u32[]{:S(2)}, u32[]{:S(2)}) async-start(f32[8,1,16512]{2,1,0:T(1,128)} %all_to_all.40), calls=%async_computation | async-start | bytes 1056768 | tf_op jit(solution)/shard_map/all_to_all | solution.py:91
  35.7 56.6 %copy-start.2 = (bf16[128,512]{1,0:T(8,128)(2,1)S(1)}, bf16[128,512]{1,0:T(8,128)(2,1)}, u32[]{:S(2)}) copy-start(bf16[128,512]{1,0:T(8,128)(2,1)} %param.15) | copy-start | bytes 393220
  35.7 34.9 %all-to-all-start.1 = ((f32[8,1,16512]{2,1,0:T(1,128)}), f32[8,1,16512]{2,1,0:T(1,128)S(1)}, u32[]{:S(2)}, u32[]{:S(2)}) async-start(f32[8,1,16512]{2,1,0:T(1,128)} %broadcast_in_dim.85), calls=%async_computation.1 | async-start | bytes 1056768 | tf_op jit(solution)/shard_map/all_to_all | solution.py:103
  50.4 97.1 %all-gather.4.cloned.1.call-start = ((), (), s32[]{:S(2)}) async-start(), calls=%async_computation.8 | async-start | bytes 3538944 | tf_op jit(solution)/shard_map/all_gather | solution.py:116
  73.6 37.5 %all-to-all-start.2 = ((f32[8,1,16384]{2,1,0:T(1,128)}), f32[8,1,16384]{2,1,0:T(1,128)S(1)}, u32[]{:S(2)}, u32[]{:S(2)}) async-start(f32[8,1,16384]{2,1,0:T(1,128)} %copy.69), calls=%async_computation.2 | async-start | bytes 1048576 | tf_op jit(solution)/shard_map/all_to_all | solution.py:112
  115.3 7.9 %copy-start.8 = (s32[1,16]{1,0:T(1,128)S(1)}, s32[1,16]{1,0:T(1,128)}, u32[]{:S(2)}) copy-start(s32[1,16]{1,0:T(1,128)} %param.22) | copy-start | bytes 196
  116.6 30.9 %copy-start.1 = (bf16[1,16,2048]{2,1,0:T(8,128)(2,1)S(1)}, bf16[1,16,2048]{2,1,0:T(8,128)(2,1)}, u32[]{:S(2)}) copy-start(bf16[1,16,2048]{2,1,0:T(8,128)(2,1)} %param.19) | copy-start | bytes 196612
  116.6 31.2 %copy-start.3 = (f32[2048]{0:T(1024)S(1)}, f32[2048]{0:T(1024)}, u32[]{:S(2)}) copy-start(f32[2048]{0:T(1024)} %param.20) | copy-start | bytes 24580
  118.1 20.2 %all-to-all-start.3 = ((f32[8,16,2048]{2,1,0:T(8,128)}), f32[8,16,2048]{2,1,0:T(8,128)S(1)}, u32[]{:S(2)}, u32[]{:S(2)}) async-start(f32[8,16,2048]{2,1,0:T(8,128)} %fusion.3), calls=%async_computation.3 | async-start | bytes 2097152 | tf_op jit(solution)/shard_map/all_to_all | solution.py:136
  123.2 76.4 %all-gather.6.cloned.1.call-start = ((), (), s32[]{:S(2)}) async-start(), calls=%async_computation.9 | async-start | bytes 5013504 | tf_op jit(solution)/shard_map/all_gather | solution.py:151
  123.3 39.4 %copy-start.10 = (s32[128]{0:T(128)S(1)}, s32[128]{0:T(128)}, u32[]{:S(2)}) copy-start(s32[128]{0:T(128)} %copy-done.9) | copy-start | bytes 1540
  209.0 18.9 %copy-start.6 = (f32[1,16]{1,0:T(1,128)S(1)}, f32[1,16]{1,0:T(1,128)}, u32[]{:S(2)}) copy-start(f32[1,16]{1,0:T(1,128)} %param.23) | copy-start | bytes 196
  209.0 19.0 %copy-start.7 = (s32[1,16]{1,0:T(1,128)S(1)}, s32[1,16]{1,0:T(1,128)}, u32[]{:S(2)}) copy-start(s32[1,16]{1,0:T(1,128)} %param.24) | copy-start | bytes 196
  209.0 54.3 %copy-start.5 = (s32[32]{0:T(128)S(1)}, s32[32]{0:T(128)}, u32[]{:S(2)}) copy-start(s32[32]{0:T(128)} %param.25) | copy-start | bytes 388
  212.5 15.0 %all-to-all-start.5 = ((f32[64,1,48]{2,1,0:T(1,128)}), f32[64,1,48]{2,1,0:T(1,128)S(1)}, u32[]{:S(2)}, u32[]{:S(2)}) async-start(f32[64,1,48]{2,1,0:T(1,128)} %bitcast.40), calls=%async_computation.5 | async-start | bytes 65536 | tf_op jit(solution)/shard_map/all_to_all | solution.py:176
  227.8 36.1 %copy-start.4 = (f32[16]{0:T(128)}, f32[16]{0:T(128)S(1)}, u32[]{:S(2)}) copy-start(f32[16]{0:T(128)S(1)} %get-tuple-element.14) | copy-start | bytes 196
  240.9 22.4 %all-to-all-start.7 = ((f32[8,1,32]{2,1,0:T(1,128)}), f32[8,1,32]{2,1,0:T(1,128)S(1)}, u32[]{:S(2)}, u32[]{:S(2)}) async-start(f32[8,1,32]{2,1,0:T(1,128)} %broadcast_in_dim.93), calls=%async_computation.7 | async-start | bytes 8192 | tf_op jit(solution)/shard_map/all_to_all | solution.py:194
Sparse Core Ops, SparseCore 0:
  53.2 94.1 all-gather.3
  162.7 36.9 all-gather.5

commit v13 on v11

--- a/solution.py
+++ b/solution.py
@@ -192,7 +192,7 @@
     )
     partial_sums = jnp.sum(member * token_ratio[:, None], axis=0)
     seq_total = partial_sums
-    for axes in (("head", "gb"), "ga"):
+    for axes in ("head", ("ga", "gb")):
         width = lax.axis_size(axes)
         spread = jnp.broadcast_to(seq_total[None, :], (width, seq_count))
         seq_total = jnp.sum(lax.all_to_all(spread, axes, 0, 0, tiled=True), axis=0)

time: 265 us -> 265 us (level)
  blocking collectives: 29.1 us -> 24.7 us
    all_to_all x1, blocking collectives: 12.2 us -> 7.78 us  [per_device(): seq_total = jnp.sum(lax.all_to_all(spread, axes, 0, 0, tiled=True), axis=0)]
where the time goes in v13:
time: 265 us; the launch traced here: 264 us
  waiting for transfers between devices  123 us (46%)
  starting transfers between devices  58.4 us (22%)
  blocking collectives  24.7 us (9%)
  between operations  17.7 us (7%)
  other arithmetic  16 us (6%)
  matrix products  13.5 us (5%)
  local copies, waits for them, and re-layouts  10.4 us (4%)
    all_gather x1, waiting for transfers between devices, per_device(): lax.all_gather(lax.all_to_all(spread, 'gb', 0, 0, tiled=True), 'head')  33 us
    all_to_all x1, waiting for transfers between devices, per_device(): lax.all_to_all(slices_out, 'gb', 0, 0, tiled=True)  19.3 us
    all_to_all x1, blocking collectives, per_device(): lax.all_to_all(spread, 'gb', 0, 0, tiled=True)  16.9 us
    all_to_all x1, waiting for transfers between devices, per_device(): octet_in = lax.all_to_all(octet_in, 'ga', 0, 0, tiled=True).reshape(chunk)  15.5 us
    all_to_all x1, waiting for transfers between devices, per_device(): lax.all_to_all(branch_parts.reshape(head_count, slice_rows, -1), 'head',...  14.9 us
    all_to_all x1, starting transfers between devices, per_device(): received = lax.all_to_all(payload, 'ga', 0, 0, tiled=True)  14.5 us
    all_to_all x1, waiting for transfers between devices, per_device(): received = lax.all_to_all(payload, 'ga', 0, 0, tiled=True)  13.1 us
    all_to_all x1, waiting for transfers between devices, per_device(): seq_total = jnp.sum(lax.all_to_all(spread, axes, 0, 0, tiled=True), axis=0)  12.9 us
  transfers between devices with their start and end apart: 9, of which 8 were waited for; matrix products, arithmetic and copies ran while one was open for 5% of the time, Pallas kernels for 0%

profile of v13, /device:TPU:1, one launch (start us, length us, event | category | flops | bytes accessed | tf_op | source)
XLA Modules:
  0.0 264.1 jit_solution(16533339074372987235)
XLA Ops:
  7.2 0.9 copy.70
  8.1 0.1 reduce.14
  8.3 0.7 sub.101
  9.2 0.6 fusion.65
  9.8 0.8 copy.71
  10.6 0.2 reduce_window_sum.18
  10.7 0.6 slice.84
  11.3 0.1 reduce.15
  12.2 1.3 fusion.63
  13.5 2.0 select_multiply_fusion
  15.5 1.4 fusion.17
  16.9 0.1 reshape.517
  17.6 1.2 all_to_all.48
  18.8 6.4 %all-to-all-start = ((f32[8,1,16512]{2,1,0:T(1,128)}), f32[8,1,16512]{2,1,0:T(1,128)S(1)}, u32[]{:S(2)}, u32[]{:S(2)}) async-start(f32[8,1,16512]{2,1,0:T(1,128)} %all_to_all.48), calls=%async_computation | async-start | bytes 1056768 | tf_op jit(solution)/shard_map/all_to_all | solution.py:91
  25.2 0.7 all-gather.4.cloned.1.call-update
  25.9 6.4 %all-to-all-done = f32[8,1,16512]{2,1,0:T(1,128)S(1)} async-done(((f32[8,1,16512]{2,1,0:T(1,128)}), f32[8,1,16512]{2,1,0:T(1,128)S(1)}, u32[]{:S(2)}, u32[]{:S(2)}) %all-to-all-start) | async-done | bytes 528416 | tf_op jit(solution)/shard_map/all_to_all | solution.py:91
  32.4 0.7 slice_reduce_fusion.4
  33.1 0.2 select_reduce_fusion.1
  33.4 0.6 fusion.52
  34.0 0.7 pad_select_fusion.1
  34.7 0.7 all_to_all.51
  35.3 14.5 %all-to-all-start.1 = ((f32[8,1,2176]{2,1,0:T(1,128)}), f32[8,1,2176]{2,1,0:T(1,128)S(1)}, u32[]{:S(2)}, u32[]{:S(2)}) async-start(f32[8,1,2176]{2,1,0:T(1,128)} %all_to_all.51), calls=%async_computation.1 | async-start | bytes 139264 | tf_op jit(solution)/shard_map/all_to_all | solution.py:110
  49.9 13.1 %all-to-all-done.1 = f32[8,1,2176]{2,1,0:T(1,128)S(1)} async-done(((f32[8,1,2176]{2,1,0:T(1,128)}), f32[8,1,2176]{2,1,0:T(1,128)S(1)}, u32[]{:S(2)}, u32[]{:S(2)}) %all-to-all-start.1) | async-done | bytes 69664 | tf_op jit(solution)/shard_map/all_to_all | solution.py:110
  63.0 0.1 slice_reduce_fusion.2
  63.1 0.3 fusion.30
  63.5 0.2 convolution_bitcast_fusion
  63.7 0.7 copy.72
  64.3 3.4 %all-to-all-start.2 = ((f32[8,1,2048]{2,1,0:T(1,128)}), f32[8,1,2048]{2,1,0:T(1,128)S(1)}, u32[]{:S(2)}, u32[]{:S(2)}) async-start(f32[8,1,2048]{2,1,0:T(1,128)} %copy.72), calls=%async_computation.2 | async-start | bytes 131072 | tf_op jit(solution)/shard_map/all_to_all | solution.py:114
  67.8 0.1 slice_reduce_fusion.3
  68.0 0.2 reduce-window.18
  68.2 15.5 %all-to-all-done.2 = f32[8,1,2048]{2,1,0:T(1,128)S(1)} async-done(((f32[8,1,2048]{2,1,0:T(1,128)}), f32[8,1,2048]{2,1,0:T(1,128)S(1)}, u32[]{:S(2)}, u32[]{:S(2)}) %all-to-all-start.2) | async-done | bytes 65568 | tf_op jit(solution)/shard_map/all_to_all | solution.py:114
  83.6 0.6 fusion
  84.2 1.3 copy.73
  85.5 8.3 %all-to-all-start.3 = ((f32[8,1,16384]{2,1,0:T(1,128)}), f32[8,1,16384]{2,1,0:T(1,128)S(1)}, u32[]{:S(2)}, u32[]{:S(2)}) async-start(f32[8,1,16384]{2,1,0:T(1,128)} %copy.73), calls=%async_computation.3 | async-start | bytes 1048576 | tf_op jit(solution)/shard_map/all_to_all | solution.py:116
  93.8 0.4 convolution_bitcast_fusion.2
  94.2 19.3 %all-to-all-done.3 = f32[8,1,16384]{2,1,0:T(1,128)S(1)} async-done(((f32[8,1,16384]{2,1,0:T(1,128)}), f32[8,1,16384]{2,1,0:T(1,128)S(1)}, u32[]{:S(2)}, u32[]{:S(2)}) %all-to-all-start.3) | async-done | bytes 524320 | tf_op jit(solution)/shard_map/all_to_all | solution.py:116
  113.5 2.8 %multiply_reduce_fusion = (f32[]{:T(128)}, f32[8,16384]{1,0:T(8,128)S(1)}) fusion(f32[8,1,16384]{2,1,0:T(1,128)S(1)} %all-to-all-done.3), kind=kLoop, calls=%fused_computation.20 | loop fusion | flops 262143 | bytes 1048580 | tf_op jit(solution)/shard_map/reduce_sum | solution.py:129
  116.3 0.1 reshape.520
  116.4 0.4 fusion.66
  116.9 0.2 multiply_reduce_fusion.1
  117.1 1.1 fusion.16
  118.1 1.4 fusion.3
  119.6 5.9 %all-to-all-start.4 = ((f32[8,16,2048]{2,1,0:T(8,128)}), f32[8,16,2048]{2,1,0:T(8,128)S(1)}, u32[]{:S(2)}, u32[]{:S(2)}) async-start(f32[8,16,2048]{2,1,0:T(8,128)} %fusion.3), calls=%async_computation.4 | async-start | bytes 2097152 | tf_op jit(solution)/shard_map/all_to_all | solution.py:140
  125.6 14.9 %all-to-all-done.4 = f32[8,16,2048]{2,1,0:T(8,128)S(1)} async-done(((f32[8,16,2048]{2,1,0:T(8,128)}), f32[8,16,2048]{2,1,0:T(8,128)S(1)}, u32[]{:S(2)}, u32[]{:S(2)}) %all-to-all-start.4) | async-done | bytes 1048608 | tf_op jit(solution)/shard_map/all_to_all | solution.py:140
  140.5 0.1 fusion.29
  140.7 0.2 multiply_reduce_fusion.2
  140.9 0.1 multiply_convert_fusion
  141.1 16.9 %all_to_all.73 = bf16[8,17,2048]{2,1,0:T(8,128)(2,1)S(1)} all-to-all(bf16[8,17,2048]{2,1,0:T(8,128)(2,1)S(1)} %broadcast_in_dim.87), channel_id=1, replica_groups=mesh['head'=8,'ga'=8,'gb'=8] {'gb'}, dimensions={0} | all-to-all | bytes 1114112 | tf_op jit(solution)/shard_map/all_to_all | solution.py:155
  158.0 1.1 copy.74
  159.4 33.0 %all-gather.6.cloned.1.call-done = bf16[64,17,2048]{2,0,1:T(8,128)(2,1)} async-done(((bf16[8,17,2048]{2,0,1:T(8,128)(2,1)}), bf16[64,17,2048]{2,0,1:T(8,128)(2,1)}) %all-gather.6.cloned.1.call-update) | async-done | bytes 4456464 | tf_op jit(solution)/shard_map/all_gather | solution.py:155
  192.4 0.7 fusion.39
  193.3 8.5 %fusion.67 = (f32[64,16]{0,1:T(8,128)S(1)}, f32[64,16,768]{2,0,1:T(8,128)}) fusion(bf16[64,17,2048]{2,0,1:T(8,128)(2,1)} %all-gather.6.cloned.1.call-done, bf16[768,2048]{1,0:T(8,128)(2,1)} %all-gather.4.cloned.1.call-done), kind=kOutput, calls=%fused_computation.137 | convolution fusion | flops 3222010880 | bytes 10752000 | tf_op jit(solution)/shard_map/slice | solution.py:167
  201.8 2.4 exponential_reduce_fusion
  204.6 0.7 all_to_all.60
  205.3 7.2 %all-to-all-start.6 = ((f32[64,1,48]{2,1,0:T(1,128)}), f32[64,1,48]{2,1,0:T(1,128)S(1)}, u32[]{:S(2)}, u32[]{:S(2)}) async-start(f32[64,1,48]{2,1,0:T(1,128)} %bitcast.41), calls=%async_computation.6 | async-start | bytes 65536 | tf_op jit(solution)/shard_map/all_to_all | solution.py:180
  212.5 0.2 convert_reduce_fusion.1
  212.7 7.6 %all-to-all-done.6 = f32[64,1,48]{2,1,0:T(1,128)S(1)} async-done(((f32[64,1,48]{2,1,0:T(1,128)}), f32[64,1,48]{2,1,0:T(1,128)S(1)}, u32[]{:S(2)}, u32[]{:S(2)}) %all-to-all-start.6) | async-done | bytes 12320 | tf_op jit(solution)/shard_map/all_to_all | solution.py:180
  220.4 0.1 slice_reduce_fusion
  220.5 0.2 fusion.41
  220.8 7.8 %all_to_all.74 = f32[8,1,32]{2,1,0:T(1,128)S(1)} all-to-all(f32[8,1,32]{2,1,0:T(1,128)S(1)} %broadcast_in_dim.89), channel_id=1, replica_groups=mesh['head'=8,'ga'=8,'gb'=8] {'head'}, dimensions={0} | all-to-all | bytes 2048 | tf_op jit(solution)/shard_map/all_to_all | solution.py:198
  228.6 0.6 broadcast_in_dim.90
  229.2 12.6 %all-to-all-start.8 = ((f32[64,1,32]{2,1,0:T(1,128)}), f32[64,1,32]{2,1,0:T(1,128)S(1)}, u32[]{:S(2)}, u32[]{:S(2)}) async-start(f32[64,1,32]{2,1,0:T(1,128)} %broadcast_in_dim.90), calls=%async_computation.8 | async-start | bytes 65536 | tf_op jit(solution)/shard_map/all_to_all | solution.py:198
  242.6 12.9 %all-to-all-done.8 = f32[64,1,32]{2,1,0:T(1,128)S(1)} async-done(((f32[64,1,32]{2,1,0:T(1,128)}), f32[64,1,32]{2,1,0:T(1,128)S(1)}, u32[]{:S(2)}, u32[]{:S(2)}) %all-to-all-start.8) | async-done | bytes 8224 | tf_op jit(solution)/shard_map/all_to_all | solution.py:198
  255.6 0.5 convert_divide_fusion
  (69 shorter events, 2.0 us)
Async XLA Ops:
  7.2 111.0 %copy-start = (bf16[512,2048]{1,0:T(8,128)(2,1)S(1)}, bf16[512,2048]{1,0:T(8,128)(2,1)}, u32[]{:S(2)}) copy-start(bf16[512,2048]{1,0:T(8,128)(2,1)} %param.18) | copy-start | bytes 6291460
  18.8 13.5 %all-to-all-start = ((f32[8,1,16512]{2,1,0:T(1,128)}), f32[8,1,16512]{2,1,0:T(1,128)S(1)}, u32[]{:S(2)}, u32[]{:S(2)}) async-start(f32[8,1,16512]{2,1,0:T(1,128)} %all_to_all.48), calls=%async_computation | async-start | bytes 1056768 | tf_op jit(solution)/shard_map/all_to_all | solution.py:91
  25.1 115.4 %all-gather.4.cloned.1.call-start = ((), (), s32[]{:S(2)}) async-start(), calls=%async_computation.9 | async-start | bytes 3538944 | tf_op jit(solution)/shard_map/all_gather | solution.py:120
  32.3 61.5 %copy-start.2 = (bf16[128,512]{1,0:T(8,128)(2,1)S(1)}, bf16[128,512]{1,0:T(8,128)(2,1)}, u32[]{:S(2)}) copy-start(bf16[128,512]{1,0:T(8,128)(2,1)} %param.15) | copy-start | bytes 393220
  32.3 61.5 %copy-start.3 = (bf16[128,256]{1,0:T(8,128)(2,1)S(1)}, bf16[128,256]{1,0:T(8,128)(2,1)}, u32[]{:S(2)}) copy-start(bf16[128,256]{1,0:T(8,128)(2,1)} %param.14) | copy-start | bytes 196612
  32.4 61.5 %copy-start.4 = (bf16[128,256]{1,0:T(8,128)(2,1)S(1)}, bf16[128,256]{1,0:T(8,128)(2,1)}, u32[]{:S(2)}) copy-start(bf16[128,256]{1,0:T(8,128)(2,1)} %param.13) | copy-start | bytes 196612
  35.3 27.6 %all-to-all-start.1 = ((f32[8,1,2176]{2,1,0:T(1,128)}), f32[8,1,2176]{2,1,0:T(1,128)S(1)}, u32[]{:S(2)}, u32[]{:S(2)}) async-start(f32[8,1,2176]{2,1,0:T(1,128)} %all_to_all.51), calls=%async_computation.1 | async-start | bytes 139264 | tf_op jit(solution)/shard_map/all_to_all | solution.py:110
  64.3 19.3 %all-to-all-start.2 = ((f32[8,1,2048]{2,1,0:T(1,128)}), f32[8,1,2048]{2,1,0:T(1,128)S(1)}, u32[]{:S(2)}, u32[]{:S(2)}) async-start(f32[8,1,2048]{2,1,0:T(1,128)} %copy.72), calls=%async_computation.2 | async-start | bytes 131072 | tf_op jit(solution)/shard_map/all_to_all | solution.py:114
  85.5 28.0 %all-to-all-start.3 = ((f32[8,1,16384]{2,1,0:T(1,128)}), f32[8,1,16384]{2,1,0:T(1,128)S(1)}, u32[]{:S(2)}, u32[]{:S(2)}) async-start(f32[8,1,16384]{2,1,0:T(1,128)} %copy.73), calls=%async_computation.3 | async-start | bytes 1048576 | tf_op jit(solution)/shard_map/all_to_all | solution.py:116
  116.8 8.6 %copy-start.10 = (s32[1,16]{1,0:T(1,128)S(1)}, s32[1,16]{1,0:T(1,128)}, u32[]{:S(2)}) copy-start(s32[1,16]{1,0:T(1,128)} %param.22) | copy-start | bytes 196
  118.1 22.4 %copy-start.1 = (bf16[1,16,2048]{2,1,0:T(8,128)(2,1)S(1)}, bf16[1,16,2048]{2,1,0:T(8,128)(2,1)}, u32[]{:S(2)}) copy-start(bf16[1,16,2048]{2,1,0:T(8,128)(2,1)} %param.19) | copy-start | bytes 196612
  118.1 22.8 %copy-start.5 = (f32[2048]{0:T(1024)S(1)}, f32[2048]{0:T(1024)}, u32[]{:S(2)}) copy-start(f32[2048]{0:T(1024)} %param.20) | copy-start | bytes 24580
  119.6 20.8 %all-to-all-start.4 = ((f32[8,16,2048]{2,1,0:T(8,128)}), f32[8,16,2048]{2,1,0:T(8,128)S(1)}, u32[]{:S(2)}, u32[]{:S(2)}) async-start(f32[8,16,2048]{2,1,0:T(8,128)} %fusion.3), calls=%async_computation.4 | async-start | bytes 2097152 | tf_op jit(solution)/shard_map/all_to_all | solution.py:140
  125.5 66.9 %all-gather.6.cloned.1.call-start = ((), (), s32[]{:S(2)}) async-start(), calls=%async_computation.10 | async-start | bytes 5013504 | tf_op jit(solution)/shard_map/all_gather | solution.py:155
  201.7 19.0 %copy-start.8 = (f32[1,16]{1,0:T(1,128)S(1)}, f32[1,16]{1,0:T(1,128)}, u32[]{:S(2)}) copy-start(f32[1,16]{1,0:T(1,128)} %param.23) | copy-start | bytes 196
  201.7 19.0 %copy-start.9 = (s32[1,16]{1,0:T(1,128)S(1)}, s32[1,16]{1,0:T(1,128)}, u32[]{:S(2)}) copy-start(s32[1,16]{1,0:T(1,128)} %param.24) | copy-start | bytes 196
  201.7 53.9 %copy-start.7 = (s32[32]{0:T(128)S(1)}, s32[32]{0:T(128)}, u32[]{:S(2)}) copy-start(s32[32]{0:T(128)} %param.25) | copy-start | bytes 388
  205.3 15.0 %all-to-all-start.6 = ((f32[64,1,48]{2,1,0:T(1,128)}), f32[64,1,48]{2,1,0:T(1,128)S(1)}, u32[]{:S(2)}, u32[]{:S(2)}) async-start(f32[64,1,48]{2,1,0:T(1,128)} %bitcast.41), calls=%async_computation.6 | async-start | bytes 65536 | tf_op jit(solution)/shard_map/all_to_all | solution.py:180
  220.5 35.6 %copy-start.6 = (f32[16]{0:T(128)}, f32[16]{0:T(128)S(1)}, u32[]{:S(2)}) copy-start(f32[16]{0:T(128)S(1)} %get-tuple-element.14) | copy-start | bytes 196
  229.2 26.3 %all-to-all-start.8 = ((f32[64,1,32]{2,1,0:T(1,128)}), f32[64,1,32]{2,1,0:T(1,128)S(1)}, u32[]{:S(2)}, u32[]{:S(2)}) async-start(f32[64,1,32]{2,1,0:T(1,128)} %broadcast_in_dim.90), calls=%async_computation.8 | async-start | bytes 65536 | tf_op jit(solution)/shard_map/all_to_all | solution.py:198
Sparse Core Ops, SparseCore 0:
  28.0 96.6 all-gather.3
  159.3 33.0 all-gather.5

commit v14 on v13

--- a/solution.py
+++ b/solution.py
@@ -148,13 +148,15 @@
 
     ga_index = lax.axis_index("ga")
     gb_index = lax.axis_index("gb")
-    code = jnp.concatenate([targets[0] // 256, targets[0] % 256]).astype(jnp.bfloat16)
-    code_row = jnp.pad(code, (0, hidden.shape[1] - code.shape[0]))[None, :]
-    hidden_ext = jnp.concatenate([hidden, code_row], axis=0)
+    code = jnp.stack([targets[0] // 256, targets[0] % 256], axis=1).astype(jnp.bfloat16)
+    hidden_ext = jnp.concatenate(
+        [hidden, jnp.pad(code, ((0, 0), (0, 128 - code.shape[1])))], axis=1
+    )
     spread = jnp.broadcast_to(hidden_ext[None], (sub,) + hidden_ext.shape)
     gathered = lax.all_gather(lax.all_to_all(spread, "gb", 0, 0, tiled=True), "head")
-    code_all = gathered[:, :, slice_rows, : 2 * slice_rows].astype(jnp.int32)
-    all_targets = (code_all[..., :slice_rows] * 256 + code_all[..., slice_rows:]).reshape(-1)
+    width = hidden.shape[1]
+    code_all = gathered[..., width : width + 2].astype(jnp.int32)
+    all_targets = (code_all[..., 0] * 256 + code_all[..., 1]).reshape(-1)
     entry_ids = (
         (
             head_index * group_count
@@ -165,12 +167,10 @@
         + jnp.arange(vocab_here, dtype=jnp.int32)[None, :]
     ).reshape(-1)
     logits = lax.dot_general(
-        gathered.reshape(-1, hidden.shape[1]),
+        gathered[..., :width].reshape(-1, width),
         vocab_rows,
         (((1,), (1,)), ((), ())),
         preferred_element_type=jnp.float32,
-    ).reshape(head_count * sub, slice_rows + 1, -1)[:, :slice_rows, :].reshape(
-        head_count * sub * slice_rows, -1
     )
     top = jnp.max(logits, axis=1)
     exp_total = jnp.sum(jnp.exp(logits - top[:, None]), axis=1)

time: 265 us -> 268 us (1.011)
  local copies, waits for them, and re-layouts: 10.4 us -> 14.1 us
    slice x1 -> x0, matrix products: 8.47 us -> none  [per_device(): lax.dot_general(gathered.reshape(-1, hidden.shape[1]), vocab_rows, (((1,)...]
    dot_general x0 -> x1, matrix products: none -> 8.29 us  [per_device(): lax.dot_general(gathered[..., :width].reshape(-1, width), vocab_rows, (((...]
    slice x0 -> x1, local copies, waits for them, and re-layouts: none -> 4.74 us  [per_device(): gathered[..., :width].reshape(-1, width)]
    all_to_all x1, starting transfers between devices: 5.87 us -> 8.65 us  [per_device(): lax.all_to_all(branch_parts.reshape(head_count, slice_rows, -1), 'head',...]
where the time goes in v14:
time: 268 us; the launch traced here: 267 us
  waiting for transfers between devices  122 us (46%)
  starting transfers between devices  59.8 us (22%)
  blocking collectives  22.9 us (9%)
  other arithmetic  17.8 us (7%)
  between operations  17.7 us (7%)
  local copies, waits for them, and re-layouts  14.1 us (5%)
  matrix products  13.3 us (5%)
    all_gather x1, waiting for transfers between devices, per_device(): lax.all_gather(lax.all_to_all(spread, 'gb', 0, 0, tiled=True), 'head')  32.7 us
    all_to_all x1, waiting for transfers between devices, per_device(): lax.all_to_all(slices_out, 'gb', 0, 0, tiled=True)  18.1 us
    all_to_all x1, waiting for transfers between devices, per_device(): octet_in = lax.all_to_all(octet_in, 'ga', 0, 0, tiled=True).reshape(chunk)  15.5 us
    all_to_all x1, blocking collectives, per_device(): lax.all_to_all(spread, 'gb', 0, 0, tiled=True)  15.1 us
    all_to_all x1, waiting for transfers between devices, per_device(): lax.all_to_all(branch_parts.reshape(head_count, slice_rows, -1), 'head',...  14.8 us
    all_to_all x1, starting transfers between devices, per_device(): received = lax.all_to_all(payload, 'ga', 0, 0, tiled=True)  14.5 us
    all_to_all x1, waiting for transfers between devices, per_device(): received = lax.all_to_all(payload, 'ga', 0, 0, tiled=True)  13.1 us
    all_to_all x1, waiting for transfers between devices, per_device(): seq_total = jnp.sum(lax.all_to_all(spread, axes, 0, 0, tiled=True), axis=0)  12.9 us
  transfers between devices with their start and end apart: 9, of which 8 were waited for; matrix products, arithmetic and copies ran while one was open for 5% of the time, Pallas kernels for 0%

profile of v14, /device:TPU:1, one launch (start us, length us, event | category | flops | bytes accessed | tf_op | source)
XLA Modules:
  0.0 267.4 jit_solution(980325154005510215)
XLA Ops:
  7.2 0.9 copy.53
  8.1 0.1 reduce.11
  8.3 0.7 sub.100
  9.2 0.6 fusion.61
  9.8 0.8 copy.54
  10.6 0.2 reduce_window_sum.18
  10.7 0.6 slice.84
  12.1 0.1 reduce.12
  12.2 1.3 fusion.59
  14.0 2.0 select_multiply_fusion
  16.0 1.4 fusion.17
  17.6 1.2 all_to_all.48
  18.8 6.4 %all-to-all-start = ((f32[8,1,16512]{2,1,0:T(1,128)}), f32[8,1,16512]{2,1,0:T(1,128)S(1)}, u32[]{:S(2)}, u32[]{:S(2)}) async-start(f32[8,1,16512]{2,1,0:T(1,128)} %all_to_all.48), calls=%async_computation | async-start | bytes 1056768 | tf_op jit(solution)/shard_map/all_to_all | solution.py:91
  25.2 0.7 all-gather.4.cloned.1.call-update
  25.9 6.4 %all-to-all-done = f32[8,1,16512]{2,1,0:T(1,128)S(1)} async-done(((f32[8,1,16512]{2,1,0:T(1,128)}), f32[8,1,16512]{2,1,0:T(1,128)S(1)}, u32[]{:S(2)}, u32[]{:S(2)}) %all-to-all-start) | async-done | bytes 528416 | tf_op jit(solution)/shard_map/all_to_all | solution.py:91
  32.4 0.7 slice_reduce_fusion.4
  33.1 0.7 pad_select_fusion.1
  33.8 0.2 select_reduce_fusion.1
  34.1 0.6 fusion.48
  34.7 0.7 all_to_all.51
  35.4 14.5 %all-to-all-start.1 = ((f32[8,1,2176]{2,1,0:T(1,128)}), f32[8,1,2176]{2,1,0:T(1,128)S(1)}, u32[]{:S(2)}, u32[]{:S(2)}) async-start(f32[8,1,2176]{2,1,0:T(1,128)} %all_to_all.51), calls=%async_computation.1 | async-start | bytes 139264 | tf_op jit(solution)/shard_map/all_to_all | solution.py:110
  49.9 13.1 %all-to-all-done.1 = f32[8,1,2176]{2,1,0:T(1,128)S(1)} async-done(((f32[8,1,2176]{2,1,0:T(1,128)}), f32[8,1,2176]{2,1,0:T(1,128)S(1)}, u32[]{:S(2)}, u32[]{:S(2)}) %all-to-all-start.1) | async-done | bytes 69664 | tf_op jit(solution)/shard_map/all_to_all | solution.py:110
  63.0 0.1 slice_reduce_fusion.2
  63.2 0.3 fusion.31
  63.5 0.2 convolution_bitcast_fusion
  63.7 0.7 copy.55
  64.4 3.4 %all-to-all-start.2 = ((f32[8,1,2048]{2,1,0:T(1,128)}), f32[8,1,2048]{2,1,0:T(1,128)S(1)}, u32[]{:S(2)}, u32[]{:S(2)}) async-start(f32[8,1,2048]{2,1,0:T(1,128)} %copy.55), calls=%async_computation.2 | async-start | bytes 131072 | tf_op jit(solution)/shard_map/all_to_all | solution.py:114
  67.8 0.1 slice_reduce_fusion.3
  68.0 0.2 reduce-window.18
  68.2 15.5 %all-to-all-done.2 = f32[8,1,2048]{2,1,0:T(1,128)S(1)} async-done(((f32[8,1,2048]{2,1,0:T(1,128)}), f32[8,1,2048]{2,1,0:T(1,128)S(1)}, u32[]{:S(2)}, u32[]{:S(2)}) %all-to-all-start.2) | async-done | bytes 65568 | tf_op jit(solution)/shard_map/all_to_all | solution.py:114
  83.7 0.6 fusion
  84.3 1.3 copy.56
  85.6 7.0 %all-to-all-start.3 = ((f32[8,1,16384]{2,1,0:T(1,128)}), f32[8,1,16384]{2,1,0:T(1,128)S(1)}, u32[]{:S(2)}, u32[]{:S(2)}) async-start(f32[8,1,16384]{2,1,0:T(1,128)} %copy.56), calls=%async_computation.3 | async-start | bytes 1048576 | tf_op jit(solution)/shard_map/all_to_all | solution.py:116
  92.6 0.4 convolution_bitcast_fusion.2
  93.0 18.1 %all-to-all-done.3 = f32[8,1,16384]{2,1,0:T(1,128)S(1)} async-done(((f32[8,1,16384]{2,1,0:T(1,128)}), f32[8,1,16384]{2,1,0:T(1,128)S(1)}, u32[]{:S(2)}, u32[]{:S(2)}) %all-to-all-start.3) | async-done | bytes 524320 | tf_op jit(solution)/shard_map/all_to_all | solution.py:116
  111.1 2.8 %multiply_reduce_fusion = (f32[]{:T(128)}, f32[8,16384]{1,0:T(8,128)S(1)}) fusion(f32[8,1,16384]{2,1,0:T(1,128)S(1)} %all-to-all-done.3), kind=kLoop, calls=%fused_computation.21 | loop fusion | flops 262143 | bytes 1048580 | tf_op jit(solution)/shard_map/reduce_sum | solution.py:129
  114.0 0.4 fusion.62
  114.4 0.2 multiply_reduce_fusion.1
  114.6 1.1 fusion.15
  115.7 1.4 fusion.1
  117.1 8.7 %all-to-all-start.4 = ((f32[8,16,2048]{2,1,0:T(8,128)}), f32[8,16,2048]{2,1,0:T(8,128)S(1)}, u32[]{:S(2)}, u32[]{:S(2)}) async-start(f32[8,16,2048]{2,1,0:T(8,128)} %fusion.1), calls=%async_computation.4 | async-start | bytes 2097152 | tf_op jit(solution)/shard_map/all_to_all | solution.py:140
  125.9 14.8 %all-to-all-done.4 = f32[8,16,2048]{2,1,0:T(8,128)S(1)} async-done(((f32[8,16,2048]{2,1,0:T(8,128)}), f32[8,16,2048]{2,1,0:T(8,128)S(1)}, u32[]{:S(2)}, u32[]{:S(2)}) %all-to-all-start.4) | async-done | bytes 1048608 | tf_op jit(solution)/shard_map/all_to_all | solution.py:140
  140.9 0.1 fusion.30
  141.0 0.2 multiply_reduce_fusion.2
  141.4 15.1 %all_to_all.73 = bf16[8,16,2176]{2,1,0:T(8,128)(2,1)} all-to-all(bf16[8,16,2176]{2,1,0:T(8,128)(2,1)S(1)} %broadcast_in_dim.83), channel_id=1, replica_groups=mesh['head'=8,'ga'=8,'gb'=8] {'gb'}, dimensions={0} | all-to-all | bytes 1114112 | tf_op jit(solution)/shard_map/all_to_all | solution.py:156
  156.7 32.7 %all-gather.6.cloned.1.call-done = bf16[64,16,2176]{2,1,0:T(8,128)(2,1)} async-done(((bf16[8,16,2176]{2,1,0:T(8,128)(2,1)}), bf16[64,16,2176]{2,1,0:T(8,128)(2,1)}) %all-gather.6.cloned.1.call-update) | async-done | bytes 4456464 | tf_op jit(solution)/shard_map/all_gather | solution.py:156
  189.4 1.0 slice_convert_fusion
  190.4 4.7 %slice.92 = bf16[8,8,16,2048]{3,2,1,0:T(8,128)(2,1)} slice(bf16[8,8,16,2176]{3,2,1,0:T(8,128)(2,1)} %bitcast.142), slice={[0:8], [0:8], [0:16], [0:2048]} | slice | bytes 8388608 | tf_op jit(solution)/shard_map/slice | solution.py:170
  195.1 1.3 fusion.9
  196.5 8.3 %fusion.63 = (f32[1024]{0:T(1024)S(1)}, f32[1024,768]{0,1:T(8,128)}) fusion(bf16[1024,2048]{1,0:T(8,128)(2,1)} %bitcast.143, bf16[768,2048]{1,0:T(8,128)(2,1)} %all-gather.4.cloned.1.call-done), kind=kOutput, calls=%fused_computation.133 | convolution fusion | flops 3222010880 | bytes 10489856 | tf_op jit(solution)/shard_map/dot_general | solution.py:169
  204.9 2.6 exponential_reduce_fusion
  207.5 0.1 stack.20
  207.8 0.1 maximum_bitcast_fusion
  207.9 0.7 all_to_all.60
  208.6 7.2 %all-to-all-start.6 = ((f32[64,1,48]{2,1,0:T(1,128)}), f32[64,1,48]{2,1,0:T(1,128)S(1)}, u32[]{:S(2)}, u32[]{:S(2)}) async-start(f32[64,1,48]{2,1,0:T(1,128)} %bitcast.35), calls=%async_computation.6 | async-start | bytes 65536 | tf_op jit(solution)/shard_map/all_to_all | solution.py:180
  215.9 0.2 convert_reduce_fusion.1
  216.0 7.6 %all-to-all-done.6 = f32[64,1,48]{2,1,0:T(1,128)S(1)} async-done(((f32[64,1,48]{2,1,0:T(1,128)}), f32[64,1,48]{2,1,0:T(1,128)S(1)}, u32[]{:S(2)}, u32[]{:S(2)}) %all-to-all-start.6) | async-done | bytes 12320 | tf_op jit(solution)/shard_map/all_to_all | solution.py:180
  223.7 0.1 slice_reduce_fusion
  223.8 0.2 fusion.40
  224.2 7.8 %all_to_all.74 = f32[8,1,32]{2,1,0:T(1,128)S(1)} all-to-all(f32[8,1,32]{2,1,0:T(1,128)S(1)} %broadcast_in_dim.86), channel_id=1, replica_groups=mesh['head'=8,'ga'=8,'gb'=8] {'head'}, dimensions={0} | all-to-all | bytes 2048 | tf_op jit(solution)/shard_map/all_to_all | solution.py:198
  232.0 0.6 broadcast_in_dim.87
  232.6 12.6 %all-to-all-start.8 = ((f32[64,1,32]{2,1,0:T(1,128)}), f32[64,1,32]{2,1,0:T(1,128)S(1)}, u32[]{:S(2)}, u32[]{:S(2)}) async-start(f32[64,1,32]{2,1,0:T(1,128)} %broadcast_in_dim.87), calls=%async_computation.8 | async-start | bytes 65536 | tf_op jit(solution)/shard_map/all_to_all | solution.py:198
  246.0 12.9 %all-to-all-done.8 = f32[64,1,32]{2,1,0:T(1,128)S(1)} async-done(((f32[64,1,32]{2,1,0:T(1,128)}), f32[64,1,32]{2,1,0:T(1,128)S(1)}, u32[]{:S(2)}, u32[]{:S(2)}) %all-to-all-start.8) | async-done | bytes 8224 | tf_op jit(solution)/shard_map/all_to_all | solution.py:198
  258.9 0.5 convert_divide_fusion
  (68 shorter events, 2.0 us)
Async XLA Ops:
  7.2 108.5 %copy-start = (bf16[512,2048]{1,0:T(8,128)(2,1)S(1)}, bf16[512,2048]{1,0:T(8,128)(2,1)}, u32[]{:S(2)}) copy-start(bf16[512,2048]{1,0:T(8,128)(2,1)} %param.18) | copy-start | bytes 6291460
  18.8 13.5 %all-to-all-start = ((f32[8,1,16512]{2,1,0:T(1,128)}), f32[8,1,16512]{2,1,0:T(1,128)S(1)}, u32[]{:S(2)}, u32[]{:S(2)}) async-start(f32[8,1,16512]{2,1,0:T(1,128)} %all_to_all.48), calls=%async_computation | async-start | bytes 1056768 | tf_op jit(solution)/shard_map/all_to_all | solution.py:91
  25.2 115.7 %all-gather.4.cloned.1.call-start = ((), (), s32[]{:S(2)}) async-start(), calls=%async_computation.9 | async-start | bytes 3538944 | tf_op jit(solution)/shard_map/all_gather | solution.py:120
  32.3 60.2 %copy-start.2 = (bf16[128,512]{1,0:T(8,128)(2,1)S(1)}, bf16[128,512]{1,0:T(8,128)(2,1)}, u32[]{:S(2)}) copy-start(bf16[128,512]{1,0:T(8,128)(2,1)} %param.15) | copy-start | bytes 393220
  32.4 60.2 %copy-start.3 = (bf16[128,256]{1,0:T(8,128)(2,1)S(1)}, bf16[128,256]{1,0:T(8,128)(2,1)}, u32[]{:S(2)}) copy-start(bf16[128,256]{1,0:T(8,128)(2,1)} %param.14) | copy-start | bytes 196612
  32.4 60.2 %copy-start.4 = (bf16[128,256]{1,0:T(8,128)(2,1)S(1)}, bf16[128,256]{1,0:T(8,128)(2,1)}, u32[]{:S(2)}) copy-start(bf16[128,256]{1,0:T(8,128)(2,1)} %param.13) | copy-start | bytes 196612
  35.4 27.7 %all-to-all-start.1 = ((f32[8,1,2176]{2,1,0:T(1,128)}), f32[8,1,2176]{2,1,0:T(1,128)S(1)}, u32[]{:S(2)}, u32[]{:S(2)}) async-start(f32[8,1,2176]{2,1,0:T(1,128)} %all_to_all.51), calls=%async_computation.1 | async-start | bytes 139264 | tf_op jit(solution)/shard_map/all_to_all | solution.py:110
  64.4 19.3 %all-to-all-start.2 = ((f32[8,1,2048]{2,1,0:T(1,128)}), f32[8,1,2048]{2,1,0:T(1,128)S(1)}, u32[]{:S(2)}, u32[]{:S(2)}) async-start(f32[8,1,2048]{2,1,0:T(1,128)} %copy.55), calls=%async_computation.2 | async-start | bytes 131072 | tf_op jit(solution)/shard_map/all_to_all | solution.py:114
  85.6 25.5 %all-to-all-start.3 = ((f32[8,1,16384]{2,1,0:T(1,128)}), f32[8,1,16384]{2,1,0:T(1,128)S(1)}, u32[]{:S(2)}, u32[]{:S(2)}) async-start(f32[8,1,16384]{2,1,0:T(1,128)} %copy.56), calls=%async_computation.3 | async-start | bytes 1048576 | tf_op jit(solution)/shard_map/all_to_all | solution.py:116
  114.4 11.4 %copy-start.10 = (s32[1,16]{1,0:T(1,128)S(1)}, s32[1,16]{1,0:T(1,128)}, u32[]{:S(2)}) copy-start(s32[1,16]{1,0:T(1,128)} %param.22) | copy-start | bytes 196
  115.7 25.2 %copy-start.1 = (bf16[1,16,2048]{2,1,0:T(8,128)(2,1)S(1)}, bf16[1,16,2048]{2,1,0:T(8,128)(2,1)}, u32[]{:S(2)}) copy-start(bf16[1,16,2048]{2,1,0:T(8,128)(2,1)} %param.19) | copy-start | bytes 196612
  115.7 25.5 %copy-start.5 = (f32[2048]{0:T(1024)S(1)}, f32[2048]{0:T(1024)}, u32[]{:S(2)}) copy-start(f32[2048]{0:T(1024)} %param.20) | copy-start | bytes 24580
  117.1 23.6 %all-to-all-start.4 = ((f32[8,16,2048]{2,1,0:T(8,128)}), f32[8,16,2048]{2,1,0:T(8,128)S(1)}, u32[]{:S(2)}, u32[]{:S(2)}) async-start(f32[8,16,2048]{2,1,0:T(8,128)} %fusion.1), calls=%async_computation.4 | async-start | bytes 2097152 | tf_op jit(solution)/shard_map/all_to_all | solution.py:140
  125.8 63.6 %all-gather.6.cloned.1.call-start = ((), (), s32[]{:S(2)}) async-start(), calls=%async_computation.10 | async-start | bytes 5013504 | tf_op jit(solution)/shard_map/all_gather | solution.py:156
  204.8 19.2 %copy-start.8 = (f32[1,16]{1,0:T(1,128)S(1)}, f32[1,16]{1,0:T(1,128)}, u32[]{:S(2)}) copy-start(f32[1,16]{1,0:T(1,128)} %param.23) | copy-start | bytes 196
  204.8 19.2 %copy-start.9 = (s32[1,16]{1,0:T(1,128)S(1)}, s32[1,16]{1,0:T(1,128)}, u32[]{:S(2)}) copy-start(s32[1,16]{1,0:T(1,128)} %param.24) | copy-start | bytes 196
  204.8 54.1 %copy-start.7 = (s32[32]{0:T(128)S(1)}, s32[32]{0:T(128)}, u32[]{:S(2)}) copy-start(s32[32]{0:T(128)} %param.25) | copy-start | bytes 388
  208.6 15.0 %all-to-all-start.6 = ((f32[64,1,48]{2,1,0:T(1,128)}), f32[64,1,48]{2,1,0:T(1,128)S(1)}, u32[]{:S(2)}, u32[]{:S(2)}) async-start(f32[64,1,48]{2,1,0:T(1,128)} %bitcast.35), calls=%async_computation.6 | async-start | bytes 65536 | tf_op jit(solution)/shard_map/all_to_all | solution.py:180
  223.8 35.6 %copy-start.6 = (f32[16]{0:T(128)}, f32[16]{0:T(128)S(1)}, u32[]{:S(2)}) copy-start(f32[16]{0:T(128)S(1)} %get-tuple-element.14) | copy-start | bytes 196
  232.6 26.3 %all-to-all-start.8 = ((f32[64,1,32]{2,1,0:T(1,128)}), f32[64,1,32]{2,1,0:T(1,128)S(1)}, u32[]{:S(2)}, u32[]{:S(2)}) async-start(f32[64,1,32]{2,1,0:T(1,128)} %broadcast_in_dim.87), calls=%async_computation.8 | async-start | bytes 65536 | tf_op jit(solution)/shard_map/all_to_all | solution.py:198
Sparse Core Ops, SparseCore 0:
  28.0 97.2 all-gather.3
  156.6 32.7 all-gather.5
